TPU v7x, 32 devices: a whole 2x2x4 slice. The times are simulated.
32 devices in a mesh: req: 16 (over z, y, x), tp: 2 (over core).
Axes of the slice: x: 2, y: 2, z: 4, core: 2. Of those that a mesh axis runs over, the one named last changes fastest.
Arguments:
- queries: bfloat16 [10240, 4096], P('req', 'tp'), may hold values from -60 to 60
- rotated_key_rows: bfloat16 [10240, 1024], P('req', 'tp'), may hold values from -9 to 9
- stream_value_rows: bfloat16 [10240, 1024], P('req', 'tp'), may hold values from -6 to 6
- out_weight: bfloat16 [4096, 8192], P('tp'), may hold values from -0.5 to 0.5
- short_pages: int32 [51], replicated, may hold values from 1 to 4, 128 in all
- short_fill: int32 [51], replicated, may hold values from 1 to 16
- stream_page_table: int32 [640], replicated, may hold values from 0 to 767, as said below
Outputs:
- mixed: bfloat16 [10240, 8192], P(('req', 'tp'))
- cache_pages: bfloat16 [2, 768, 16, 1024], P(None, 'req', None, 'tp')
Inputs may be any that keep to these rules, and one draw needn't show every extreme that they name: `stream_page_table`: entries are distinct. Owner = entry // 48. Of the 40 pages of one block of the stream at most 3 have one owner; in every draw some owner gets 3 pages from every block.
All inputs are finite; a program needn't handle non-finite values.
Results may differ from a plain program's by a relative error of at most 0.0061.
Values may be sent and summed in bfloat16 or wider, within the bound.
No kernel may reach another device: no remote copies, remote signals or barrier semaphores. Data moves between devices by JAX's collectives and lax.ppermute only.
A program may use at most 192 MiB of HBM per device.

v0:
```python
import jax
import jax.numpy as jnp
from jax import lax
from jax.sharding import PartitionSpec as P

HEAD_SIZE = 128
LONG_DEV = 512
SHORT_DEV = 128
PAGE_ROWS = 16
BLOCK_TOKENS = 640


NEGATIVE_FILL = -1e30


def stream_layout(short_pages, short_fill, req_count):
    token_id = jnp.arange(req_count * BLOCK_TOKENS, dtype=jnp.int32)
    device_block = token_id // BLOCK_TOKENS
    in_block = token_id % BLOCK_TOKENS
    is_long = in_block < LONG_DEV
    offset = jnp.where(is_long, 0, device_block * SHORT_DEV + in_block - LONG_DEV)
    page_id = offset // PAGE_ROWS
    page_ends = jnp.cumsum(short_pages)
    page_starts = page_ends - short_pages
    limits = page_starts * PAGE_ROWS + (short_pages - 1) * PAGE_ROWS + short_fill
    owner_hit = page_ends[None, :] <= page_id[:, None]
    prompt = jnp.sum(owner_hit.astype(jnp.int32), axis=1)
    select = jnp.arange(short_pages.shape[0], dtype=jnp.int32)[None, :] == prompt[:, None]
    begin_at = jnp.sum(jnp.where(select, page_starts[None, :], 0), axis=1) * PAGE_ROWS
    limit_at = jnp.sum(jnp.where(select, limits[None, :], 0), axis=1)
    segment = jnp.where(is_long, 0, prompt + 1)
    position = jnp.where(is_long, device_block * LONG_DEV + in_block, offset - begin_at)
    is_valid = is_long | (offset < limit_at)
    return (segment, position, is_valid)


def attend(carried, query_block, q_seg, q_pos, key_portion, value_portion, k_seg, k_pos, k_live):
    heads_kv = key_portion.shape[1] // HEAD_SIZE
    allowed = (
        (q_seg[:, None] == k_seg[None, :]) & (k_pos[None, :] <= q_pos[:, None]) & k_live[None, :]
    )

    def update(current):
        row_max, denom, weighted = current
        k_heads = key_portion.reshape(key_portion.shape[0], heads_kv, HEAD_SIZE)
        v_heads = value_portion.reshape(value_portion.shape[0], heads_kv, HEAD_SIZE)
        scores = jnp.einsum(
            "qhgd,khd->qhgk", query_block, k_heads, preferred_element_type=jnp.float32
        ) * HEAD_SIZE ** (-0.5)
        scores = jnp.where(allowed[:, None, None, :], scores, NEGATIVE_FILL)
        new_max = jnp.maximum(row_max, jnp.max(scores, axis=-1))
        factor = jnp.exp(row_max - new_max)
        weights = jnp.exp(scores - new_max[..., None])
        denom = denom * factor + jnp.sum(weights, axis=-1)
        weighted = weighted * factor[..., None] + jnp.einsum(
            "qhgk,khd->qhgd",
            weights.astype(jnp.bfloat16),
            v_heads,
            preferred_element_type=jnp.float32,
        )
        return (new_max, denom, weighted)

    return lax.cond(jnp.any(allowed), update, lambda current: current, carried)


def sweep(carried, queried, k_block, v_block, k_index, k_ok, layout, block_rows):
    query_block, q_seg, q_pos = queried
    segment, position, is_valid = layout
    step_total = k_block.shape[0] // block_rows

    def advance(step_id, current):
        leading_row = step_id * block_rows
        key_portion = lax.dynamic_slice_in_dim(k_block, leading_row, block_rows, 0)
        value_portion = lax.dynamic_slice_in_dim(v_block, leading_row, block_rows, 0)
        index_part = lax.dynamic_slice_in_dim(k_index, leading_row, block_rows, 0)
        ok_part = lax.dynamic_slice_in_dim(k_ok, leading_row, block_rows, 0)
        k_seg = jnp.take(segment, index_part)
        k_pos = jnp.take(position, index_part)
        k_live = jnp.take(is_valid, index_part) & ok_part
        return attend(
            current, query_block, q_seg, q_pos, key_portion, value_portion, k_seg, k_pos, k_live
        )

    return lax.fori_loop(0, step_total, advance, carried)


def local(
    queries,
    rotated_key_rows,
    stream_value_rows,
    out_weight,
    short_pages,
    short_fill,
    stream_page_table,
):
    req_count = lax.axis_size("req")
    my_index = lax.axis_index("req")
    tok_rows = queries.shape[0]
    heads_q = queries.shape[1] // HEAD_SIZE
    heads_kv = rotated_key_rows.shape[1] // HEAD_SIZE
    query_group_size = heads_q // heads_kv
    layout = stream_layout(short_pages, short_fill, req_count)
    segment, position, is_valid = layout
    own_index = my_index * tok_rows + jnp.arange(tok_rows, dtype=jnp.int32)
    query_block = queries.reshape(tok_rows, heads_kv, query_group_size, HEAD_SIZE)
    queried = (query_block, jnp.take(segment, own_index), jnp.take(position, own_index))
    q_live = jnp.take(is_valid, own_index)
    initial_state = (
        jnp.full((tok_rows, heads_kv, query_group_size), NEGATIVE_FILL, jnp.float32),
        jnp.zeros((tok_rows, heads_kv, query_group_size), jnp.float32),
        jnp.zeros((tok_rows, heads_kv, query_group_size, HEAD_SIZE), jnp.float32),
    )
    pieces = (
        lax.all_gather(rotated_key_rows, "req", axis=0, tiled=True),
        lax.all_gather(stream_value_rows, "req", axis=0, tiled=True),
    )
    piece_rows = pieces[0].shape[0]
    k_index = jnp.arange(piece_rows, dtype=jnp.int32)
    k_ok = jnp.ones((piece_rows,), bool)
    carried = sweep(initial_state, queried, pieces[0], pieces[1], k_index, k_ok, layout, tok_rows)
    row_max, denom, weighted = carried
    attended = weighted / denom[..., None]
    attended = jnp.where(q_live[:, None, None, None], attended, 0.0)
    attended = attended.reshape(tok_rows, heads_q * HEAD_SIZE).astype(jnp.bfloat16)
    mixed_out = lax.psum_scatter(
        jnp.dot(attended, out_weight, preferred_element_type=jnp.float32).astype(jnp.bfloat16),
        "tp",
        scatter_dimension=0,
        tiled=True,
    )
    pages_per = tok_rows // PAGE_ROWS
    capacity = (pages_per + req_count - 1) // req_count
    slot_count = capacity * req_count
    width = rotated_key_rows.shape[1]
    own_live = jnp.take(is_valid, own_index)
    kv_rows = jnp.stack([rotated_key_rows, stream_value_rows])
    kv_rows = jnp.where(own_live[None, :, None], kv_rows, jnp.zeros_like(kv_rows))
    kv_pages = kv_rows.reshape(2, pages_per, PAGE_ROWS * width)
    page_map = stream_page_table.reshape(req_count, pages_per)
    owners = page_map // slot_count
    earlier = (
        jnp.arange(pages_per, dtype=jnp.int32)[:, None]
        > jnp.arange(pages_per, dtype=jnp.int32)[None, :]
    )
    matching = owners[:, :, None] == owners[:, None, :]
    order_in = jnp.sum((matching & earlier[None]).astype(jnp.int32), axis=2)
    my_owner = owners[my_index]
    my_order = order_in[my_index]
    send_map = (
        (my_owner * capacity + my_order)[:, None]
        == jnp.arange(slot_count, dtype=jnp.int32)[None, :]
    ).astype(jnp.bfloat16)
    outgoing = jnp.einsum(
        "ks,xkr->xsr", send_map, kv_pages, preferred_element_type=jnp.float32
    ).astype(jnp.bfloat16)
    outgoing = outgoing.reshape(2, req_count, capacity, PAGE_ROWS * width)
    incoming = lax.all_to_all(outgoing, "req", split_axis=1, concat_axis=1, tiled=True)
    mine_mask = owners == my_index
    placing = mine_mask[:, :, None] & (
        order_in[:, :, None] == jnp.arange(capacity, dtype=jnp.int32)[None, None, :]
    )
    target = (page_map % slot_count)[:, :, None] == jnp.arange(slot_count, dtype=jnp.int32)[
        None, None, :
    ]
    routing = jnp.einsum(
        "skc,skt->sct",
        placing.astype(jnp.bfloat16),
        target.astype(jnp.bfloat16),
        preferred_element_type=jnp.float32,
    ).astype(jnp.bfloat16)
    written_cache = jnp.einsum(
        "sct,xscr->xtr", routing, incoming, preferred_element_type=jnp.float32
    ).astype(jnp.bfloat16)
    written_cache = written_cache.reshape(2, slot_count, PAGE_ROWS, width)
    return (mixed_out, written_cache)


def solution(mesh):
    in_specs = (P("req", "tp"), P("req", "tp"), P("req", "tp"), P("tp", None), P(), P(), P())
    out_specs = (P(("req", "tp"), None), P(None, "req", None, "tp"))
    return jax.shard_map(local, mesh=mesh, in_specs=in_specs, out_specs=out_specs, check_vma=False)
```

profile of v0, /device:TPU:29, one launch (start us, length us, event | category | flops | bytes accessed | tf_op | source)
XLA Modules:
  0.0 1270.9 jit_solution(17588710795483478737)
XLA Ops:
  33.2 119.4 %all-gather.3.cloned.1.call-done = bf16[10240,512]{0,1:T(8,128)(2,1)} async-done(((bf16[640,512]{0,1:T(8,128)(2,1)}), bf16[10240,512]{0,1:T(8,128)(2,1)}) %all-gather.3.cloned.1.call-update) | async-done | bytes 10485776 | tf_op jit(solution)/shard_map/all_gather | solution.py:114
  152.6 143.9 %all-gather.5.cloned.1.call-done = bf16[10240,512]{0,1:T(8,128)(2,1)} async-done(((bf16[640,512]{0,1:T(8,128)(2,1)}), bf16[10240,512]{0,1:T(8,128)(2,1)}) %all-gather.5.cloned.1.call-update) | async-done | bytes 10485776 | tf_op jit(solution)/shard_map/all_gather | solution.py:115
  299.5 836.2 %while.17 = (s32[]{:T(128)}, f32[640,4,4]{0,2,1:T(4,128)S(1)}, f32[640,4,4]{0,2,1:T(4,128)S(1)}, f32[640,4,4,128]{3,0,2,1:T(8,128)}, s32[640]{0:T(1024)S(1)}, /*...) while((s32[]{:T(128)}, f32[640,4,4]{0,2,1:T(4,128)S(1)}, ...), condition=%wide.region_10.13_spmd, body=%wide.region_4.12_spmd.sunk | while | flops 3432231424 | bytes 98033880 | solution.py:84
  313.6 40.7 %conditional.2 = ((f32[640,4,4]{0,2,1:T(4,128)S(1)}, f32[640,4,4]{0,2,1:T(4,128)S(1)}, f32[640,4,4,128]{3,0,2,1:T(8,128)})) conditional(s32[]{:T(128)} %convert_element_type.69, (f32[640,4,4]{0,2,1:T(4,128)S(1)}, f32[640,4,4]{0,2,1:T(4,128)S(1)}, f32[640,4,4,128]{3,0,2,1:T(8,128)}) %tuple.69, (pred[640,640]{0,1:T(8,128)(4,1)S(1)}, ...), branch_computations={%region_6.8_spmd, %region_7.11_spmd} | conditional | flops 3430174720 | bytes 97566752 | solution.py:63
  327.1 11.4 fusion.1
  338.6 15.7 %bitcast_add_fusion = f32[640,4,4,128]{3,0,2,1:T(8,128)} fusion(f32[640,4,4,128]{3,0,2,1:T(8,128)} %get-tuple-element.276, f32[640,4,4]{0,2,1:T(4,128)S(1)} %bitcast.72, bf16[640,4,128,1]{0,2,3,1:T(8,128)(2,1)} %bitcast.62, f32[4,640,640,4]{2,1,3,0:T(8,128)} %get-tuple-element.392, f32[640,4,4]{0,2,1:T(4,128)S(1)} %max.4, ...), kind=kOutput, calls=%fused_computation.13 | convolution fusion | flops 1706557440 | bytes 37847040 | tf_op jit(solution)/shard_map/while/body/eval_jaxpr/cond/branch_1_fun/qhgk,khd->qhgd/dot_general | solution.py:55
  368.4 40.7 %conditional.2 = ((f32[640,4,4]{0,2,1:T(4,128)S(1)}, f32[640,4,4]{0,2,1:T(4,128)S(1)}, f32[640,4,4,128]{3,0,2,1:T(8,128)})) conditional(s32[]{:T(128)} %convert_element_type.69, (f32[640,4,4]{0,2,1:T(4,128)S(1)}, f32[640,4,4]{0,2,1:T(4,128)S(1)}, f32[640,4,4,128]{3,0,2,1:T(8,128)}) %tuple.69, (pred[640,640]{0,1:T(8,128)(4,1)S(1)}, ...), branch_computations={%region_6.8_spmd, %region_7.11_spmd} | conditional | flops 3430174720 | bytes 97566752 | solution.py:63
  381.9 11.4 fusion.1
  393.4 15.7 %bitcast_add_fusion = f32[640,4,4,128]{3,0,2,1:T(8,128)} fusion(f32[640,4,4,128]{3,0,2,1:T(8,128)} %get-tuple-element.276, f32[640,4,4]{0,2,1:T(4,128)S(1)} %bitcast.72, bf16[640,4,128,1]{0,2,3,1:T(8,128)(2,1)} %bitcast.62, f32[4,640,640,4]{2,1,3,0:T(8,128)} %get-tuple-element.392, f32[640,4,4]{0,2,1:T(4,128)S(1)} %max.4, ...), kind=kOutput, calls=%fused_computation.13 | convolution fusion | flops 1706557440 | bytes 37847040 | tf_op jit(solution)/shard_map/while/body/eval_jaxpr/cond/branch_1_fun/qhgk,khd->qhgd/dot_general | solution.py:55
  423.2 40.7 %conditional.2 = ((f32[640,4,4]{0,2,1:T(4,128)S(1)}, f32[640,4,4]{0,2,1:T(4,128)S(1)}, f32[640,4,4,128]{3,0,2,1:T(8,128)})) conditional(s32[]{:T(128)} %convert_element_type.69, (f32[640,4,4]{0,2,1:T(4,128)S(1)}, f32[640,4,4]{0,2,1:T(4,128)S(1)}, f32[640,4,4,128]{3,0,2,1:T(8,128)}) %tuple.69, (pred[640,640]{0,1:T(8,128)(4,1)S(1)}, ...), branch_computations={%region_6.8_spmd, %region_7.11_spmd} | conditional | flops 3430174720 | bytes 97566752 | solution.py:63
  436.7 11.4 fusion.1
  448.2 15.7 %bitcast_add_fusion = f32[640,4,4,128]{3,0,2,1:T(8,128)} fusion(f32[640,4,4,128]{3,0,2,1:T(8,128)} %get-tuple-element.276, f32[640,4,4]{0,2,1:T(4,128)S(1)} %bitcast.72, bf16[640,4,128,1]{0,2,3,1:T(8,128)(2,1)} %bitcast.62, f32[4,640,640,4]{2,1,3,0:T(8,128)} %get-tuple-element.392, f32[640,4,4]{0,2,1:T(4,128)S(1)} %max.4, ...), kind=kOutput, calls=%fused_computation.13 | convolution fusion | flops 1706557440 | bytes 37847040 | tf_op jit(solution)/shard_map/while/body/eval_jaxpr/cond/branch_1_fun/qhgk,khd->qhgd/dot_general | solution.py:55
  478.0 40.7 %conditional.2 = ((f32[640,4,4]{0,2,1:T(4,128)S(1)}, f32[640,4,4]{0,2,1:T(4,128)S(1)}, f32[640,4,4,128]{3,0,2,1:T(8,128)})) conditional(s32[]{:T(128)} %convert_element_type.69, (f32[640,4,4]{0,2,1:T(4,128)S(1)}, f32[640,4,4]{0,2,1:T(4,128)S(1)}, f32[640,4,4,128]{3,0,2,1:T(8,128)}) %tuple.69, (pred[640,640]{0,1:T(8,128)(4,1)S(1)}, ...), branch_computations={%region_6.8_spmd, %region_7.11_spmd} | conditional | flops 3430174720 | bytes 97566752 | solution.py:63
  491.5 11.4 fusion.1
  503.0 15.7 %bitcast_add_fusion = f32[640,4,4,128]{3,0,2,1:T(8,128)} fusion(f32[640,4,4,128]{3,0,2,1:T(8,128)} %get-tuple-element.276, f32[640,4,4]{0,2,1:T(4,128)S(1)} %bitcast.72, bf16[640,4,128,1]{0,2,3,1:T(8,128)(2,1)} %bitcast.62, f32[4,640,640,4]{2,1,3,0:T(8,128)} %get-tuple-element.392, f32[640,4,4]{0,2,1:T(4,128)S(1)} %max.4, ...), kind=kOutput, calls=%fused_computation.13 | convolution fusion | flops 1706557440 | bytes 37847040 | tf_op jit(solution)/shard_map/while/body/eval_jaxpr/cond/branch_1_fun/qhgk,khd->qhgd/dot_general | solution.py:55
  532.9 40.7 %conditional.2 = ((f32[640,4,4]{0,2,1:T(4,128)S(1)}, f32[640,4,4]{0,2,1:T(4,128)S(1)}, f32[640,4,4,128]{3,0,2,1:T(8,128)})) conditional(s32[]{:T(128)} %convert_element_type.69, (f32[640,4,4]{0,2,1:T(4,128)S(1)}, f32[640,4,4]{0,2,1:T(4,128)S(1)}, f32[640,4,4,128]{3,0,2,1:T(8,128)}) %tuple.69, (pred[640,640]{0,1:T(8,128)(4,1)S(1)}, ...), branch_computations={%region_6.8_spmd, %region_7.11_spmd} | conditional | flops 3430174720 | bytes 97566752 | solution.py:63
  546.3 11.4 fusion.1
  557.8 15.7 %bitcast_add_fusion = f32[640,4,4,128]{3,0,2,1:T(8,128)} fusion(f32[640,4,4,128]{3,0,2,1:T(8,128)} %get-tuple-element.276, f32[640,4,4]{0,2,1:T(4,128)S(1)} %bitcast.72, bf16[640,4,128,1]{0,2,3,1:T(8,128)(2,1)} %bitcast.62, f32[4,640,640,4]{2,1,3,0:T(8,128)} %get-tuple-element.392, f32[640,4,4]{0,2,1:T(4,128)S(1)} %max.4, ...), kind=kOutput, calls=%fused_computation.13 | convolution fusion | flops 1706557440 | bytes 37847040 | tf_op jit(solution)/shard_map/while/body/eval_jaxpr/cond/branch_1_fun/qhgk,khd->qhgd/dot_general | solution.py:55
  587.7 40.7 %conditional.2 = ((f32[640,4,4]{0,2,1:T(4,128)S(1)}, f32[640,4,4]{0,2,1:T(4,128)S(1)}, f32[640,4,4,128]{3,0,2,1:T(8,128)})) conditional(s32[]{:T(128)} %convert_element_type.69, (f32[640,4,4]{0,2,1:T(4,128)S(1)}, f32[640,4,4]{0,2,1:T(4,128)S(1)}, f32[640,4,4,128]{3,0,2,1:T(8,128)}) %tuple.69, (pred[640,640]{0,1:T(8,128)(4,1)S(1)}, ...), branch_computations={%region_6.8_spmd, %region_7.11_spmd} | conditional | flops 3430174720 | bytes 97566752 | solution.py:63
  601.1 11.4 fusion.1
  612.6 15.7 %bitcast_add_fusion = f32[640,4,4,128]{3,0,2,1:T(8,128)} fusion(f32[640,4,4,128]{3,0,2,1:T(8,128)} %get-tuple-element.276, f32[640,4,4]{0,2,1:T(4,128)S(1)} %bitcast.72, bf16[640,4,128,1]{0,2,3,1:T(8,128)(2,1)} %bitcast.62, f32[4,640,640,4]{2,1,3,0:T(8,128)} %get-tuple-element.392, f32[640,4,4]{0,2,1:T(4,128)S(1)} %max.4, ...), kind=kOutput, calls=%fused_computation.13 | convolution fusion | flops 1706557440 | bytes 37847040 | tf_op jit(solution)/shard_map/while/body/eval_jaxpr/cond/branch_1_fun/qhgk,khd->qhgd/dot_general | solution.py:55
  642.5 40.7 %conditional.2 = ((f32[640,4,4]{0,2,1:T(4,128)S(1)}, f32[640,4,4]{0,2,1:T(4,128)S(1)}, f32[640,4,4,128]{3,0,2,1:T(8,128)})) conditional(s32[]{:T(128)} %convert_element_type.69, (f32[640,4,4]{0,2,1:T(4,128)S(1)}, f32[640,4,4]{0,2,1:T(4,128)S(1)}, f32[640,4,4,128]{3,0,2,1:T(8,128)}) %tuple.69, (pred[640,640]{0,1:T(8,128)(4,1)S(1)}, ...), branch_computations={%region_6.8_spmd, %region_7.11_spmd} | conditional | flops 3430174720 | bytes 97566752 | solution.py:63
  667.4 15.7 %bitcast_add_fusion = f32[640,4,4,128]{3,0,2,1:T(8,128)} fusion(f32[640,4,4,128]{3,0,2,1:T(8,128)} %get-tuple-element.276, f32[640,4,4]{0,2,1:T(4,128)S(1)} %bitcast.72, bf16[640,4,128,1]{0,2,3,1:T(8,128)(2,1)} %bitcast.62, f32[4,640,640,4]{2,1,3,0:T(8,128)} %get-tuple-element.392, f32[640,4,4]{0,2,1:T(4,128)S(1)} %max.4, ...), kind=kOutput, calls=%fused_computation.13 | convolution fusion | flops 1706557440 | bytes 37847040 | tf_op jit(solution)/shard_map/while/body/eval_jaxpr/cond/branch_1_fun/qhgk,khd->qhgd/dot_general | solution.py:55
  697.3 40.7 %conditional.2 = ((f32[640,4,4]{0,2,1:T(4,128)S(1)}, f32[640,4,4]{0,2,1:T(4,128)S(1)}, f32[640,4,4,128]{3,0,2,1:T(8,128)})) conditional(s32[]{:T(128)} %convert_element_type.69, (f32[640,4,4]{0,2,1:T(4,128)S(1)}, f32[640,4,4]{0,2,1:T(4,128)S(1)}, f32[640,4,4,128]{3,0,2,1:T(8,128)}) %tuple.69, (pred[640,640]{0,1:T(8,128)(4,1)S(1)}, ...), branch_computations={%region_6.8_spmd, %region_7.11_spmd} | conditional | flops 3430174720 | bytes 97566752 | solution.py:63
  710.7 11.4 fusion.1
  722.2 15.7 %bitcast_add_fusion = f32[640,4,4,128]{3,0,2,1:T(8,128)} fusion(f32[640,4,4,128]{3,0,2,1:T(8,128)} %get-tuple-element.276, f32[640,4,4]{0,2,1:T(4,128)S(1)} %bitcast.72, bf16[640,4,128,1]{0,2,3,1:T(8,128)(2,1)} %bitcast.62, f32[4,640,640,4]{2,1,3,0:T(8,128)} %get-tuple-element.392, f32[640,4,4]{0,2,1:T(4,128)S(1)} %max.4, ...), kind=kOutput, calls=%fused_computation.13 | convolution fusion | flops 1706557440 | bytes 37847040 | tf_op jit(solution)/shard_map/while/body/eval_jaxpr/cond/branch_1_fun/qhgk,khd->qhgd/dot_general | solution.py:55
  752.1 40.7 %conditional.2 = ((f32[640,4,4]{0,2,1:T(4,128)S(1)}, f32[640,4,4]{0,2,1:T(4,128)S(1)}, f32[640,4,4,128]{3,0,2,1:T(8,128)})) conditional(s32[]{:T(128)} %convert_element_type.69, (f32[640,4,4]{0,2,1:T(4,128)S(1)}, f32[640,4,4]{0,2,1:T(4,128)S(1)}, f32[640,4,4,128]{3,0,2,1:T(8,128)}) %tuple.69, (pred[640,640]{0,1:T(8,128)(4,1)S(1)}, ...), branch_computations={%region_6.8_spmd, %region_7.11_spmd} | conditional | flops 3430174720 | bytes 97566752 | solution.py:63
  765.5 11.4 fusion.1
  777.0 15.7 %bitcast_add_fusion = f32[640,4,4,128]{3,0,2,1:T(8,128)} fusion(f32[640,4,4,128]{3,0,2,1:T(8,128)} %get-tuple-element.276, f32[640,4,4]{0,2,1:T(4,128)S(1)} %bitcast.72, bf16[640,4,128,1]{0,2,3,1:T(8,128)(2,1)} %bitcast.62, f32[4,640,640,4]{2,1,3,0:T(8,128)} %get-tuple-element.392, f32[640,4,4]{0,2,1:T(4,128)S(1)} %max.4, ...), kind=kOutput, calls=%fused_computation.13 | convolution fusion | flops 1706557440 | bytes 37847040 | tf_op jit(solution)/shard_map/while/body/eval_jaxpr/cond/branch_1_fun/qhgk,khd->qhgd/dot_general | solution.py:55
  806.9 40.7 %conditional.2 = ((f32[640,4,4]{0,2,1:T(4,128)S(1)}, f32[640,4,4]{0,2,1:T(4,128)S(1)}, f32[640,4,4,128]{3,0,2,1:T(8,128)})) conditional(s32[]{:T(128)} %convert_element_type.69, (f32[640,4,4]{0,2,1:T(4,128)S(1)}, f32[640,4,4]{0,2,1:T(4,128)S(1)}, f32[640,4,4,128]{3,0,2,1:T(8,128)}) %tuple.69, (pred[640,640]{0,1:T(8,128)(4,1)S(1)}, ...), branch_computations={%region_6.8_spmd, %region_7.11_spmd} | conditional | flops 3430174720 | bytes 97566752 | solution.py:63
  820.3 11.4 fusion.1
  831.8 15.7 %bitcast_add_fusion = f32[640,4,4,128]{3,0,2,1:T(8,128)} fusion(f32[640,4,4,128]{3,0,2,1:T(8,128)} %get-tuple-element.276, f32[640,4,4]{0,2,1:T(4,128)S(1)} %bitcast.72, bf16[640,4,128,1]{0,2,3,1:T(8,128)(2,1)} %bitcast.62, f32[4,640,640,4]{2,1,3,0:T(8,128)} %get-tuple-element.392, f32[640,4,4]{0,2,1:T(4,128)S(1)} %max.4, ...), kind=kOutput, calls=%fused_computation.13 | convolution fusion | flops 1706557440 | bytes 37847040 | tf_op jit(solution)/shard_map/while/body/eval_jaxpr/cond/branch_1_fun/qhgk,khd->qhgd/dot_general | solution.py:55
  861.7 40.7 %conditional.2 = ((f32[640,4,4]{0,2,1:T(4,128)S(1)}, f32[640,4,4]{0,2,1:T(4,128)S(1)}, f32[640,4,4,128]{3,0,2,1:T(8,128)})) conditional(s32[]{:T(128)} %convert_element_type.69, (f32[640,4,4]{0,2,1:T(4,128)S(1)}, f32[640,4,4]{0,2,1:T(4,128)S(1)}, f32[640,4,4,128]{3,0,2,1:T(8,128)}) %tuple.69, (pred[640,640]{0,1:T(8,128)(4,1)S(1)}, ...), branch_computations={%region_6.8_spmd, %region_7.11_spmd} | conditional | flops 3430174720 | bytes 97566752 | solution.py:63
  875.1 11.4 fusion.1
  886.6 15.7 %bitcast_add_fusion = f32[640,4,4,128]{3,0,2,1:T(8,128)} fusion(f32[640,4,4,128]{3,0,2,1:T(8,128)} %get-tuple-element.276, f32[640,4,4]{0,2,1:T(4,128)S(1)} %bitcast.72, bf16[640,4,128,1]{0,2,3,1:T(8,128)(2,1)} %bitcast.62, f32[4,640,640,4]{2,1,3,0:T(8,128)} %get-tuple-element.392, f32[640,4,4]{0,2,1:T(4,128)S(1)} %max.4, ...), kind=kOutput, calls=%fused_computation.13 | convolution fusion | flops 1706557440 | bytes 37847040 | tf_op jit(solution)/shard_map/while/body/eval_jaxpr/cond/branch_1_fun/qhgk,khd->qhgd/dot_general | solution.py:55
  916.5 40.7 %conditional.2 = ((f32[640,4,4]{0,2,1:T(4,128)S(1)}, f32[640,4,4]{0,2,1:T(4,128)S(1)}, f32[640,4,4,128]{3,0,2,1:T(8,128)})) conditional(s32[]{:T(128)} %convert_element_type.69, (f32[640,4,4]{0,2,1:T(4,128)S(1)}, f32[640,4,4]{0,2,1:T(4,128)S(1)}, f32[640,4,4,128]{3,0,2,1:T(8,128)}) %tuple.69, (pred[640,640]{0,1:T(8,128)(4,1)S(1)}, ...), branch_computations={%region_6.8_spmd, %region_7.11_spmd} | conditional | flops 3430174720 | bytes 97566752 | solution.py:63
  941.4 15.7 %bitcast_add_fusion = f32[640,4,4,128]{3,0,2,1:T(8,128)} fusion(f32[640,4,4,128]{3,0,2,1:T(8,128)} %get-tuple-element.276, f32[640,4,4]{0,2,1:T(4,128)S(1)} %bitcast.72, bf16[640,4,128,1]{0,2,3,1:T(8,128)(2,1)} %bitcast.62, f32[4,640,640,4]{2,1,3,0:T(8,128)} %get-tuple-element.392, f32[640,4,4]{0,2,1:T(4,128)S(1)} %max.4, ...), kind=kOutput, calls=%fused_computation.13 | convolution fusion | flops 1706557440 | bytes 37847040 | tf_op jit(solution)/shard_map/while/body/eval_jaxpr/cond/branch_1_fun/qhgk,khd->qhgd/dot_general | solution.py:55
  971.3 40.7 %conditional.2 = ((f32[640,4,4]{0,2,1:T(4,128)S(1)}, f32[640,4,4]{0,2,1:T(4,128)S(1)}, f32[640,4,4,128]{3,0,2,1:T(8,128)})) conditional(s32[]{:T(128)} %convert_element_type.69, (f32[640,4,4]{0,2,1:T(4,128)S(1)}, f32[640,4,4]{0,2,1:T(4,128)S(1)}, f32[640,4,4,128]{3,0,2,1:T(8,128)}) %tuple.69, (pred[640,640]{0,1:T(8,128)(4,1)S(1)}, ...), branch_computations={%region_6.8_spmd, %region_7.11_spmd} | conditional | flops 3430174720 | bytes 97566752 | solution.py:63
  984.7 11.4 fusion.1
  996.2 15.7 %bitcast_add_fusion = f32[640,4,4,128]{3,0,2,1:T(8,128)} fusion(f32[640,4,4,128]{3,0,2,1:T(8,128)} %get-tuple-element.276, f32[640,4,4]{0,2,1:T(4,128)S(1)} %bitcast.72, bf16[640,4,128,1]{0,2,3,1:T(8,128)(2,1)} %bitcast.62, f32[4,640,640,4]{2,1,3,0:T(8,128)} %get-tuple-element.392, f32[640,4,4]{0,2,1:T(4,128)S(1)} %max.4, ...), kind=kOutput, calls=%fused_computation.13 | convolution fusion | flops 1706557440 | bytes 37847040 | tf_op jit(solution)/shard_map/while/body/eval_jaxpr/cond/branch_1_fun/qhgk,khd->qhgd/dot_general | solution.py:55
  1026.1 40.7 %conditional.2 = ((f32[640,4,4]{0,2,1:T(4,128)S(1)}, f32[640,4,4]{0,2,1:T(4,128)S(1)}, f32[640,4,4,128]{3,0,2,1:T(8,128)})) conditional(s32[]{:T(128)} %convert_element_type.69, (f32[640,4,4]{0,2,1:T(4,128)S(1)}, f32[640,4,4]{0,2,1:T(4,128)S(1)}, f32[640,4,4,128]{3,0,2,1:T(8,128)}) %tuple.69, (pred[640,640]{0,1:T(8,128)(4,1)S(1)}, ...), branch_computations={%region_6.8_spmd, %region_7.11_spmd} | conditional | flops 3430174720 | bytes 97566752 | solution.py:63
  1051.0 15.7 %bitcast_add_fusion = f32[640,4,4,128]{3,0,2,1:T(8,128)} fusion(f32[640,4,4,128]{3,0,2,1:T(8,128)} %get-tuple-element.276, f32[640,4,4]{0,2,1:T(4,128)S(1)} %bitcast.72, bf16[640,4,128,1]{0,2,3,1:T(8,128)(2,1)} %bitcast.62, f32[4,640,640,4]{2,1,3,0:T(8,128)} %get-tuple-element.392, f32[640,4,4]{0,2,1:T(4,128)S(1)} %max.4, ...), kind=kOutput, calls=%fused_computation.13 | convolution fusion | flops 1706557440 | bytes 37847040 | tf_op jit(solution)/shard_map/while/body/eval_jaxpr/cond/branch_1_fun/qhgk,khd->qhgd/dot_general | solution.py:55
  1080.9 40.7 %conditional.2 = ((f32[640,4,4]{0,2,1:T(4,128)S(1)}, f32[640,4,4]{0,2,1:T(4,128)S(1)}, f32[640,4,4,128]{3,0,2,1:T(8,128)})) conditional(s32[]{:T(128)} %convert_element_type.69, (f32[640,4,4]{0,2,1:T(4,128)S(1)}, f32[640,4,4]{0,2,1:T(4,128)S(1)}, f32[640,4,4,128]{3,0,2,1:T(8,128)}) %tuple.69, (pred[640,640]{0,1:T(8,128)(4,1)S(1)}, ...), branch_computations={%region_6.8_spmd, %region_7.11_spmd} | conditional | flops 3430174720 | bytes 97566752 | solution.py:63
  1094.3 11.4 fusion.1
  1105.8 15.7 %bitcast_add_fusion = f32[640,4,4,128]{3,0,2,1:T(8,128)} fusion(f32[640,4,4,128]{3,0,2,1:T(8,128)} %get-tuple-element.276, f32[640,4,4]{0,2,1:T(4,128)S(1)} %bitcast.72, bf16[640,4,128,1]{0,2,3,1:T(8,128)(2,1)} %bitcast.62, f32[4,640,640,4]{2,1,3,0:T(8,128)} %get-tuple-element.392, f32[640,4,4]{0,2,1:T(4,128)S(1)} %max.4, ...), kind=kOutput, calls=%fused_computation.13 | convolution fusion | flops 1706557440 | bytes 37847040 | tf_op jit(solution)/shard_map/while/body/eval_jaxpr/cond/branch_1_fun/qhgk,khd->qhgd/dot_general | solution.py:55
  1144.9 27.9 %convolution_convert_fusion = bf16[640,8192]{1,0:T(8,128)(2,1)} fusion(bf16[640,2048]{0,1:T(8,128)(2,1)S(1)} %bitcast.67, bf16[2048,8192]{1,0:T(8,128)(2,1)} %param.18), kind=kOutput, calls=%fused_computation.27 | convolution fusion | flops 21480079360 | bytes 46661632 | tf_op jit(solution)/shard_map/dot_general | solution.py:126
  1179.3 47.0 %all-to-all-start = ((bf16[2,16,3,8192]{3,0,2,1:T(2,128)(2,1)}), bf16[2,16,3,8192]{3,0,2,1:T(2,128)(2,1)S(1)}, u32[]{:S(2)}, u32[]{:S(2)}) async-start(bf16[2,16,3,8192]{3,0,2,1:T(2,128)(2,1)} %bitcast.12), calls=%async_computation.1 | async-start | bytes 3145728 | tf_op jit(solution)/shard_map/all_to_all | solution.py:157
  1226.5 34.9 %all-to-all-done = bf16[2,16,3,8192]{3,0,2,1:T(2,128)(2,1)S(1)} async-done(((bf16[2,16,3,8192]{3,0,2,1:T(2,128)(2,1)}), bf16[2,16,3,8192]{3,0,2,1:T(2,128)(2,1)S(1)}, u32[]{:S(2)}, u32[]{:S(2)}) %all-to-all-start) | async-done | bytes 1572896 | tf_op jit(solution)/shard_map/all_to_all | solution.py:157
  (271 shorter events, 499.2 us)
Async XLA Ops:
  7.2 145.5 %all-gather.3.cloned.1.call-start = ((), (), s32[]{:S(2)}) async-start(), calls=%async_computation.2 | async-start | bytes 11141120 | tf_op jit(solution)/shard_map/all_gather | solution.py:114
  9.4 13.1 %copy-start = (bf16[640,2048]{1,0:T(8,128)(2,1)S(1)}, bf16[640,2048]{1,0:T(8,128)(2,1)}, u32[]{:S(2)}) copy-start(bf16[640,2048]{1,0:T(8,128)(2,1)} %param.15) | copy-start | bytes 7864324
  9.4 287.1 %all-gather.5.cloned.1.call-start = ((), (), s32[]{:S(2)}) async-start(), calls=%async_computation.3 | async-start | bytes 11141120 | tf_op jit(solution)/shard_map/all_gather | solution.py:115
  11.8 1252.6 %reduce-scatter.2.cloned.1.call-start = ((), (), s32[]{:S(2)}) async-start(), calls=%async_computation.4 | async-start | bytes 15728640 | tf_op jit(solution)/shard_map/reduce_scatter | solution.py:125
  1135.7 6.1 copy-start.4
  1172.8 1.1 copy-start.1
  1172.8 1.4 copy-start.2
  1172.8 2.2 copy-start.3
  1179.3 82.1 %all-to-all-start = ((bf16[2,16,3,8192]{3,0,2,1:T(2,128)(2,1)}), bf16[2,16,3,8192]{3,0,2,1:T(2,128)(2,1)S(1)}, u32[]{:S(2)}, u32[]{:S(2)}) async-start(bf16[2,16,3,8192]{3,0,2,1:T(2,128)(2,1)} %bitcast.12), calls=%async_computation.1 | async-start | bytes 3145728 | tf_op jit(solution)/shard_map/all_to_all | solution.py:157
Sparse Core Ops, SparseCore 0:
  11.3 141.2 all-gather.2
  155.3 141.1 all-gather.4
  1173.0 61.0 reduce-scatter.1
where the time goes:
time: 1280 us; the launch traced here: 1270 us
  matrix products  433 us (34%)
  waiting for transfers between devices  298 us (23%)
  local copies, waits for them, and re-layouts  265 us (21%)
  other arithmetic  202 us (16%)
  starting transfers between devices  47.1 us (4%)
  between operations  14 us (1%)
    dot_general x15, matrix products, update(): jnp.einsum('qhgk,khd->qhgd', weights.astype(jnp.bfloat16), v_heads, prefe...  236 us
    reduce_sum x15, other arithmetic, update(): denom = denom * factor + jnp.sum(weights, axis=-1)  171 us
    dot_general x15, matrix products, update(): jnp.einsum('qhgd,khd->qhgk', query_block, k_heads, preferred_element_type...  167 us
    all_gather x1, waiting for transfers between devices, local(): lax.all_gather(stream_value_rows, 'req', axis=0, tiled=True)  144 us
    all_gather x1, waiting for transfers between devices, local(): lax.all_gather(rotated_key_rows, 'req', axis=0, tiled=True)  119 us
    gather x16, local copies, waits for them, and re-layouts, advance(): k_live = jnp.take(is_valid, index_part) & ok_part  68.6 us
    gather x16, local copies, waits for them, and re-layouts, advance(): k_pos = jnp.take(position, index_part)  61.7 us
    gather x16, local copies, waits for them, and re-layouts, advance(): k_seg = jnp.take(segment, index_part)  61.6 us
  transfers between devices with their start and end apart: 4, of which 3 were waited for; matrix products, arithmetic and copies ran while one was open for 3% of the time, Pallas kernels for 0%

commit v1 on v0

v1 whole, which is shorter than its diff:
```python
import functools

import jax
import jax.numpy as jnp
from jax import lax
from jax.experimental import pallas as pl
from jax.experimental.pallas import tpu as pltpu
from jax.sharding import PartitionSpec as P

HEAD_SIZE = 128
LONG_DEV = 512
SHORT_DEV = 128
PAGE_ROWS = 16
BLOCK_TOKENS = 640


NEGATIVE_FILL = -1e30


def short_layout(offset, short_pages, short_fill):
    page_id = offset // PAGE_ROWS
    page_ends = jnp.cumsum(short_pages)
    page_starts = page_ends - short_pages
    limits = page_starts * PAGE_ROWS + (short_pages - 1) * PAGE_ROWS + short_fill
    owner_hit = page_ends[None, :] <= page_id[:, None]
    prompt = jnp.sum(owner_hit.astype(jnp.int32), axis=1)
    select = jnp.arange(short_pages.shape[0], dtype=jnp.int32)[None, :] == prompt[:, None]
    begin_at = jnp.sum(jnp.where(select, page_starts[None, :], 0), axis=1) * PAGE_ROWS
    limit_at = jnp.sum(jnp.where(select, limits[None, :], 0), axis=1)
    return (prompt, offset - begin_at, offset < limit_at)


def flash_kernel(b_ref, q_ref, k_ref, v_ref, o_ref, m_sc, l_sc, acc_sc, *, group, tq, nb):
    i = pl.program_id(1)
    j = pl.program_id(2)
    b = b_ref[0]
    scale = HEAD_SIZE ** (-0.5)

    @pl.when(j == 0)
    def _init():
        m_sc[...] = jnp.full(m_sc.shape, NEGATIVE_FILL, jnp.float32)
        l_sc[...] = jnp.zeros(l_sc.shape, jnp.float32)
        acc_sc[...] = jnp.zeros(acc_sc.shape, jnp.float32)

    def step(masked):
        k = k_ref[...]
        v = v_ref[...]
        if masked:
            rows = i * tq + lax.broadcasted_iota(jnp.int32, (tq, k.shape[0]), 0)
            cols = lax.broadcasted_iota(jnp.int32, (tq, k.shape[0]), 1)
            allowed = cols <= rows
        for g in range(group):
            qg = q_ref[:, g * HEAD_SIZE:(g + 1) * HEAD_SIZE]
            s = lax.dot_general(
                qg, k, (((1,), (1,)), ((), ())), preferred_element_type=jnp.float32
            ) * scale
            if masked:
                s = jnp.where(allowed, s, NEGATIVE_FILL)
            m_prev = m_sc[g]
            m_new = jnp.maximum(m_prev, jnp.max(s, axis=1, keepdims=True))
            p = jnp.exp(s - m_new[:, :1])
            alpha = jnp.exp(m_prev - m_new)
            l_sc[g] = alpha * l_sc[g] + jnp.sum(p, axis=1, keepdims=True)
            acc_sc[g] = acc_sc[g] * alpha + lax.dot_general(
                p.astype(jnp.bfloat16), v, (((1,), (0,)), ((), ())),
                preferred_element_type=jnp.float32,
            )
            m_sc[g] = m_new

    @pl.when(j < b)
    def _full():
        step(False)

    @pl.when(j == b)
    def _diag():
        step(True)

    @pl.when(j == nb - 1)
    def _fin():
        for g in range(group):
            o_ref[:, g * HEAD_SIZE:(g + 1) * HEAD_SIZE] = (acc_sc[g] / l_sc[g]).astype(o_ref.dtype)


def long_attention(my_index, q_long, kv_long):
    rows, q_cols = q_long.shape
    kv_cols = kv_long.shape[1] // 2
    heads_kv = kv_cols // HEAD_SIZE
    group = q_cols // kv_cols
    nb = kv_long.shape[0] // LONG_DEV
    tq = LONG_DEV
    kernel = functools.partial(flash_kernel, group=group, tq=tq, nb=nb)
    grid_spec = pltpu.PrefetchScalarGridSpec(
        num_scalar_prefetch=1,
        grid=(heads_kv, rows // tq, nb),
        in_specs=[
            pl.BlockSpec((tq, group * HEAD_SIZE), lambda h, i, j, b: (i, h)),
            pl.BlockSpec((LONG_DEV, HEAD_SIZE), lambda h, i, j, b: (jnp.minimum(j, b[0]), h)),
            pl.BlockSpec(
                (LONG_DEV, HEAD_SIZE), lambda h, i, j, b: (jnp.minimum(j, b[0]), heads_kv + h)
            ),
        ],
        out_specs=pl.BlockSpec((tq, group * HEAD_SIZE), lambda h, i, j, b: (i, h)),
        scratch_shapes=[
            pltpu.VMEM((group, tq, HEAD_SIZE), jnp.float32),
            pltpu.VMEM((group, tq, HEAD_SIZE), jnp.float32),
            pltpu.VMEM((group, tq, HEAD_SIZE), jnp.float32),
        ],
    )
    b_arr = jnp.reshape(my_index, (1,)).astype(jnp.int32)
    return pl.pallas_call(
        kernel,
        grid_spec=grid_spec,
        out_shape=jax.ShapeDtypeStruct((rows, q_cols), jnp.bfloat16),
        compiler_params=pltpu.CompilerParams(
            dimension_semantics=("arbitrary", "arbitrary", "arbitrary")
        ),
    )(b_arr, q_long, kv_long, kv_long)


def short_attention(my_index, req_count, q_short, k_short, v_short, short_pages, short_fill):
    heads_kv = k_short.shape[1] // HEAD_SIZE
    group = q_short.shape[1] // k_short.shape[1]
    perm = [(s, s + 1) for s in range(req_count - 1)]
    k_prev = lax.ppermute(k_short, "req", perm)
    v_prev = lax.ppermute(v_short, "req", perm)
    own_off = my_index * SHORT_DEV + jnp.arange(SHORT_DEV, dtype=jnp.int32)
    key_off = (my_index - 1) * SHORT_DEV + jnp.arange(2 * SHORT_DEV, dtype=jnp.int32)
    q_seg, q_pos, q_live = short_layout(own_off, short_pages, short_fill)
    k_seg, k_pos, k_live = short_layout(key_off, short_pages, short_fill)
    k_live = k_live & (key_off >= 0)
    allowed = (q_seg[:, None] == k_seg[None, :]) & (k_pos[None, :] <= q_pos[:, None]) & k_live[None, :]
    keys = jnp.concatenate([k_prev, k_short]).reshape(2 * SHORT_DEV, heads_kv, HEAD_SIZE)
    values = jnp.concatenate([v_prev, v_short]).reshape(2 * SHORT_DEV, heads_kv, HEAD_SIZE)
    qs = q_short.reshape(SHORT_DEV, heads_kv, group, HEAD_SIZE)
    scores = jnp.einsum(
        "qhgd,khd->hgqk", qs, keys, preferred_element_type=jnp.float32
    ) * HEAD_SIZE ** (-0.5)
    scores = jnp.where(allowed[None, None], scores, NEGATIVE_FILL)
    row_max = jnp.max(scores, axis=-1, keepdims=True)
    weights = jnp.exp(scores - row_max)
    denom = jnp.sum(weights, axis=-1)
    weighted = jnp.einsum(
        "hgqk,khd->qhgd", weights.astype(jnp.bfloat16), values, preferred_element_type=jnp.float32
    )
    attended = weighted / jnp.transpose(denom, (2, 0, 1))[..., None]
    attended = jnp.where(q_live[:, None, None, None], attended, 0.0)
    return attended.reshape(SHORT_DEV, -1).astype(jnp.bfloat16)


def local(
    queries,
    rotated_key_rows,
    stream_value_rows,
    out_weight,
    short_pages,
    short_fill,
    stream_page_table,
):
    req_count = lax.axis_size("req")
    my_index = lax.axis_index("req")
    tok_rows = queries.shape[0]
    kv_long = jnp.concatenate(
        [rotated_key_rows[:LONG_DEV], stream_value_rows[:LONG_DEV]], axis=1
    )
    kv_long = lax.all_gather(kv_long, "req", axis=0, tiled=True)
    att_long = long_attention(my_index, queries[:LONG_DEV], kv_long)
    att_short = short_attention(
        my_index,
        req_count,
        queries[LONG_DEV:],
        rotated_key_rows[LONG_DEV:],
        stream_value_rows[LONG_DEV:],
        short_pages,
        short_fill,
    )
    attended = jnp.concatenate([att_long, att_short])
    mixed_out = lax.psum_scatter(
        jnp.dot(attended, out_weight, preferred_element_type=jnp.float32).astype(jnp.bfloat16),
        "tp",
        scatter_dimension=0,
        tiled=True,
    )
    pages_per = tok_rows // PAGE_ROWS
    capacity = (pages_per + req_count - 1) // req_count
    slot_count = capacity * req_count
    width = rotated_key_rows.shape[1]
    own_off = my_index * SHORT_DEV + jnp.arange(SHORT_DEV, dtype=jnp.int32)
    short_live = short_layout(own_off, short_pages, short_fill)[2]
    own_live = jnp.concatenate([jnp.ones((LONG_DEV,), bool), short_live])
    kv_rows = jnp.stack([rotated_key_rows, stream_value_rows])
    kv_rows = jnp.where(own_live[None, :, None], kv_rows, jnp.zeros_like(kv_rows))
    kv_pages = kv_rows.reshape(2, pages_per, PAGE_ROWS * width)
    page_map = stream_page_table.reshape(req_count, pages_per)
    owners = page_map // slot_count
    earlier = (
        jnp.arange(pages_per, dtype=jnp.int32)[:, None]
        > jnp.arange(pages_per, dtype=jnp.int32)[None, :]
    )
    matching = owners[:, :, None] == owners[:, None, :]
    order_in = jnp.sum((matching & earlier[None]).astype(jnp.int32), axis=2)
    my_owner = owners[my_index]
    my_order = order_in[my_index]
    send_map = (
        (my_owner * capacity + my_order)[:, None]
        == jnp.arange(slot_count, dtype=jnp.int32)[None, :]
    ).astype(jnp.bfloat16)
    outgoing = jnp.einsum(
        "ks,xkr->xsr", send_map, kv_pages, preferred_element_type=jnp.float32
    ).astype(jnp.bfloat16)
    outgoing = outgoing.reshape(2, req_count, capacity, PAGE_ROWS * width)
    incoming = lax.all_to_all(outgoing, "req", split_axis=1, concat_axis=1, tiled=True)
    mine_mask = owners == my_index
    placing = mine_mask[:, :, None] & (
        order_in[:, :, None] == jnp.arange(capacity, dtype=jnp.int32)[None, None, :]
    )
    target = (page_map % slot_count)[:, :, None] == jnp.arange(slot_count, dtype=jnp.int32)[
        None, None, :
    ]
    routing = jnp.einsum(
        "skc,skt->sct",
        placing.astype(jnp.bfloat16),
        target.astype(jnp.bfloat16),
        preferred_element_type=jnp.float32,
    ).astype(jnp.bfloat16)
    written_cache = jnp.einsum(
        "sct,xscr->xtr", routing, incoming, preferred_element_type=jnp.float32
    ).astype(jnp.bfloat16)
    written_cache = written_cache.reshape(2, slot_count, PAGE_ROWS, width)
    return (mixed_out, written_cache)


def solution(mesh):
    in_specs = (P("req", "tp"), P("req", "tp"), P("req", "tp"), P("tp", None), P(), P(), P())
    out_specs = (P(("req", "tp"), None), P(None, "req", None, "tp"))
    return jax.shard_map(local, mesh=mesh, in_specs=in_specs, out_specs=out_specs, check_vma=False)
```

time: 1280 us -> 478 us (0.37)
  matrix products: 433 us -> 31.1 us
  local copies, waits for them, and re-layouts: 265 us -> 11.3 us
  other arithmetic: 202 us -> 4.64 us
  Pallas kernels: 0 us -> 179 us
  waiting for transfers between devices: 298 us -> 215 us
  starting transfers between devices: 47.1 us -> 18.7 us
    dot_general x30 -> x2, matrix products: 403 us -> 1.02 us  [the longest x1 0.51 us: short_attention(): jnp.einsum('hgqk,khd->qhgd', weights.astype(jnp.bfloat16), values, prefer...]
    gather x51 -> x0, local copies, waits for them, and re-layouts: 204 us -> none  [the longest x16 68.6 us: advance(): k_live = jnp.take(is_valid, index_part) & ok_part]
    pallas_call x0 -> x1, Pallas kernels: none -> 179 us  [long_attention(): pl.pallas_call(kernel, grid_spec=grid_spec, out_shape=jax.ShapeDtypeStruc...]
    reduce_sum x17 -> x5, other arithmetic: 173 us -> 0.68 us  [the longest x1 0.31 us: short_attention(): denom = jnp.sum(weights, axis=-1)]
    all_gather x2 -> x1, waiting for transfers between devices: 263 us -> 178 us  [local(): kv_long = lax.all_gather(kv_long, 'req', axis=0, tiled=True)]
    dynamic_slice x15 -> x0, local copies, waits for them, and re-layouts: 33.7 us -> none  [advance(): lax.dynamic_slice_in_dim(v_block, leading_row, block_rows, 0)]
    all_to_all x1, starting transfers between devices: 47 us -> 13.6 us  [local(): lax.all_to_all(outgoing, 'req', split_axis=1, concat_axis=1, tiled=True)]
    reduce_or x16 -> x0, other arithmetic: 20.7 us -> none  [attend(): return lax.cond(jnp.any(allowed), update, lambda current: current, carried)]
  transfers between devices with their start and end apart: 4 -> 5, of which waited for: 3 -> 3; matrix products, arithmetic and copies ran while one was open for 3% -> 3% of each run, Pallas kernels for 0% -> 0%
where the time goes in v1:
time: 478 us; the launch traced here: 475 us
  waiting for transfers between devices  215 us (45%)
  Pallas kernels  179 us (37%)
  matrix products  31.1 us (7%)
  starting transfers between devices  18.7 us (4%)
  between operations  14.4 us (3%)
  local copies, waits for them, and re-layouts  11.3 us (2%)
    pallas_call x1, Pallas kernels, long_attention(): pl.pallas_call(kernel, grid_spec=grid_spec, out_shape=jax.ShapeDtypeStruc...  179 us
    all_gather x1, waiting for transfers between devices, local(): kv_long = lax.all_gather(kv_long, 'req', axis=0, tiled=True)  178 us
    all_to_all x1, waiting for transfers between devices, local(): lax.all_to_all(outgoing, 'req', split_axis=1, concat_axis=1, tiled=True)  34.9 us
    dot_general x1, matrix products, local(): jnp.dot(attended, out_weight, preferred_element_type=jnp.float32)  27.9 us
    all_to_all x1, starting transfers between devices, local(): lax.all_to_all(outgoing, 'req', split_axis=1, concat_axis=1, tiled=True)  13.6 us
  transfers between devices with their start and end apart: 5, of which 3 were waited for; matrix products, arithmetic and copies ran while one was open for 3% of the time, Pallas kernels for 0%

profile of v1, /device:TPU:29, one launch (start us, length us, event | category | flops | bytes accessed | tf_op | source)
XLA Modules:
  0.0 474.6 jit_solution(6979154860357708632)
XLA Ops:
  7.2 0.0 all-gather.2.cloned.1.call-start
  7.2 1.0 slice-done.1
  8.2 0.2 slice-done.2
  8.4 1.1 pad_maximum_fusion
  9.5 0.0 all-gather.2.cloned.1.call-update
  9.5 0.0 reduce-scatter.2.cloned.1.call-start
  9.6 0.1 copy.66
  9.7 3.1 collective-permute-start.1
  12.8 0.9 slice.21
  13.8 1.9 collective-permute-start
  15.7 0.1 copy.47
  15.8 0.1 reduce-window.8
  15.9 0.1 reduce
  16.0 0.1 convert_reduce_fusion.2
  16.1 0.1 convert_reduce_fusion.1
  16.2 0.1 select_reduce_fusion.3
  16.3 0.1 select_reduce_fusion
  16.5 0.2 and_and_fusion
  16.7 1.5 slice.18.q_ref
  18.1 0.3 copy.67
  18.4 2.1 collective-permute-done
  20.5 0.9 pad_maximum_fusion.1
  21.4 0.1 copy.48
  21.6 1.0 pad_maximum_fusion.2
  22.5 0.5 fusion.31
  23.0 0.3 fusion.5
  23.4 0.5 fusion.13
  23.9 0.2 copy.65
  24.1 178.2 %all-gather.2.cloned.1.call-done.k_ref.v_ref = bf16[8192,1024]{1,0:T(8,128)(2,1)} async-done(((bf16[512,1024]{1,0:T(8,128)(2,1)}), bf16[8192,1024]{1,0:T(8,128)(2,1)}) %all-gather.2.cloned.1.call-update) | async-done | bytes 16777232 | tf_op jit(solution)/shard_map/all_gather | solution.py:165
  202.3 179.4 %shard_map.86 = bf16[512,2048]{1,0:T(8,128)(2,1)} custom-call(s32[1]{0:T(128)} %bitcast.b_ref, bf16[512,2048]{1,0:T(8,128)(2,1)} %slice.18.q_ref, bf16[8192,1024]{1,0:T(8,128)(2,1)} %all-gather.2.cloned.1.call-done.k_ref.v_ref, bf16[8192,1024]{1,0:T(8,128)(2,1)} %all-gather.2.cloned.1.call-done.k_ref.v_ref), custom_call_target="tpu_custom_call" | custom-call | tf_op jit(solution)/shard_map/pallas_call | solution.py:110
  381.7 27.9 %convolution_convert_fusion = bf16[640,8192]{1,0:T(8,128)(2,1)} fusion(bf16[2048,8192]{1,0:T(8,128)(2,1)} %param.10, bf16[128,2048]{1,0:T(8,128)(2,1)S(1)} %copy.65, bf16[512,2048]{1,0:T(8,128)(2,1)} %shard_map.86), kind=kOutput, calls=%fused_computation | convolution fusion | flops 21485322240 | bytes 46661632 | tf_op jit(solution)/shard_map/dot_general | solution.py:178
  409.5 1.0 copy-done.1
  410.6 0.3 stack.10
  410.9 0.3 stack.9
  411.2 0.1 rem.91
  411.3 0.1 div.65
  411.4 0.1 ne.110
  411.5 0.1 broadcast_in_dim.131
  411.6 0.2 broadcast_in_dim.132
  411.8 0.2 copy.68
  412.1 0.5 convert_reduce_fusion
  412.5 0.7 fusion.1
  413.2 2.8 copy.55
  416.0 13.6 %all-to-all-start = ((bf16[2,16,3,8192]{3,0,2,1:T(2,128)(2,1)}), bf16[2,16,3,8192]{3,0,2,1:T(2,128)(2,1)S(1)}, u32[]{:S(2)}, u32[]{:S(2)}) async-start(bf16[2,16,3,8192]{3,0,2,1:T(2,128)(2,1)} %bitcast.15), calls=%async_computation.1 | async-start | bytes 3145728 | tf_op jit(solution)/shard_map/all_to_all | solution.py:211
  429.6 0.3 convolution_convert_fusion.2
  429.8 34.9 %all-to-all-done = bf16[2,16,3,8192]{3,0,2,1:T(2,128)(2,1)S(1)} async-done(((bf16[2,16,3,8192]{3,0,2,1:T(2,128)(2,1)}), bf16[2,16,3,8192]{3,0,2,1:T(2,128)(2,1)S(1)}, u32[]{:S(2)}, u32[]{:S(2)}) %all-to-all-start) | async-done | bytes 1572896 | tf_op jit(solution)/shard_map/all_to_all | solution.py:211
  464.7 1.3 fusion
  466.0 1.7 copy.69
  (34 shorter events, 0.2 us)
Async XLA Ops:
  7.2 1.0 slice-start.1
  7.2 195.1 %all-gather.2.cloned.1.call-start = ((), (), s32[]{:S(2)}) async-start(), calls=%async_computation.2 | async-start | bytes 17825792 | tf_op jit(solution)/shard_map/all_gather | solution.py:165
  7.2 1.2 slice-start.2
  7.2 2.3 slice-start.3
  8.4 7.3 %copy-start.4 = (s32[51]{0:T(128)S(1)}, s32[51]{0:T(128)}, u32[]{:S(2)}) copy-start(s32[51]{0:T(128)} %param.11) | copy-start | bytes 616
  8.4 7.8 %copy-start.5 = (s32[51]{0:T(128)S(1)}, s32[51]{0:T(128)}, u32[]{:S(2)}) copy-start(s32[51]{0:T(128)} %param.12) | copy-start | bytes 616
  8.4 8.3 %copy-start = (bf16[640,2048]{1,0:T(8,128)(2,1)S(1)}, bf16[640,2048]{1,0:T(8,128)(2,1)}, u32[]{:S(2)}) copy-start(bf16[640,2048]{1,0:T(8,128)(2,1)} %param.7) | copy-start | bytes 7864324
  9.5 458.2 %reduce-scatter.2.cloned.1.call-start = ((), (), s32[]{:S(2)}) async-start(), calls=%async_computation.3 | async-start | bytes 15728640 | tf_op jit(solution)/shard_map/reduce_scatter | solution.py:177
  9.7 11.9 %collective-permute-start.1 = (bf16[128,512]{0,1:T(8,128)(2,1)S(1)}, bf16[128,512]{0,1:T(8,128)(2,1)}, u32[]{:S(2)}, u32[]{:S(2)}) collective-permute-start(bf16[128,512]{0,1:T(8,128)(2,1)S(1)} %copy.66), channel_id=1, source_target_pairs={{0,2},{2,4},{4,6},{6,8},{8,10},{10,12},{12,14},{14,16},{16,18},{18... | collective-permute-start | bytes 393224 | tf_op jit(solution)/shard_map/ppermute | solution.py:124
  13.8 6.7 %collective-permute-start = (bf16[128,512]{1,0:T(8,128)(2,1)S(1)}, bf16[128,512]{1,0:T(8,128)(2,1)}, u32[]{:S(2)}, u32[]{:S(2)}) collective-permute-start(bf16[128,512]{1,0:T(8,128)(2,1)S(1)} %slice.21), channel_id=1, source_target_pairs={{0,2},{2,4},{4,6},{6,8},{8,10},{10,12},{12,14},{14,16},{16,18},{18... | collective-permute-start | bytes 393224 | tf_op jit(solution)/shard_map/ppermute | solution.py:125
  16.7 1.5 slice-start
  409.5 1.1 copy-start.1
  409.5 1.4 copy-start.2
  409.5 1.7 copy-start.3
  416.0 48.7 %all-to-all-start = ((bf16[2,16,3,8192]{3,0,2,1:T(2,128)(2,1)}), bf16[2,16,3,8192]{3,0,2,1:T(2,128)(2,1)S(1)}, u32[]{:S(2)}, u32[]{:S(2)}) async-start(bf16[2,16,3,8192]{3,0,2,1:T(2,128)(2,1)} %bitcast.15), calls=%async_computation.1 | async-start | bytes 3145728 | tf_op jit(solution)/shard_map/all_to_all | solution.py:211
Sparse Core Ops, SparseCore 0:
  11.3 190.8 all-gather.1
  409.7 27.6 reduce-scatter.1

commit v2 on v1

--- a/solution.py
+++ b/solution.py
@@ -12,6 +12,7 @@
 SHORT_DEV = 128
 PAGE_ROWS = 16
 BLOCK_TOKENS = 640
+LONG_CHUNKS = 4
 
 
 NEGATIVE_FILL = -1e30
@@ -30,25 +31,41 @@
     return (prompt, offset - begin_at, offset < limit_at)
 
 
-def flash_kernel(b_ref, q_ref, k_ref, v_ref, o_ref, m_sc, l_sc, acc_sc, *, group, tq, nb):
+def flash_kernel(b_ref, q_ref, k_ref, v_ref, *refs, group, tq, tk, chunk_rows, chunk, first, last):
+    if first:
+        m_out, l_out, acc_out = refs[-3:]
+        m_in, l_in, acc_in = m_out, l_out, acc_out
+    elif last:
+        m_in, l_in, acc_in, o_ref = refs
+        m_out, l_out, acc_out = m_in, l_in, acc_in
+    else:
+        m_in, l_in, acc_in, m_out, l_out, acc_out = refs
     i = pl.program_id(1)
-    j = pl.program_id(2)
+    t = pl.program_id(2)
     b = b_ref[0]
+    per_tile = tk // chunk_rows
     scale = HEAD_SIZE ** (-0.5)
 
-    @pl.when(j == 0)
+    @pl.when(t == 0)
     def _init():
-        m_sc[...] = jnp.full(m_sc.shape, NEGATIVE_FILL, jnp.float32)
-        l_sc[...] = jnp.zeros(l_sc.shape, jnp.float32)
-        acc_sc[...] = jnp.zeros(acc_sc.shape, jnp.float32)
+        if first:
+            m_out[...] = jnp.full(m_out.shape, NEGATIVE_FILL, jnp.float32)
+            l_out[...] = jnp.zeros(l_out.shape, jnp.float32)
+            acc_out[...] = jnp.zeros(acc_out.shape, jnp.float32)
+        elif not last:
+            m_out[...] = m_in[...]
+            l_out[...] = l_in[...]
+            acc_out[...] = acc_in[...]
 
     def step(masked):
         k = k_ref[...]
         v = v_ref[...]
         if masked:
-            rows = i * tq + lax.broadcasted_iota(jnp.int32, (tq, k.shape[0]), 0)
-            cols = lax.broadcasted_iota(jnp.int32, (tq, k.shape[0]), 1)
-            allowed = cols <= rows
+            rows = i * tq + lax.broadcasted_iota(jnp.int32, (tq, tk), 0)
+            cols = lax.broadcasted_iota(jnp.int32, (tq, tk), 1)
+            src = t * per_tile + cols // chunk_rows
+            key_pos = chunk * chunk_rows + cols % chunk_rows
+            allowed = (src < b) | ((src == b) & (key_pos <= rows))
         for g in range(group):
             qg = q_ref[:, g * HEAD_SIZE:(g + 1) * HEAD_SIZE]
             s = lax.dot_general(
@@ -56,65 +73,100 @@
             ) * scale
             if masked:
                 s = jnp.where(allowed, s, NEGATIVE_FILL)
-            m_prev = m_sc[g]
+            m_prev = m_out[g]
             m_new = jnp.maximum(m_prev, jnp.max(s, axis=1, keepdims=True))
             p = jnp.exp(s - m_new[:, :1])
             alpha = jnp.exp(m_prev - m_new)
-            l_sc[g] = alpha * l_sc[g] + jnp.sum(p, axis=1, keepdims=True)
-            acc_sc[g] = acc_sc[g] * alpha + lax.dot_general(
+            l_out[g] = alpha * l_out[g] + jnp.sum(p, axis=1, keepdims=True)
+            acc_out[g] = acc_out[g] * alpha + lax.dot_general(
                 p.astype(jnp.bfloat16), v, (((1,), (0,)), ((), ())),
                 preferred_element_type=jnp.float32,
             )
-            m_sc[g] = m_new
-
-    @pl.when(j < b)
+            m_out[g] = m_new
+
+    @pl.when(t * per_tile + per_tile - 1 < b)
     def _full():
         step(False)
 
-    @pl.when(j == b)
+    @pl.when((t * per_tile + per_tile - 1 >= b) & (t * per_tile <= b))
     def _diag():
         step(True)
 
-    @pl.when(j == nb - 1)
-    def _fin():
-        for g in range(group):
-            o_ref[:, g * HEAD_SIZE:(g + 1) * HEAD_SIZE] = (acc_sc[g] / l_sc[g]).astype(o_ref.dtype)
-
-
-def long_attention(my_index, q_long, kv_long):
+    if last:
+        @pl.when(t == pl.num_programs(2) - 1)
+        def _fin():
+            for g in range(group):
+                o_ref[:, g * HEAD_SIZE:(g + 1) * HEAD_SIZE] = (
+                    acc_out[g] / l_out[g]
+                ).astype(o_ref.dtype)
+
+
+def long_attention_chunk(b_arr, q_long, kv_chunk, state, chunk, first, last):
     rows, q_cols = q_long.shape
-    kv_cols = kv_long.shape[1] // 2
+    kv_cols = kv_chunk.shape[1] // 2
     heads_kv = kv_cols // HEAD_SIZE
     group = q_cols // kv_cols
-    nb = kv_long.shape[0] // LONG_DEV
+    chunk_rows = LONG_DEV // LONG_CHUNKS
+    total = kv_chunk.shape[0]
+    tk = min(512, total)
+    per_tile = tk // chunk_rows
     tq = LONG_DEV
-    kernel = functools.partial(flash_kernel, group=group, tq=tq, nb=nb)
+    kernel = functools.partial(
+        flash_kernel, group=group, tq=tq, tk=tk, chunk_rows=chunk_rows, chunk=chunk,
+        first=first, last=last,
+    )
+    state_shape = jax.ShapeDtypeStruct((heads_kv, group, rows, HEAD_SIZE), jnp.float32)
+    state_spec = pl.BlockSpec((None, group, tq, HEAD_SIZE), lambda h, i, t, b: (h, 0, i, 0))
+    kv_spec_k = pl.BlockSpec((tk, HEAD_SIZE), lambda h, i, t, b: (jnp.minimum(t, b[0] // per_tile), h))
+    kv_spec_v = pl.BlockSpec(
+        (tk, HEAD_SIZE), lambda h, i, t, b: (jnp.minimum(t, b[0] // per_tile), heads_kv + h)
+    )
+    q_spec = pl.BlockSpec((tq, group * HEAD_SIZE), lambda h, i, t, b: (i, h))
+    in_specs = [q_spec, kv_spec_k, kv_spec_v]
+    operands = [b_arr, q_long, kv_chunk, kv_chunk]
+    aliases = {}
+    if not first:
+        in_specs += [state_spec] * 3
+        operands += list(state)
+    if last:
+        out_specs = q_spec
+        out_shape = jax.ShapeDtypeStruct((rows, q_cols), jnp.bfloat16)
+    else:
+        out_specs = [state_spec] * 3
+        out_shape = [state_shape] * 3
+        if not first:
+            aliases = {4: 0, 5: 1, 6: 2}
     grid_spec = pltpu.PrefetchScalarGridSpec(
         num_scalar_prefetch=1,
-        grid=(heads_kv, rows // tq, nb),
-        in_specs=[
-            pl.BlockSpec((tq, group * HEAD_SIZE), lambda h, i, j, b: (i, h)),
-            pl.BlockSpec((LONG_DEV, HEAD_SIZE), lambda h, i, j, b: (jnp.minimum(j, b[0]), h)),
-            pl.BlockSpec(
-                (LONG_DEV, HEAD_SIZE), lambda h, i, j, b: (jnp.minimum(j, b[0]), heads_kv + h)
-            ),
-        ],
-        out_specs=pl.BlockSpec((tq, group * HEAD_SIZE), lambda h, i, j, b: (i, h)),
-        scratch_shapes=[
-            pltpu.VMEM((group, tq, HEAD_SIZE), jnp.float32),
-            pltpu.VMEM((group, tq, HEAD_SIZE), jnp.float32),
-            pltpu.VMEM((group, tq, HEAD_SIZE), jnp.float32),
-        ],
-    )
-    b_arr = jnp.reshape(my_index, (1,)).astype(jnp.int32)
+        grid=(heads_kv, rows // tq, total // tk),
+        in_specs=in_specs,
+        out_specs=out_specs,
+    )
     return pl.pallas_call(
         kernel,
         grid_spec=grid_spec,
-        out_shape=jax.ShapeDtypeStruct((rows, q_cols), jnp.bfloat16),
+        out_shape=out_shape,
+        input_output_aliases=aliases,
         compiler_params=pltpu.CompilerParams(
             dimension_semantics=("arbitrary", "arbitrary", "arbitrary")
         ),
-    )(b_arr, q_long, kv_long, kv_long)
+    )(*operands)
+
+
+def long_attention(my_index, q_long, k_long, v_long):
+    b_arr = jnp.reshape(my_index, (1,)).astype(jnp.int32)
+    chunk_rows = LONG_DEV // LONG_CHUNKS
+    state = None
+    for c in range(LONG_CHUNKS):
+        kv = jnp.concatenate(
+            [k_long[c * chunk_rows:(c + 1) * chunk_rows], v_long[c * chunk_rows:(c + 1) * chunk_rows]],
+            axis=1,
+        )
+        kv = lax.all_gather(kv, "req", axis=0, tiled=True)
+        state = long_attention_chunk(
+            b_arr, q_long, kv, state, c, c == 0, c == LONG_CHUNKS - 1
+        )
+    return state
 
 
 def short_attention(my_index, req_count, q_short, k_short, v_short, short_pages, short_fill):
@@ -159,27 +211,6 @@
     req_count = lax.axis_size("req")
     my_index = lax.axis_index("req")
     tok_rows = queries.shape[0]
-    kv_long = jnp.concatenate(
-        [rotated_key_rows[:LONG_DEV], stream_value_rows[:LONG_DEV]], axis=1
-    )
-    kv_long = lax.all_gather(kv_long, "req", axis=0, tiled=True)
-    att_long = long_attention(my_index, queries[:LONG_DEV], kv_long)
-    att_short = short_attention(
-        my_index,
-        req_count,
-        queries[LONG_DEV:],
-        rotated_key_rows[LONG_DEV:],
-        stream_value_rows[LONG_DEV:],
-        short_pages,
-        short_fill,
-    )
-    attended = jnp.concatenate([att_long, att_short])
-    mixed_out = lax.psum_scatter(
-        jnp.dot(attended, out_weight, preferred_element_type=jnp.float32).astype(jnp.bfloat16),
-        "tp",
-        scatter_dimension=0,
-        tiled=True,
-    )
     pages_per = tok_rows // PAGE_ROWS
     capacity = (pages_per + req_count - 1) // req_count
     slot_count = capacity * req_count
@@ -222,6 +253,26 @@
         target.astype(jnp.bfloat16),
         preferred_element_type=jnp.float32,
     ).astype(jnp.bfloat16)
+    incoming, queries = lax.optimization_barrier((incoming, queries))
+    att_long = long_attention(
+        my_index, queries[:LONG_DEV], rotated_key_rows[:LONG_DEV], stream_value_rows[:LONG_DEV]
+    )
+    att_short = short_attention(
+        my_index,
+        req_count,
+        queries[LONG_DEV:],
+        rotated_key_rows[LONG_DEV:],
+        stream_value_rows[LONG_DEV:],
+        short_pages,
+        short_fill,
+    )
+    attended = jnp.concatenate([att_long, att_short])
+    mixed_out = lax.psum_scatter(
+        jnp.dot(attended, out_weight, preferred_element_type=jnp.float32).astype(jnp.bfloat16),
+        "tp",
+        scatter_dimension=0,
+        tiled=True,
+    )
     written_cache = jnp.einsum(
         "sct,xscr->xtr", routing, incoming, preferred_element_type=jnp.float32
     ).astype(jnp.bfloat16)

time: 478 us -> 446 us (0.933)
  waiting for transfers between devices: 215 us -> 166 us
  Pallas kernels: 179 us -> 202 us
  starting transfers between devices: 18.7 us -> 12 us
    all_gather x1 -> x4, waiting for transfers between devices: 178 us -> 107 us  [long_attention(): kv = lax.all_gather(kv, 'req', axis=0, tiled=True)]
    pallas_call x1 -> x4, Pallas kernels: 179 us -> 202 us  [long_attention_chunk(): pl.pallas_call(kernel, grid_spec=grid_spec, out_shape=out_shape, input_ou...]
    reduce_scatter x1, waiting for transfers between devices: 0.01 us -> 15.2 us  [local(): lax.psum_scatter(jnp.dot(attended, out_weight, preferred_element_type=jnp...]
    ppermute x1, waiting for transfers between devices: 2.06 us -> 10.4 us  [short_attention(): v_prev = lax.ppermute(v_short, 'req', perm)]
    all_to_all x1, starting transfers between devices: 13.6 us -> 6.65 us  [local(): lax.all_to_all(outgoing, 'req', split_axis=1, concat_axis=1, tiled=True)]
  transfers between devices with their start and end apart: 5 -> 8, of which waited for: 3 -> 7; matrix products, arithmetic and copies ran while one was open for 3% -> 5% of each run, Pallas kernels for 0% -> 34%
where the time goes in v2:
time: 446 us; the launch traced here: 444 us
  Pallas kernels  202 us (45%)
  waiting for transfers between devices  166 us (37%)
  matrix products  32.5 us (7%)
  between operations  14.1 us (3%)
  local copies, waits for them, and re-layouts  13.1 us (3%)
  starting transfers between devices  12 us (3%)
  other arithmetic  5.52 us (1%)
    pallas_call x4, Pallas kernels, long_attention_chunk(): pl.pallas_call(kernel, grid_spec=grid_spec, out_shape=out_shape, input_ou...  202 us
    all_gather x4, waiting for transfers between devices, long_attention(): kv = lax.all_gather(kv, 'req', axis=0, tiled=True)  107 us
    all_to_all x1, waiting for transfers between devices, local(): lax.all_to_all(outgoing, 'req', split_axis=1, concat_axis=1, tiled=True)  33.1 us
    dot_general x1, matrix products, local(): jnp.dot(attended, out_weight, preferred_element_type=jnp.float32)  27.9 us
    reduce_scatter x1, waiting for transfers between devices, local(): lax.psum_scatter(jnp.dot(attended, out_weight, preferred_element_type=jnp...  15.2 us
    ppermute x1, waiting for transfers between devices, short_attention(): v_prev = lax.ppermute(v_short, 'req', perm)  10.4 us
  transfers between devices with their start and end apart: 8, of which 7 were waited for; matrix products, arithmetic and copies ran while one was open for 5% of the time, Pallas kernels for 34%

profile of v2, /device:TPU:29, one launch (start us, length us, event | category | flops | bytes accessed | tf_op | source)
XLA Modules:
  0.0 444.5 jit_solution(5701887676480813591)
XLA Ops:
  7.2 1.5 fusion.31
  8.7 0.7 pad_maximum_fusion.3
  9.5 0.7 pad_maximum_fusion.2
  10.4 0.7 pad_maximum_fusion.1
  11.2 0.7 pad_maximum_fusion
  12.0 0.3 stack.10
  12.3 0.3 stack.9
  12.8 0.1 ne.107
  12.9 0.1 copy.30
  13.1 0.1 reduce
  13.2 0.1 convert_reduce_fusion.2
  13.4 0.1 select_reduce_fusion.2
  13.6 0.2 broadcast_in_dim.124
  13.7 0.2 copy.50
  14.0 0.5 convert_reduce_fusion
  14.5 0.7 fusion.1
  15.2 2.8 copy.31
  17.9 6.6 %all-to-all-start = ((bf16[2,16,3,8192]{3,0,2,1:T(2,128)(2,1)}), bf16[2,16,3,8192]{3,0,2,1:T(2,128)(2,1)}, u32[]{:S(2)}, u32[]{:S(2)}) async-start(bf16[2,16,3,8192]{3,0,2,1:T(2,128)(2,1)} %bitcast.52), calls=%async_computation | async-start | bytes 3145728 | tf_op jit(solution)/shard_map/all_to_all | solution.py:242
  24.6 0.1 copy.49
  24.8 3.1 collective-permute-start.1
  27.9 2.1 collective-permute-start
  30.0 0.1 convert_reduce_fusion.1
  30.1 0.1 select_reduce_fusion
  30.2 0.2 and_and_fusion
  30.4 10.4 %collective-permute-done = bf16[128,512]{1,0:T(8,128)(2,1)S(1)} collective-permute-done((bf16[128,512]{1,0:T(8,128)(2,1)S(1)}, bf16[128,512]{1,0:T(8,128)(2,1)S(1)}, u32[]{:S(2)}, u32[]{:S(2)}) %collective-permute-start) | collective-permute-done | bytes 131104 | tf_op jit(solution)/shard_map/ppermute | solution.py:177
  40.9 0.1 copy.32
  41.0 0.9 pad_maximum_fusion.5
  41.9 33.1 %all-to-all-done = bf16[2,16,3,8192]{3,0,2,1:T(2,128)(2,1)} async-done(((bf16[2,16,3,8192]{3,0,2,1:T(2,128)(2,1)}), bf16[2,16,3,8192]{3,0,2,1:T(2,128)(2,1)}, u32[]{:S(2)}, u32[]{:S(2)}) %all-to-all-start) | async-done | bytes 1572896 | tf_op jit(solution)/shard_map/all_to_all | solution.py:242
  75.1 1.5 slice.46.q_ref
  76.6 2.6 copy.34
  79.2 1.1 slice.58
  80.3 0.5 fusion.33
  80.8 0.3 fusion.5
  81.1 0.5 fusion.13
  81.6 0.2 copy.48
  81.8 26.2 %all-gather.11.cloned.1.call-done.k_ref.v_ref = bf16[2048,1024]{1,0:T(8,128)(2,1)} async-done(((bf16[128,1024]{1,0:T(8,128)(2,1)}), bf16[2048,1024]{1,0:T(8,128)(2,1)}) %all-gather.11.cloned.1.call-update) | async-done | bytes 4194320 | tf_op jit(solution)/shard_map/all_gather | solution.py:165
  108.0 49.7 %shard_map.86 = (f32[4,4,512,128]{3,2,1,0:T(8,128)}, f32[4,4,512,128]{3,2,1,0:T(8,128)}, f32[4,4,512,128]{3,2,1,0:T(8,128)}) custom-call(s32[1]{0:T(128)} %bitcast.b_ref, bf16[512,2048]{1,0:T(8,128)(2,1)} %slice.46.q_ref, bf16[2048,1024]{1,0:T(8,128)(2,1)} %all-gather.11.cloned.1.call-done.k_ref.v_ref, ...), custom_call_target="tpu_custom_call" | custom-call | tf_op jit(solution)/shard_map/pallas_call | solution.py:145
  157.7 27.8 %all-gather.9.cloned.1.call-done.k_ref.v_ref = bf16[2048,1024]{1,0:T(8,128)(2,1)} async-done(((bf16[128,1024]{1,0:T(8,128)(2,1)}), bf16[2048,1024]{1,0:T(8,128)(2,1)}) %all-gather.9.cloned.1.call-update) | async-done | bytes 4194320 | tf_op jit(solution)/shard_map/all_gather | solution.py:165
  185.5 51.2 %shard_map.87 = (f32[4,4,512,128]{3,2,1,0:T(8,128)}, f32[4,4,512,128]{3,2,1,0:T(8,128)}, f32[4,4,512,128]{3,2,1,0:T(8,128)}) custom-call(s32[1]{0:T(128)} %bitcast.b_ref, bf16[512,2048]{1,0:T(8,128)(2,1)} %slice.46.q_ref, bf16[2048,1024]{1,0:T(8,128)(2,1)} %all-gather.9.cloned.1.call-done.k_ref.v_ref, ...), custom_call_target="tpu_custom_call", output_to_operand_aliasing={{0}: (4, {}), {1}: (5, {}), {2}: (6, {})} | custom-call | tf_op jit(solution)/shard_map/pallas_call | solution.py:145
  236.7 26.3 %all-gather.7.cloned.1.call-done.k_ref.v_ref = bf16[2048,1024]{1,0:T(8,128)(2,1)} async-done(((bf16[128,1024]{1,0:T(8,128)(2,1)}), bf16[2048,1024]{1,0:T(8,128)(2,1)}) %all-gather.7.cloned.1.call-update) | async-done | bytes 4194320 | tf_op jit(solution)/shard_map/all_gather | solution.py:165
  263.0 50.9 %shard_map.88 = (f32[4,4,512,128]{3,2,1,0:T(8,128)}, f32[4,4,512,128]{3,2,1,0:T(8,128)}, f32[4,4,512,128]{3,2,1,0:T(8,128)}) custom-call(s32[1]{0:T(128)} %bitcast.b_ref, bf16[512,2048]{1,0:T(8,128)(2,1)} %slice.46.q_ref, bf16[2048,1024]{1,0:T(8,128)(2,1)} %all-gather.7.cloned.1.call-done.k_ref.v_ref, ...), custom_call_target="tpu_custom_call", output_to_operand_aliasing={{0}: (4, {}), {1}: (5, {}), {2}: (6, {})} | custom-call | tf_op jit(solution)/shard_map/pallas_call | solution.py:145
  313.9 26.4 %all-gather.5.cloned.1.call-done.k_ref.v_ref = bf16[2048,1024]{1,0:T(8,128)(2,1)} async-done(((bf16[128,1024]{1,0:T(8,128)(2,1)}), bf16[2048,1024]{1,0:T(8,128)(2,1)}) %all-gather.5.cloned.1.call-update) | async-done | bytes 4194320 | tf_op jit(solution)/shard_map/all_gather | solution.py:165
  340.4 49.8 %shard_map.89 = bf16[512,2048]{1,0:T(8,128)(2,1)} custom-call(s32[1]{0:T(128)} %bitcast.b_ref, bf16[512,2048]{1,0:T(8,128)(2,1)} %slice.46.q_ref, bf16[2048,1024]{1,0:T(8,128)(2,1)} %all-gather.5.cloned.1.call-done.k_ref.v_ref, bf16[2048,1024]{1,0:T(8,128)(2,1)} %all-gather.5.cloned.1.call-done.k_ref.v_ref, f32[4,4,512,128]{3,2,1,0:T(8,128)} %get-tuple-element.20.refs_0_, ...), custom_call_target="tpu_custom_call" | custom-call | tf_op jit(solution)/shard_map/pallas_call | solution.py:145
  390.2 27.9 %convolution_convert_fusion = bf16[640,8192]{1,0:T(8,128)(2,1)} fusion(bf16[2048,8192]{1,0:T(8,128)(2,1)} %param.10, bf16[128,2048]{1,0:T(8,128)(2,1)S(1)} %copy.48, bf16[512,2048]{1,0:T(8,128)(2,1)} %shard_map.89), kind=kOutput, calls=%fused_computation | convolution fusion | flops 21485322240 | bytes 46661632 | tf_op jit(solution)/shard_map/dot_general | solution.py:271
  418.0 0.3 convolution_convert_fusion.2
  418.3 2.7 fusion
  421.0 1.7 copy.51
  422.7 15.2 %reduce-scatter.2.cloned.1.call-done = bf16[320,8192]{1,0:T(8,128)(2,1)} async-done(((bf16[640,8192]{1,0:T(8,128)(2,1)}), bf16[320,8192]{1,0:T(8,128)(2,1)}) %reduce-scatter.2.cloned.1.call-update) | async-done | bytes 5242896 | tf_op jit(solution)/shard_map/reduce_scatter | solution.py:270
  (42 shorter events, 0.8 us)
Async XLA Ops:
  7.2 100.9 %all-gather.11.cloned.1.call-start = ((), (), s32[]{:S(2)}) async-start(), calls=%async_computation.5 | async-start | bytes 4456448 | tf_op jit(solution)/shard_map/all_gather | solution.py:165
  8.7 3.2 copy-start.1
  9.5 2.8 copy-start.2
  9.5 176.0 %all-gather.9.cloned.1.call-start = ((), (), s32[]{:S(2)}) async-start(), calls=%async_computation.4 | async-start | bytes 4456448 | tf_op jit(solution)/shard_map/all_gather | solution.py:165
  10.3 252.7 %all-gather.7.cloned.1.call-start = ((), (), s32[]{:S(2)}) async-start(), calls=%async_computation.3 | async-start | bytes 4456448 | tf_op jit(solution)/shard_map/all_gather | solution.py:165
  10.3 2.3 copy-start.3
  10.4 2.6 copy-start.4
  10.4 3.0 copy-start.5
  11.1 329.2 %all-gather.5.cloned.1.call-start = ((), (), s32[]{:S(2)}) async-start(), calls=%async_computation.2 | async-start | bytes 4456448 | tf_op jit(solution)/shard_map/all_gather | solution.py:165
  17.9 57.1 %copy-start = (bf16[640,2048]{1,0:T(8,128)(2,1)S(1)}, bf16[640,2048]{1,0:T(8,128)(2,1)}, u32[]{:S(2)}) copy-start(bf16[640,2048]{1,0:T(8,128)(2,1)} %param.7) | copy-start | bytes 7864324
  17.9 57.1 %all-to-all-start = ((bf16[2,16,3,8192]{3,0,2,1:T(2,128)(2,1)}), bf16[2,16,3,8192]{3,0,2,1:T(2,128)(2,1)}, u32[]{:S(2)}, u32[]{:S(2)}) async-start(bf16[2,16,3,8192]{3,0,2,1:T(2,128)(2,1)} %bitcast.52), calls=%async_computation | async-start | bytes 3145728 | tf_op jit(solution)/shard_map/all_to_all | solution.py:242
  24.6 413.3 %reduce-scatter.2.cloned.1.call-start = ((), (), s32[]{:S(2)}) async-start(), calls=%async_computation.6 | async-start | bytes 15728640 | tf_op jit(solution)/shard_map/reduce_scatter | solution.py:270
  24.8 16.2 %collective-permute-start.1 = (bf16[128,512]{0,1:T(8,128)(2,1)S(1)}, bf16[128,512]{0,1:T(8,128)(2,1)}, u32[]{:S(2)}, u32[]{:S(2)}) collective-permute-start(bf16[128,512]{0,1:T(8,128)(2,1)S(1)} %copy.49), channel_id=1, source_target_pairs={{0,2},{2,4},{4,6},{6,8},{8,10},{10,12},{12,14},{14,16},{16,18},{18... | collective-permute-start | bytes 393224 | tf_op jit(solution)/shard_map/ppermute | solution.py:176
  27.9 13.0 %collective-permute-start = (bf16[128,512]{1,0:T(8,128)(2,1)S(1)}, bf16[128,512]{1,0:T(8,128)(2,1)S(1)}, u32[]{:S(2)}, u32[]{:S(2)}) collective-permute-start(bf16[128,512]{1,0:T(8,128)(2,1)S(1)} %get-tuple-element.46), channel_id=1, source_target_pairs={{0,2},{2,4},{4,6},{6,8},{8,10},{10,12},{12,14},{14,16},{16,18},{18... | collective-permute-start | bytes 393224 | tf_op jit(solution)/shard_map/ppermute | solution.py:177
Sparse Core Ops, SparseCore 0:
  10.8 97.2 all-gather.10
  110.8 74.6 all-gather.8
  188.3 74.6 all-gather.6
  265.6 74.6 all-gather.4
  418.2 19.7 reduce-scatter.1

commit v3 on v2

--- a/solution.py
+++ b/solution.py
@@ -12,7 +12,7 @@
 SHORT_DEV = 128
 PAGE_ROWS = 16
 BLOCK_TOKENS = 640
-LONG_CHUNKS = 4
+LONG_CHUNKS = 2
 
 
 NEGATIVE_FILL = -1e30

time: 446 us -> 414 us (0.928)
  waiting for transfers between devices: 166 us -> 144 us
  Pallas kernels: 202 us -> 192 us
    all_gather x4 -> x2, waiting for transfers between devices: 107 us -> 72.1 us  [long_attention(): kv = lax.all_gather(kv, 'req', axis=0, tiled=True)]
    all_to_all x1, waiting for transfers between devices: 33.1 us -> 50.1 us  [local(): lax.all_to_all(outgoing, 'req', split_axis=1, concat_axis=1, tiled=True)]
    pallas_call x4 -> x2, Pallas kernels: 202 us -> 192 us  [long_attention_chunk(): pl.pallas_call(kernel, grid_spec=grid_spec, out_shape=out_shape, input_ou...]
  transfers between devices with their start and end apart: 8 -> 6, of which waited for: 7 -> 5; matrix products, arithmetic and copies ran while one was open for 5% -> 5% of each run, Pallas kernels for 34% -> 23%
where the time goes in v3:
time: 414 us; the launch traced here: 412 us
  Pallas kernels  192 us (46%)
  waiting for transfers between devices  144 us (35%)
  matrix products  32.5 us (8%)
  local copies, waits for them, and re-layouts  14.7 us (4%)
  between operations  14.1 us (3%)
  starting transfers between devices  12 us (3%)
    pallas_call x2, Pallas kernels, long_attention_chunk(): pl.pallas_call(kernel, grid_spec=grid_spec, out_shape=out_shape, input_ou...  192 us
    all_gather x2, waiting for transfers between devices, long_attention(): kv = lax.all_gather(kv, 'req', axis=0, tiled=True)  72.1 us
    all_to_all x1, waiting for transfers between devices, local(): lax.all_to_all(outgoing, 'req', split_axis=1, concat_axis=1, tiled=True)  50.1 us
    dot_general x1, matrix products, local(): jnp.dot(attended, out_weight, preferred_element_type=jnp.float32)  27.9 us
    reduce_scatter x1, waiting for transfers between devices, local(): lax.psum_scatter(jnp.dot(attended, out_weight, preferred_element_type=jnp...  15 us
  transfers between devices with their start and end apart: 6, of which 5 were waited for; matrix products, arithmetic and copies ran while one was open for 5% of the time, Pallas kernels for 23%

profile of v3, /device:TPU:29, one launch (start us, length us, event | category | flops | bytes accessed | tf_op | source)
XLA Modules:
  0.0 412.1 jit_solution(2642528106027742230)
XLA Ops:
  7.2 1.1 fusion.31
  8.3 1.1 fusion.32
  9.4 0.9 pad_maximum_fusion.1
  10.3 0.0 all-gather.3.cloned.1.call-start
  10.4 0.9 pad_maximum_fusion
  11.3 0.3 stack.10
  11.6 0.3 stack.9
  12.0 0.1 rem.82
  12.1 0.1 div.59
  12.2 0.1 ne.107
  12.3 0.1 copy.24
  12.4 0.1 reduce-window.8
  12.5 0.1 reduce
  12.6 0.1 convert_reduce_fusion.2
  12.7 0.1 select_reduce_fusion.2
  12.8 0.1 broadcast_in_dim.123
  12.9 0.2 broadcast_in_dim.124
  13.1 0.2 copy.44
  13.3 0.5 convert_reduce_fusion
  13.8 0.7 fusion.1
  14.5 2.8 copy.25
  17.3 6.6 %all-to-all-start = ((bf16[2,16,3,8192]{3,0,2,1:T(2,128)(2,1)}), bf16[2,16,3,8192]{3,0,2,1:T(2,128)(2,1)}, u32[]{:S(2)}, u32[]{:S(2)}) async-start(bf16[2,16,3,8192]{3,0,2,1:T(2,128)(2,1)} %bitcast.52), calls=%async_computation | async-start | bytes 3145728 | tf_op jit(solution)/shard_map/all_to_all | solution.py:242
  24.0 0.1 copy.43
  24.1 3.1 collective-permute-start.1
  27.2 0.9 slice.35
  28.1 2.1 collective-permute-start
  30.3 0.1 convert_reduce_fusion.1
  30.4 0.1 select_reduce_fusion
  30.5 0.2 and_and_fusion
  30.7 6.4 %collective-permute-done = bf16[128,512]{1,0:T(8,128)(2,1)S(1)} collective-permute-done((bf16[128,512]{1,0:T(8,128)(2,1)S(1)}, bf16[128,512]{1,0:T(8,128)(2,1)S(1)}, u32[]{:S(2)}, u32[]{:S(2)}) %collective-permute-start) | collective-permute-done | bytes 131104 | tf_op jit(solution)/shard_map/ppermute | solution.py:177
  37.1 0.1 copy.26
  37.3 50.1 %all-to-all-done = bf16[2,16,3,8192]{3,0,2,1:T(2,128)(2,1)} async-done(((bf16[2,16,3,8192]{3,0,2,1:T(2,128)(2,1)}), bf16[2,16,3,8192]{3,0,2,1:T(2,128)(2,1)}, u32[]{:S(2)}, u32[]{:S(2)}) %all-to-all-start) | async-done | bytes 1572896 | tf_op jit(solution)/shard_map/all_to_all | solution.py:242
  87.4 1.5 slice.30.q_ref
  88.9 2.6 copy.28
  91.5 1.1 slice.38
  92.6 0.5 fusion.33
  93.1 0.3 fusion.5
  93.4 0.5 fusion.13
  93.9 0.2 copy.42
  94.1 54.1 %all-gather.5.cloned.1.call-done.k_ref.v_ref = bf16[4096,1024]{1,0:T(8,128)(2,1)} async-done(((bf16[256,1024]{1,0:T(8,128)(2,1)}), bf16[4096,1024]{1,0:T(8,128)(2,1)}) %all-gather.5.cloned.1.call-update) | async-done | bytes 8388624 | tf_op jit(solution)/shard_map/all_gather | solution.py:165
  148.3 95.8 %shard_map.86 = (f32[4,4,512,128]{3,2,1,0:T(8,128)}, f32[4,4,512,128]{3,2,1,0:T(8,128)}, f32[4,4,512,128]{3,2,1,0:T(8,128)}) custom-call(s32[1]{0:T(128)} %bitcast.b_ref, bf16[512,2048]{1,0:T(8,128)(2,1)} %slice.30.q_ref, bf16[4096,1024]{1,0:T(8,128)(2,1)} %all-gather.5.cloned.1.call-done.k_ref.v_ref, bf16[4096,1024]{1,0:T(8,128)(2,1)} %all-gather.5.cloned.1.call-done.k_ref.v_ref), custom_call_target="tpu_custom_call" | custom-call | tf_op jit(solution)/shard_map/pallas_call | solution.py:145
  244.1 18.0 %all-gather.3.cloned.1.call-done.k_ref.v_ref = bf16[4096,1024]{1,0:T(8,128)(2,1)} async-done(((bf16[256,1024]{1,0:T(8,128)(2,1)}), bf16[4096,1024]{1,0:T(8,128)(2,1)}) %all-gather.3.cloned.1.call-update) | async-done | bytes 8388624 | tf_op jit(solution)/shard_map/all_gather | solution.py:165
  262.1 95.9 %shard_map.87 = bf16[512,2048]{1,0:T(8,128)(2,1)} custom-call(s32[1]{0:T(128)} %bitcast.b_ref, bf16[512,2048]{1,0:T(8,128)(2,1)} %slice.30.q_ref, bf16[4096,1024]{1,0:T(8,128)(2,1)} %all-gather.3.cloned.1.call-done.k_ref.v_ref, bf16[4096,1024]{1,0:T(8,128)(2,1)} %all-gather.3.cloned.1.call-done.k_ref.v_ref, f32[4,4,512,128]{3,2,1,0:T(8,128)} %get-tuple-element.8.refs_0_, ...), custom_call_target="tpu_custom_call" | custom-call | tf_op jit(solution)/shard_map/pallas_call | solution.py:145
  358.0 27.9 %convolution_convert_fusion = bf16[640,8192]{1,0:T(8,128)(2,1)} fusion(bf16[2048,8192]{1,0:T(8,128)(2,1)} %param.10, bf16[128,2048]{1,0:T(8,128)(2,1)S(1)} %copy.42, bf16[512,2048]{1,0:T(8,128)(2,1)} %shard_map.87), kind=kOutput, calls=%fused_computation | convolution fusion | flops 21485322240 | bytes 46661632 | tf_op jit(solution)/shard_map/dot_general | solution.py:271
  385.9 0.3 convolution_convert_fusion.2
  386.2 2.7 fusion
  388.9 1.7 copy.45
  390.6 15.0 %reduce-scatter.2.cloned.1.call-done = bf16[320,8192]{1,0:T(8,128)(2,1)} async-done(((bf16[640,8192]{1,0:T(8,128)(2,1)}), bf16[320,8192]{1,0:T(8,128)(2,1)}) %reduce-scatter.2.cloned.1.call-update) | async-done | bytes 5242896 | tf_op jit(solution)/shard_map/reduce_scatter | solution.py:270
  (36 shorter events, 0.3 us)
Async XLA Ops:
  7.2 141.1 %all-gather.5.cloned.1.call-start = ((), (), s32[]{:S(2)}) async-start(), calls=%async_computation.3 | async-start | bytes 8912896 | tf_op jit(solution)/shard_map/all_gather | solution.py:165
  8.3 3.0 copy-start.2
  9.4 2.2 copy-start.1
  10.3 251.8 %all-gather.3.cloned.1.call-start = ((), (), s32[]{:S(2)}) async-start(), calls=%async_computation.2 | async-start | bytes 8912896 | tf_op jit(solution)/shard_map/all_gather | solution.py:165
  10.4 1.6 copy-start.3
  10.4 1.9 copy-start.4
  10.4 2.3 copy-start.5
  17.3 6.7 %slice-start = ((bf16[640,512]{1,0:T(8,128)(2,1)}), bf16[128,512]{1,0:T(8,128)(2,1)S(1)}, s32[]{:S(2)}) async-start(bf16[640,512]{1,0:T(8,128)(2,1)} %param.8), calls=%async_computation.5 | async-start | bytes 262144 | tf_op jit(solution)/shard_map/slice | solution.py:264
  17.3 70.1 %copy-start = (bf16[640,2048]{1,0:T(8,128)(2,1)S(1)}, bf16[640,2048]{1,0:T(8,128)(2,1)}, u32[]{:S(2)}) copy-start(bf16[640,2048]{1,0:T(8,128)(2,1)} %param.7) | copy-start | bytes 7864324
  17.3 70.1 %all-to-all-start = ((bf16[2,16,3,8192]{3,0,2,1:T(2,128)(2,1)}), bf16[2,16,3,8192]{3,0,2,1:T(2,128)(2,1)}, u32[]{:S(2)}, u32[]{:S(2)}) async-start(bf16[2,16,3,8192]{3,0,2,1:T(2,128)(2,1)} %bitcast.52), calls=%async_computation | async-start | bytes 3145728 | tf_op jit(solution)/shard_map/all_to_all | solution.py:242
  24.0 381.7 %reduce-scatter.2.cloned.1.call-start = ((), (), s32[]{:S(2)}) async-start(), calls=%async_computation.4 | async-start | bytes 15728640 | tf_op jit(solution)/shard_map/reduce_scatter | solution.py:270
  24.1 13.1 %collective-permute-start.1 = (bf16[128,512]{0,1:T(8,128)(2,1)S(1)}, bf16[128,512]{0,1:T(8,128)(2,1)S(1)}, u32[]{:S(2)}, u32[]{:S(2)}) collective-permute-start(bf16[128,512]{0,1:T(8,128)(2,1)S(1)} %copy.43), channel_id=1, source_target_pairs={{0,2},{2,4},{4,6},{6,8},{8,10},{10,12},{12,14},{14,16},{16,18},{18... | collective-permute-start | bytes 393224 | tf_op jit(solution)/shard_map/ppermute | solution.py:176
  28.1 8.9 %collective-permute-start = (bf16[128,512]{1,0:T(8,128)(2,1)S(1)}, bf16[128,512]{1,0:T(8,128)(2,1)S(1)}, u32[]{:S(2)}, u32[]{:S(2)}) collective-permute-start(bf16[128,512]{1,0:T(8,128)(2,1)S(1)} %slice.35), channel_id=1, source_target_pairs={{0,2},{2,4},{4,6},{6,8},{8,10},{10,12},{12,14},{14,16},{16,18},{18... | collective-permute-start | bytes 393224 | tf_op jit(solution)/shard_map/ppermute | solution.py:177
Sparse Core Ops, SparseCore 0:
  10.8 137.4 all-gather.4
  151.1 111.0 all-gather.2
  386.0 19.5 reduce-scatter.1

commit v4 on v3

--- a/solution.py
+++ b/solution.py
@@ -12,7 +12,7 @@
 SHORT_DEV = 128
 PAGE_ROWS = 16
 BLOCK_TOKENS = 640
-LONG_CHUNKS = 2
+LONG_CHUNK_ROWS = (256, 128, 128)
 
 
 NEGATIVE_FILL = -1e30
@@ -31,7 +31,7 @@
     return (prompt, offset - begin_at, offset < limit_at)
 
 
-def flash_kernel(b_ref, q_ref, k_ref, v_ref, *refs, group, tq, tk, chunk_rows, chunk, first, last):
+def flash_kernel(b_ref, q_ref, k_ref, v_ref, *refs, group, tq, tk, chunk_rows, chunk_start, first, last):
     if first:
         m_out, l_out, acc_out = refs[-3:]
         m_in, l_in, acc_in = m_out, l_out, acc_out
@@ -64,7 +64,7 @@
             rows = i * tq + lax.broadcasted_iota(jnp.int32, (tq, tk), 0)
             cols = lax.broadcasted_iota(jnp.int32, (tq, tk), 1)
             src = t * per_tile + cols // chunk_rows
-            key_pos = chunk * chunk_rows + cols % chunk_rows
+            key_pos = chunk_start + cols % chunk_rows
             allowed = (src < b) | ((src == b) & (key_pos <= rows))
         for g in range(group):
             qg = q_ref[:, g * HEAD_SIZE:(g + 1) * HEAD_SIZE]
@@ -101,18 +101,17 @@
                 ).astype(o_ref.dtype)
 
 
-def long_attention_chunk(b_arr, q_long, kv_chunk, state, chunk, first, last):
+def long_attention_chunk(b_arr, q_long, kv_chunk, state, chunk_rows, chunk_start, first, last):
     rows, q_cols = q_long.shape
     kv_cols = kv_chunk.shape[1] // 2
     heads_kv = kv_cols // HEAD_SIZE
     group = q_cols // kv_cols
-    chunk_rows = LONG_DEV // LONG_CHUNKS
     total = kv_chunk.shape[0]
     tk = min(512, total)
     per_tile = tk // chunk_rows
     tq = LONG_DEV
     kernel = functools.partial(
-        flash_kernel, group=group, tq=tq, tk=tk, chunk_rows=chunk_rows, chunk=chunk,
+        flash_kernel, group=group, tq=tq, tk=tk, chunk_rows=chunk_rows, chunk_start=chunk_start,
         first=first, last=last,
     )
     state_shape = jax.ShapeDtypeStruct((heads_kv, group, rows, HEAD_SIZE), jnp.float32)
@@ -155,17 +154,17 @@
 
 def long_attention(my_index, q_long, k_long, v_long):
     b_arr = jnp.reshape(my_index, (1,)).astype(jnp.int32)
-    chunk_rows = LONG_DEV // LONG_CHUNKS
     state = None
-    for c in range(LONG_CHUNKS):
+    start = 0
+    for c, rows in enumerate(LONG_CHUNK_ROWS):
         kv = jnp.concatenate(
-            [k_long[c * chunk_rows:(c + 1) * chunk_rows], v_long[c * chunk_rows:(c + 1) * chunk_rows]],
-            axis=1,
+            [k_long[start:start + rows], v_long[start:start + rows]], axis=1
         )
         kv = lax.all_gather(kv, "req", axis=0, tiled=True)
         state = long_attention_chunk(
-            b_arr, q_long, kv, state, c, c == 0, c == LONG_CHUNKS - 1
+            b_arr, q_long, kv, state, rows, start, c == 0, c == len(LONG_CHUNK_ROWS) - 1
         )
+        start += rows
     return state
 
 
@@ -267,12 +266,19 @@
         short_fill,
     )
     attended = jnp.concatenate([att_long, att_short])
-    mixed_out = lax.psum_scatter(
-        jnp.dot(attended, out_weight, preferred_element_type=jnp.float32).astype(jnp.bfloat16),
-        "tp",
-        scatter_dimension=0,
-        tiled=True,
-    )
+    half = out_weight.shape[1] // 2
+    mixed_parts = [
+        lax.psum_scatter(
+            jnp.dot(
+                attended, out_weight[:, p * half:(p + 1) * half], preferred_element_type=jnp.float32
+            ).astype(jnp.bfloat16),
+            "tp",
+            scatter_dimension=0,
+            tiled=True,
+        )
+        for p in range(2)
+    ]
+    mixed_out = jnp.concatenate(mixed_parts, axis=1)
     written_cache = jnp.einsum(
         "sct,xscr->xtr", routing, incoming, preferred_element_type=jnp.float32
     ).astype(jnp.bfloat16)

time: 414 us -> 415 us (level)
  waiting for transfers between devices: 144 us -> 128 us
  other arithmetic: 3.42 us -> 10.4 us
  Pallas kernels: 192 us -> 197 us
  matrix products: 32.5 us -> 37.4 us
    all_gather x2 -> x3, waiting for transfers between devices: 72.1 us -> 62.2 us  [long_attention(): kv = lax.all_gather(kv, 'req', axis=0, tiled=True)]
    concatenate x2 -> x4, other arithmetic: 1.74 us -> 7.82 us  [the longest x1 5.48 us: local(): mixed_out = jnp.concatenate(mixed_parts, axis=1)]
    reduce_scatter x1 -> x2, waiting for transfers between devices: 15 us -> 9.34 us  [local(): lax.psum_scatter(jnp.dot(attended, out_weight[:, p * half:(p + 1) * half]...]
    pallas_call x2 -> x3, Pallas kernels: 192 us -> 197 us  [long_attention_chunk(): pl.pallas_call(kernel, grid_spec=grid_spec, out_shape=out_shape, input_ou...]
    dot_general x1 -> x2, matrix products: 27.9 us -> 32.8 us  [local(): jnp.dot(attended, out_weight[:, p * half:(p + 1) * half], preferred_eleme...]
  transfers between devices with their start and end apart: 6 -> 8, of which waited for: 5 -> 5; matrix products, arithmetic and copies ran while one was open for 5% -> 9% of each run, Pallas kernels for 23% -> 36%
where the time goes in v4:
time: 415 us; the launch traced here: 413 us
  Pallas kernels  197 us (47%)
  waiting for transfers between devices  128 us (31%)
  matrix products  37.4 us (9%)
  local copies, waits for them, and re-layouts  15.2 us (4%)
  between operations  14.1 us (3%)
  starting transfers between devices  12 us (3%)
  other arithmetic  10.4 us (3%)
    pallas_call x3, Pallas kernels, long_attention_chunk(): pl.pallas_call(kernel, grid_spec=grid_spec, out_shape=out_shape, input_ou...  197 us
    all_gather x3, waiting for transfers between devices, long_attention(): kv = lax.all_gather(kv, 'req', axis=0, tiled=True)  62.2 us
    all_to_all x1, waiting for transfers between devices, local(): lax.all_to_all(outgoing, 'req', split_axis=1, concat_axis=1, tiled=True)  48.7 us
    dot_general x2, matrix products, local(): jnp.dot(attended, out_weight[:, p * half:(p + 1) * half], preferred_eleme...  32.8 us
    reduce_scatter x2, waiting for transfers between devices, local(): lax.psum_scatter(jnp.dot(attended, out_weight[:, p * half:(p + 1) * half]...  9.34 us
  transfers between devices with their start and end apart: 8, of which 5 were waited for; matrix products, arithmetic and copies ran while one was open for 9% of the time, Pallas kernels for 36%

profile of v4, /device:TPU:29, one launch (start us, length us, event | category | flops | bytes accessed | tf_op | source)
XLA Modules:
  0.0 413.5 jit_solution(1600930265581962314)
XLA Ops:
  7.2 1.1 slice.49
  8.3 1.0 slice.50
  9.3 0.9 pad_maximum_fusion.4
  10.3 0.7 pad_maximum_fusion.6
  11.2 0.7 pad_maximum_fusion.5
  11.9 0.3 stack.10
  12.2 0.3 stack.9
  12.8 0.1 ne.107
  12.9 0.1 copy.27
  13.1 0.1 reduce
  13.2 0.1 convert_reduce_fusion.2
  13.3 0.1 select_reduce_fusion.2
  13.5 0.2 broadcast_in_dim.124
  13.7 0.2 copy.47
  13.9 0.5 convert_reduce_fusion
  14.4 0.7 fusion.5
  15.1 2.8 copy.28
  17.9 6.6 %all-to-all-start = ((bf16[2,16,3,8192]{3,0,2,1:T(2,128)(2,1)}), bf16[2,16,3,8192]{3,0,2,1:T(2,128)(2,1)}, u32[]{:S(2)}, u32[]{:S(2)}) async-start(bf16[2,16,3,8192]{3,0,2,1:T(2,128)(2,1)} %bitcast.51), calls=%async_computation | async-start | bytes 3145728 | tf_op jit(solution)/shard_map/all_to_all | solution.py:241
  24.6 0.1 copy.46
  24.7 3.1 collective-permute-start.1
  27.8 2.1 collective-permute-start
  29.9 0.1 convert_reduce_fusion.1
  30.0 0.1 select_reduce_fusion
  30.2 0.2 and_and_fusion
  30.3 7.2 %collective-permute-done = bf16[128,512]{1,0:T(8,128)(2,1)S(1)} collective-permute-done((bf16[128,512]{1,0:T(8,128)(2,1)S(1)}, bf16[128,512]{1,0:T(8,128)(2,1)S(1)}, u32[]{:S(2)}, u32[]{:S(2)}) %collective-permute-start) | collective-permute-done | bytes 131104 | tf_op jit(solution)/shard_map/ppermute | solution.py:176
  37.6 0.1 copy.29
  37.7 0.9 pad_maximum_fusion.8
  38.7 48.7 %all-to-all-done = bf16[2,16,3,8192]{3,0,2,1:T(2,128)(2,1)} async-done(((bf16[2,16,3,8192]{3,0,2,1:T(2,128)(2,1)}), bf16[2,16,3,8192]{3,0,2,1:T(2,128)(2,1)}, u32[]{:S(2)}, u32[]{:S(2)}) %all-to-all-start) | async-done | bytes 1572896 | tf_op jit(solution)/shard_map/all_to_all | solution.py:241
  87.4 1.5 slice.44.q_ref
  88.9 2.6 copy.31
  91.5 1.1 slice.56
  92.6 0.5 fusion.41
  93.1 0.3 fusion.12
  93.4 0.5 fusion.20
  93.9 0.2 copy.45
  94.1 54.2 %all-gather.8.cloned.1.call-done.k_ref.v_ref = bf16[4096,1024]{1,0:T(8,128)(2,1)} async-done(((bf16[256,1024]{1,0:T(8,128)(2,1)}), bf16[4096,1024]{1,0:T(8,128)(2,1)}) %all-gather.8.cloned.1.call-update) | async-done | bytes 8388624 | tf_op jit(solution)/shard_map/all_gather | solution.py:163
  148.3 95.8 %shard_map.86 = (f32[4,4,512,128]{3,2,1,0:T(8,128)}, f32[4,4,512,128]{3,2,1,0:T(8,128)}, f32[4,4,512,128]{3,2,1,0:T(8,128)}) custom-call(s32[1]{0:T(128)} %bitcast.b_ref, bf16[512,2048]{1,0:T(8,128)(2,1)} %slice.44.q_ref, bf16[4096,1024]{1,0:T(8,128)(2,1)} %all-gather.8.cloned.1.call-done.k_ref.v_ref, bf16[4096,1024]{1,0:T(8,128)(2,1)} %all-gather.8.cloned.1.call-done.k_ref.v_ref), custom_call_target="tpu_custom_call" | custom-call | tf_op jit(solution)/shard_map/pallas_call | solution.py:144
  244.1 51.1 %shard_map.87 = (f32[4,4,512,128]{3,2,1,0:T(8,128)}, f32[4,4,512,128]{3,2,1,0:T(8,128)}, f32[4,4,512,128]{3,2,1,0:T(8,128)}) custom-call(s32[1]{0:T(128)} %bitcast.b_ref, bf16[512,2048]{1,0:T(8,128)(2,1)} %slice.44.q_ref, bf16[2048,1024]{1,0:T(8,128)(2,1)} %all-gather.6.cloned.1.call-done.k_ref.v_ref, ...), custom_call_target="tpu_custom_call", output_to_operand_aliasing={{0}: (4, {}), {1}: (5, {}), {2}: (6, {})} | custom-call | tf_op jit(solution)/shard_map/pallas_call | solution.py:144
  295.3 8.0 %all-gather.4.cloned.1.call-done.k_ref.v_ref = bf16[2048,1024]{1,0:T(8,128)(2,1)} async-done(((bf16[128,1024]{1,0:T(8,128)(2,1)}), bf16[2048,1024]{1,0:T(8,128)(2,1)}) %all-gather.4.cloned.1.call-update) | async-done | bytes 4194320 | tf_op jit(solution)/shard_map/all_gather | solution.py:163
  303.2 49.8 %shard_map.88 = bf16[512,2048]{1,0:T(8,128)(2,1)} custom-call(s32[1]{0:T(128)} %bitcast.b_ref, bf16[512,2048]{1,0:T(8,128)(2,1)} %slice.44.q_ref, bf16[2048,1024]{1,0:T(8,128)(2,1)} %all-gather.4.cloned.1.call-done.k_ref.v_ref, bf16[2048,1024]{1,0:T(8,128)(2,1)} %all-gather.4.cloned.1.call-done.k_ref.v_ref, f32[4,4,512,128]{3,2,1,0:T(8,128)} %get-tuple-element.14.refs_0_, ...), custom_call_target="tpu_custom_call" | custom-call | tf_op jit(solution)/shard_map/pallas_call | solution.py:144
  353.1 16.7 %fusion.6 = bf16[640,4096]{1,0:T(8,128)(2,1)} fusion(bf16[2048,8192]{1,0:T(8,128)(2,1)} %param.10, bf16[128,2048]{1,0:T(8,128)(2,1)S(1)} %copy.45, bf16[512,2048]{1,0:T(8,128)(2,1)} %shard_map.88), kind=kOutput, calls=%fused_computation.8 | convolution fusion | flops 10745282560 | bytes 24641536 | tf_op jit(solution)/shard_map/dot_general | solution.py:272
  369.8 1.5 copy-done.3
  371.4 16.0 %fusion.9 = bf16[640,4096]{1,0:T(8,128)(2,1)} fusion(bf16[2048,8192]{1,0:T(8,128)(2,1)} %param.10, bf16[128,2048]{1,0:T(8,128)(2,1)S(1)} %copy.45, bf16[512,2048]{1,0:T(8,128)(2,1)S(1)} %copy-done.3), kind=kOutput, calls=%fused_computation.9 | convolution fusion | flops 10745282560 | bytes 24641536 | tf_op jit(solution)/shard_map/dot_general | solution.py:272
  387.4 0.3 convolution_convert_fusion.1
  387.7 2.7 fusion.4
  390.4 1.7 copy.48
  392.1 9.3 %reduce-scatter.5.cloned.1.call-done = bf16[320,4096]{1,0:T(8,128)(2,1)} async-done(((bf16[640,4096]{1,0:T(8,128)(2,1)}), bf16[320,4096]{1,0:T(8,128)(2,1)}) %reduce-scatter.5.cloned.1.call-update) | async-done | bytes 2621456 | tf_op jit(solution)/shard_map/reduce_scatter | solution.py:271
  401.5 5.5 %pad_maximum_fusion = bf16[320,8192]{1,0:T(8,128)(2,1)} fusion(bf16[320,4096]{1,0:T(8,128)(2,1)} %reduce-scatter.5.cloned.1.call-done, bf16[320,4096]{1,0:T(8,128)(2,1)} %reduce-scatter.3.cloned.1.call-done), kind=kLoop, calls=%fused_computation.10 | loop fusion | flops 10485760 | bytes 10485760 | tf_op jit(solution)/shard_map/concatenate | solution.py:281
  (46 shorter events, 0.9 us)
Async XLA Ops:
  7.2 3.1 copy-start.2
  7.2 3.1 copy-start.1
  7.2 141.1 %all-gather.8.cloned.1.call-start = ((), (), s32[]{:S(2)}) async-start(), calls=%async_computation.5 | async-start | bytes 8912896 | tf_op jit(solution)/shard_map/all_gather | solution.py:163
  10.2 2.4 copy-start.4
  10.2 2.7 copy-start.5
  10.2 3.1 copy-start.6
  10.2 233.9 %all-gather.6.cloned.1.call-start = ((), (), s32[]{:S(2)}) async-start(), calls=%async_computation.4 | async-start | bytes 4456448 | tf_op jit(solution)/shard_map/all_gather | solution.py:163
  11.1 292.1 %all-gather.4.cloned.1.call-start = ((), (), s32[]{:S(2)}) async-start(), calls=%async_computation.3 | async-start | bytes 4456448 | tf_op jit(solution)/shard_map/all_gather | solution.py:163
  17.9 69.5 %copy-start = (bf16[640,2048]{1,0:T(8,128)(2,1)S(1)}, bf16[640,2048]{1,0:T(8,128)(2,1)}, u32[]{:S(2)}) copy-start(bf16[640,2048]{1,0:T(8,128)(2,1)} %param.7) | copy-start | bytes 7864324
  17.9 69.5 %all-to-all-start = ((bf16[2,16,3,8192]{3,0,2,1:T(2,128)(2,1)}), bf16[2,16,3,8192]{3,0,2,1:T(2,128)(2,1)}, u32[]{:S(2)}, u32[]{:S(2)}) async-start(bf16[2,16,3,8192]{3,0,2,1:T(2,128)(2,1)} %bitcast.51), calls=%async_computation | async-start | bytes 3145728 | tf_op jit(solution)/shard_map/all_to_all | solution.py:241
  24.5 367.6 %reduce-scatter.3.cloned.1.call-start = ((), (), s32[]{:S(2)}) async-start(), calls=%async_computation.6 | async-start | bytes 7864320 | tf_op jit(solution)/shard_map/reduce_scatter | solution.py:271
  24.7 13.0 %collective-permute-start.1 = (bf16[128,512]{0,1:T(8,128)(2,1)S(1)}, bf16[128,512]{0,1:T(8,128)(2,1)}, u32[]{:S(2)}, u32[]{:S(2)}) collective-permute-start(bf16[128,512]{0,1:T(8,128)(2,1)S(1)} %copy.46), channel_id=1, source_target_pairs={{0,2},{2,4},{4,6},{6,8},{8,10},{10,12},{12,14},{14,16},{16,18},{18... | collective-permute-start | bytes 393224 | tf_op jit(solution)/shard_map/ppermute | solution.py:175
  27.8 9.8 %collective-permute-start = (bf16[128,512]{1,0:T(8,128)(2,1)S(1)}, bf16[128,512]{1,0:T(8,128)(2,1)S(1)}, u32[]{:S(2)}, u32[]{:S(2)}) collective-permute-start(bf16[128,512]{1,0:T(8,128)(2,1)S(1)} %get-tuple-element.36), channel_id=1, source_target_pairs={{0,2},{2,4},{4,6},{6,8},{8,10},{10,12},{12,14},{14,16},{16,18},{18... | collective-permute-start | bytes 393224 | tf_op jit(solution)/shard_map/ppermute | solution.py:176
  369.8 1.6 copy-start.3
  369.8 31.7 %reduce-scatter.5.cloned.1.call-start = ((), (), s32[]{:S(2)}) async-start(), calls=%async_computation.7 | async-start | bytes 7864320 | tf_op jit(solution)/shard_map/reduce_scatter | solution.py:271
Sparse Core Ops, SparseCore 0:
  10.8 137.4 all-gather.7
  151.1 74.5 all-gather.5
  228.5 74.7 all-gather.3
  369.9 13.8 reduce-scatter.2
  387.5 13.8 reduce-scatter.4

commit v5 on v4

--- a/solution.py
+++ b/solution.py
@@ -12,7 +12,7 @@
 SHORT_DEV = 128
 PAGE_ROWS = 16
 BLOCK_TOKENS = 640
-LONG_CHUNK_ROWS = (256, 128, 128)
+LONG_CHUNK_ROWS = (128, 256, 128)
 
 
 NEGATIVE_FILL = -1e30
@@ -266,19 +266,12 @@
         short_fill,
     )
     attended = jnp.concatenate([att_long, att_short])
-    half = out_weight.shape[1] // 2
-    mixed_parts = [
-        lax.psum_scatter(
-            jnp.dot(
-                attended, out_weight[:, p * half:(p + 1) * half], preferred_element_type=jnp.float32
-            ).astype(jnp.bfloat16),
-            "tp",
-            scatter_dimension=0,
-            tiled=True,
-        )
-        for p in range(2)
-    ]
-    mixed_out = jnp.concatenate(mixed_parts, axis=1)
+    mixed_out = lax.psum_scatter(
+        jnp.dot(attended, out_weight, preferred_element_type=jnp.float32).astype(jnp.bfloat16),
+        "tp",
+        scatter_dimension=0,
+        tiled=True,
+    )
     written_cache = jnp.einsum(
         "sct,xscr->xtr", routing, incoming, preferred_element_type=jnp.float32
     ).astype(jnp.bfloat16)

time: 415 us -> 424 us (1.022)
  waiting for transfers between devices: 128 us -> 149 us
  other arithmetic: 10.4 us -> 4.92 us
  matrix products: 37.4 us -> 32.5 us
    all_gather x3, waiting for transfers between devices: 62.2 us -> 90.5 us  [long_attention(): kv = lax.all_gather(kv, 'req', axis=0, tiled=True)]
    all_to_all x1, waiting for transfers between devices: 48.7 us -> 33.7 us  [local(): lax.all_to_all(outgoing, 'req', split_axis=1, concat_axis=1, tiled=True)]
    reduce_scatter x2 -> x1, waiting for transfers between devices: 9.34 us -> 15 us  [local(): lax.psum_scatter(jnp.dot(attended, out_weight, preferred_element_type=jnp...]
    concatenate x1 -> x0, other arithmetic: 5.48 us -> none  [local(): mixed_out = jnp.concatenate(mixed_parts, axis=1)]
    dot_general x2 -> x1, matrix products: 32.8 us -> 27.9 us  [local(): jnp.dot(attended, out_weight, preferred_element_type=jnp.float32)]
  transfers between devices with their start and end apart: 8 -> 7, of which waited for: 5 -> 5; matrix products, arithmetic and copies ran while one was open for 9% -> 5% of each run, Pallas kernels for 36% -> 35%
where the time goes in v5:
time: 424 us; the launch traced here: 422 us
  Pallas kernels  197 us (46%)
  waiting for transfers between devices  149 us (35%)
  matrix products  32.5 us (8%)
  between operations  14.1 us (3%)
  local copies, waits for them, and re-layouts  12.9 us (3%)
  starting transfers between devices  12 us (3%)
  other arithmetic  4.92 us (1%)
    pallas_call x3, Pallas kernels, long_attention_chunk(): pl.pallas_call(kernel, grid_spec=grid_spec, out_shape=out_shape, input_ou...  197 us
    all_gather x3, waiting for transfers between devices, long_attention(): kv = lax.all_gather(kv, 'req', axis=0, tiled=True)  90.5 us
    all_to_all x1, waiting for transfers between devices, local(): lax.all_to_all(outgoing, 'req', split_axis=1, concat_axis=1, tiled=True)  33.7 us
    dot_general x1, matrix products, local(): jnp.dot(attended, out_weight, preferred_element_type=jnp.float32)  27.9 us
    reduce_scatter x1, waiting for transfers between devices, local(): lax.psum_scatter(jnp.dot(attended, out_weight, preferred_element_type=jnp...  15 us
    ppermute x1, waiting for transfers between devices, short_attention(): v_prev = lax.ppermute(v_short, 'req', perm)  9.88 us
  transfers between devices with their start and end apart: 7, of which 5 were waited for; matrix products, arithmetic and copies ran while one was open for 5% of the time, Pallas kernels for 35%

profile of v5, /device:TPU:29, one launch (start us, length us, event | category | flops | bytes accessed | tf_op | source)
XLA Modules:
  0.0 422.4 jit_solution(17270371474527655120)
XLA Ops:
  7.2 1.3 fusion.31
  8.5 0.7 pad_maximum_fusion.2
  9.4 0.9 pad_maximum_fusion
  10.3 0.7 pad_maximum_fusion.1
  11.1 0.3 stack.10
  11.4 0.3 stack.9
  11.8 0.1 rem.82
  11.9 0.1 div.59
  12.0 0.1 ne.107
  12.1 0.1 copy.27
  12.2 0.1 reduce-window.8
  12.3 0.1 reduce
  12.4 0.1 convert_reduce_fusion.2
  12.5 0.1 select_reduce_fusion.2
  12.6 0.1 broadcast_in_dim.123
  12.7 0.2 broadcast_in_dim.124
  12.9 0.2 copy.47
  13.1 0.5 convert_reduce_fusion
  13.6 0.7 fusion.1
  14.3 2.8 copy.28
  17.1 6.6 %all-to-all-start = ((bf16[2,16,3,8192]{3,0,2,1:T(2,128)(2,1)}), bf16[2,16,3,8192]{3,0,2,1:T(2,128)(2,1)}, u32[]{:S(2)}, u32[]{:S(2)}) async-start(bf16[2,16,3,8192]{3,0,2,1:T(2,128)(2,1)} %bitcast.52), calls=%async_computation | async-start | bytes 3145728 | tf_op jit(solution)/shard_map/all_to_all | solution.py:241
  23.8 0.1 copy.46
  23.9 3.1 collective-permute-start.1
  27.0 2.1 collective-permute-start
  29.1 0.1 convert_reduce_fusion.1
  29.2 0.1 select_reduce_fusion
  29.4 0.2 and_and_fusion
  29.5 9.9 %collective-permute-done = bf16[128,512]{1,0:T(8,128)(2,1)S(1)} collective-permute-done((bf16[128,512]{1,0:T(8,128)(2,1)S(1)}, bf16[128,512]{1,0:T(8,128)(2,1)S(1)}, u32[]{:S(2)}, u32[]{:S(2)}) %collective-permute-start) | collective-permute-done | bytes 131104 | tf_op jit(solution)/shard_map/ppermute | solution.py:176
  39.4 0.1 copy.29
  39.6 0.9 pad_maximum_fusion.4
  40.5 33.7 %all-to-all-done = bf16[2,16,3,8192]{3,0,2,1:T(2,128)(2,1)} async-done(((bf16[2,16,3,8192]{3,0,2,1:T(2,128)(2,1)}), bf16[2,16,3,8192]{3,0,2,1:T(2,128)(2,1)}, u32[]{:S(2)}, u32[]{:S(2)}) %all-to-all-start) | async-done | bytes 1572896 | tf_op jit(solution)/shard_map/all_to_all | solution.py:241
  74.2 1.5 slice.38.q_ref
  75.7 2.6 copy.31
  78.3 1.1 slice.48
  79.4 0.5 fusion.33
  79.9 0.3 fusion.5
  80.2 0.5 fusion.13
  80.7 0.2 copy.45
  80.9 26.3 %all-gather.8.cloned.1.call-done.k_ref.v_ref = bf16[2048,1024]{1,0:T(8,128)(2,1)} async-done(((bf16[128,1024]{1,0:T(8,128)(2,1)}), bf16[2048,1024]{1,0:T(8,128)(2,1)}) %all-gather.8.cloned.1.call-update) | async-done | bytes 4194320 | tf_op jit(solution)/shard_map/all_gather | solution.py:163
  107.2 49.7 %shard_map.86 = (f32[4,4,512,128]{3,2,1,0:T(8,128)}, f32[4,4,512,128]{3,2,1,0:T(8,128)}, f32[4,4,512,128]{3,2,1,0:T(8,128)}) custom-call(s32[1]{0:T(128)} %bitcast.b_ref, bf16[512,2048]{1,0:T(8,128)(2,1)} %slice.38.q_ref, bf16[2048,1024]{1,0:T(8,128)(2,1)} %all-gather.8.cloned.1.call-done.k_ref.v_ref, bf16[2048,1024]{1,0:T(8,128)(2,1)} %all-gather.8.cloned.1.call-done.k_ref.v_ref), custom_call_target="tpu_custom_call" | custom-call | tf_op jit(solution)/shard_map/pallas_call | solution.py:144
  156.9 64.2 %all-gather.6.cloned.1.call-done.k_ref.v_ref = bf16[4096,1024]{1,0:T(8,128)(2,1)} async-done(((bf16[256,1024]{1,0:T(8,128)(2,1)}), bf16[4096,1024]{1,0:T(8,128)(2,1)}) %all-gather.6.cloned.1.call-update) | async-done | bytes 8388624 | tf_op jit(solution)/shard_map/all_gather | solution.py:163
  221.1 97.2 %shard_map.87 = (f32[4,4,512,128]{3,2,1,0:T(8,128)}, f32[4,4,512,128]{3,2,1,0:T(8,128)}, f32[4,4,512,128]{3,2,1,0:T(8,128)}) custom-call(s32[1]{0:T(128)} %bitcast.b_ref, bf16[512,2048]{1,0:T(8,128)(2,1)} %slice.38.q_ref, bf16[4096,1024]{1,0:T(8,128)(2,1)} %all-gather.6.cloned.1.call-done.k_ref.v_ref, ...), custom_call_target="tpu_custom_call", output_to_operand_aliasing={{0}: (4, {}), {1}: (5, {}), {2}: (6, {})} | custom-call | tf_op jit(solution)/shard_map/pallas_call | solution.py:144
  318.4 49.8 %shard_map.88 = bf16[512,2048]{1,0:T(8,128)(2,1)} custom-call(s32[1]{0:T(128)} %bitcast.b_ref, bf16[512,2048]{1,0:T(8,128)(2,1)} %slice.38.q_ref, bf16[2048,1024]{1,0:T(8,128)(2,1)} %all-gather.4.cloned.1.call-done.k_ref.v_ref, bf16[2048,1024]{1,0:T(8,128)(2,1)} %all-gather.4.cloned.1.call-done.k_ref.v_ref, f32[4,4,512,128]{3,2,1,0:T(8,128)} %get-tuple-element.14.refs_0_, ...), custom_call_target="tpu_custom_call" | custom-call | tf_op jit(solution)/shard_map/pallas_call | solution.py:144
  368.2 27.9 %convolution_convert_fusion = bf16[640,8192]{1,0:T(8,128)(2,1)} fusion(bf16[2048,8192]{1,0:T(8,128)(2,1)} %param.10, bf16[128,2048]{1,0:T(8,128)(2,1)S(1)} %copy.45, bf16[512,2048]{1,0:T(8,128)(2,1)} %shard_map.88), kind=kOutput, calls=%fused_computation | convolution fusion | flops 21485322240 | bytes 46661632 | tf_op jit(solution)/shard_map/dot_general | solution.py:270
  396.1 0.3 convolution_convert_fusion.2
  396.4 2.7 fusion
  399.1 1.7 copy.48
  400.8 15.0 %reduce-scatter.2.cloned.1.call-done = bf16[320,8192]{1,0:T(8,128)(2,1)} async-done(((bf16[640,8192]{1,0:T(8,128)(2,1)}), bf16[320,8192]{1,0:T(8,128)(2,1)}) %reduce-scatter.2.cloned.1.call-update) | async-done | bytes 5242896 | tf_op jit(solution)/shard_map/reduce_scatter | solution.py:269
  (41 shorter events, 0.4 us)
Async XLA Ops:
  7.2 2.2 slice-start
  7.2 2.2 slice-start.1
  7.2 100.0 %all-gather.8.cloned.1.call-start = ((), (), s32[]{:S(2)}) async-start(), calls=%async_computation.4 | async-start | bytes 4456448 | tf_op jit(solution)/shard_map/all_gather | solution.py:163
  8.5 2.6 copy-start.1
  9.3 211.8 %all-gather.6.cloned.1.call-start = ((), (), s32[]{:S(2)}) async-start(), calls=%async_computation.3 | async-start | bytes 8912896 | tf_op jit(solution)/shard_map/all_gather | solution.py:163
  9.3 2.1 copy-start.2
  10.3 1.5 copy-start.3
  10.3 1.8 copy-start.4
  10.3 2.2 copy-start.5
  10.3 308.1 %all-gather.4.cloned.1.call-start = ((), (), s32[]{:S(2)}) async-start(), calls=%async_computation.2 | async-start | bytes 4456448 | tf_op jit(solution)/shard_map/all_gather | solution.py:163
  17.1 57.1 %copy-start = (bf16[640,2048]{1,0:T(8,128)(2,1)S(1)}, bf16[640,2048]{1,0:T(8,128)(2,1)}, u32[]{:S(2)}) copy-start(bf16[640,2048]{1,0:T(8,128)(2,1)} %param.7) | copy-start | bytes 7864324
  17.1 57.1 %all-to-all-start = ((bf16[2,16,3,8192]{3,0,2,1:T(2,128)(2,1)}), bf16[2,16,3,8192]{3,0,2,1:T(2,128)(2,1)}, u32[]{:S(2)}, u32[]{:S(2)}) async-start(bf16[2,16,3,8192]{3,0,2,1:T(2,128)(2,1)} %bitcast.52), calls=%async_computation | async-start | bytes 3145728 | tf_op jit(solution)/shard_map/all_to_all | solution.py:241
  23.7 392.1 %reduce-scatter.2.cloned.1.call-start = ((), (), s32[]{:S(2)}) async-start(), calls=%async_computation.5 | async-start | bytes 15728640 | tf_op jit(solution)/shard_map/reduce_scatter | solution.py:269
  23.9 15.7 %collective-permute-start.1 = (bf16[128,512]{0,1:T(8,128)(2,1)S(1)}, bf16[128,512]{0,1:T(8,128)(2,1)}, u32[]{:S(2)}, u32[]{:S(2)}) collective-permute-start(bf16[128,512]{0,1:T(8,128)(2,1)S(1)} %copy.46), channel_id=1, source_target_pairs={{0,2},{2,4},{4,6},{6,8},{8,10},{10,12},{12,14},{14,16},{16,18},{18... | collective-permute-start | bytes 393224 | tf_op jit(solution)/shard_map/ppermute | solution.py:175
  27.0 12.4 %collective-permute-start = (bf16[128,512]{1,0:T(8,128)(2,1)S(1)}, bf16[128,512]{1,0:T(8,128)(2,1)S(1)}, u32[]{:S(2)}, u32[]{:S(2)}) collective-permute-start(bf16[128,512]{1,0:T(8,128)(2,1)S(1)} %get-tuple-element.36), channel_id=1, source_target_pairs={{0,2},{2,4},{4,6},{6,8},{8,10},{10,12},{12,14},{14,16},{16,18},{18... | collective-permute-start | bytes 393224 | tf_op jit(solution)/shard_map/ppermute | solution.py:176
Sparse Core Ops, SparseCore 0:
  10.8 96.3 all-gather.7
  110.0 111.1 all-gather.5
  223.9 74.6 all-gather.3
  396.2 19.5 reduce-scatter.1

commit v6 on v3

--- a/solution.py
+++ b/solution.py
@@ -42,8 +42,12 @@
         m_in, l_in, acc_in, m_out, l_out, acc_out = refs
     i = pl.program_id(1)
     t = pl.program_id(2)
-    b = b_ref[0]
+    lo = b_ref[0]
+    hi = b_ref[1]
+    diag = b_ref[2]
     per_tile = tk // chunk_rows
+    tile_lo = t * per_tile
+    tile_hi = tile_lo + per_tile - 1
     scale = HEAD_SIZE ** (-0.5)
 
     @pl.when(t == 0)
@@ -65,7 +69,9 @@
             cols = lax.broadcasted_iota(jnp.int32, (tq, tk), 1)
             src = t * per_tile + cols // chunk_rows
             key_pos = chunk * chunk_rows + cols % chunk_rows
-            allowed = (src < b) | ((src == b) & (key_pos <= rows))
+            allowed = (src >= lo) & (src <= hi) & (
+                (src < diag) | ((src == diag) & (key_pos <= rows))
+            )
         for g in range(group):
             qg = q_ref[:, g * HEAD_SIZE:(g + 1) * HEAD_SIZE]
             s = lax.dot_general(
@@ -84,11 +90,14 @@
             )
             m_out[g] = m_new
 
-    @pl.when(t * per_tile + per_tile - 1 < b)
+    full = (tile_lo >= lo) & (tile_hi <= hi) & (tile_hi < diag)
+    touched = (tile_hi >= lo) & (tile_lo <= hi)
+
+    @pl.when(full)
     def _full():
         step(False)
 
-    @pl.when((t * per_tile + per_tile - 1 >= b) & (t * per_tile <= b))
+    @pl.when(touched & jnp.logical_not(full))
     def _diag():
         step(True)
 
@@ -117,10 +126,13 @@
     )
     state_shape = jax.ShapeDtypeStruct((heads_kv, group, rows, HEAD_SIZE), jnp.float32)
     state_spec = pl.BlockSpec((None, group, tq, HEAD_SIZE), lambda h, i, t, b: (h, 0, i, 0))
-    kv_spec_k = pl.BlockSpec((tk, HEAD_SIZE), lambda h, i, t, b: (jnp.minimum(t, b[0] // per_tile), h))
-    kv_spec_v = pl.BlockSpec(
-        (tk, HEAD_SIZE), lambda h, i, t, b: (jnp.minimum(t, b[0] // per_tile), heads_kv + h)
-    )
+    def tile_of(t, b):
+        return jnp.minimum(
+            jnp.maximum(t, b[0] // per_tile), jnp.maximum(b[0], b[1]) // per_tile
+        )
+
+    kv_spec_k = pl.BlockSpec((tk, HEAD_SIZE), lambda h, i, t, b: (tile_of(t, b), h))
+    kv_spec_v = pl.BlockSpec((tk, HEAD_SIZE), lambda h, i, t, b: (tile_of(t, b), heads_kv + h))
     q_spec = pl.BlockSpec((tq, group * HEAD_SIZE), lambda h, i, t, b: (i, h))
     in_specs = [q_spec, kv_spec_k, kv_spec_v]
     operands = [b_arr, q_long, kv_chunk, kv_chunk]
@@ -153,20 +165,49 @@
     )(*operands)
 
 
-def long_attention(my_index, q_long, k_long, v_long):
-    b_arr = jnp.reshape(my_index, (1,)).astype(jnp.int32)
-    chunk_rows = LONG_DEV // LONG_CHUNKS
-    state = None
-    for c in range(LONG_CHUNKS):
+def long_attention(my_index, req_count, q_long, k_long, v_long):
+    half = req_count // 2
+    chunk_rows = LONG_DEV // 2
+    rows, q_cols = q_long.shape
+    heavy = my_index >= half
+    partner = jnp.where(heavy, my_index - half, my_index + half)
+    gathered = []
+    for c in range(2):
         kv = jnp.concatenate(
             [k_long[c * chunk_rows:(c + 1) * chunk_rows], v_long[c * chunk_rows:(c + 1) * chunk_rows]],
             axis=1,
         )
-        kv = lax.all_gather(kv, "req", axis=0, tiled=True)
-        state = long_attention_chunk(
-            b_arr, q_long, kv, state, c, c == 0, c == LONG_CHUNKS - 1
-        )
-    return state
+        gathered.append(lax.all_gather(kv, "req", axis=0, tiled=True))
+    partner_q = lax.ppermute(q_long, "req", [(s + half, s) for s in range(half)])
+
+    def params(lo, hi, diag):
+        return jnp.stack([lo, hi, diag]).astype(jnp.int32)
+
+    own_lo = jnp.where(heavy, half, 0)
+    state = long_attention_chunk(
+        params(own_lo, my_index, my_index), q_long, gathered[0], None, 0, True, False
+    )
+    help_hi = jnp.where(heavy, -1, half - 1)
+    helped = long_attention_chunk(
+        params(jnp.int32(0), help_hi, partner), partner_q, gathered[0], None, 0, True, False
+    )
+    state, helped = lax.optimization_barrier((state, helped))
+    h_max, h_sum, h_acc = helped
+    h_out = (h_acc / jnp.where(h_sum > 0, h_sum, 1.0)).astype(jnp.bfloat16)
+    back = [(s, s + half) for s in range(half)]
+    h_out = lax.ppermute(h_out, "req", back)
+    h_max = lax.ppermute(h_max[..., :1], "req", back)
+    h_sum = lax.ppermute(h_sum[..., :1], "req", back)
+    own_max, own_sum, own_acc = long_attention_chunk(
+        params(jnp.int32(0), my_index, my_index), q_long, gathered[1], state, 1, False, False,
+    )
+    top = jnp.maximum(own_max, jnp.where(heavy, h_max, NEGATIVE_FILL))
+    own_w = jnp.exp(own_max - top)
+    help_w = jnp.where(heavy, jnp.exp(h_max - top) * h_sum, 0.0)
+    total = own_sum * own_w + help_w
+    out = (own_acc * own_w + h_out.astype(jnp.float32) * help_w) / total
+    heads_kv, group = out.shape[0], out.shape[1]
+    return out.transpose(2, 0, 1, 3).reshape(rows, heads_kv * group * HEAD_SIZE).astype(jnp.bfloat16)
 
 
 def short_attention(my_index, req_count, q_short, k_short, v_short, short_pages, short_fill):
@@ -255,7 +296,7 @@
     ).astype(jnp.bfloat16)
     incoming, queries = lax.optimization_barrier((incoming, queries))
     att_long = long_attention(
-        my_index, queries[:LONG_DEV], rotated_key_rows[:LONG_DEV], stream_value_rows[:LONG_DEV]
+        my_index, req_count, queries[:LONG_DEV], rotated_key_rows[:LONG_DEV], stream_value_rows[:LONG_DEV]
     )
     att_short = short_attention(
         my_index,

time: 414 us -> 545 us (1.32)
  blocking collectives: 0 us -> 71.9 us
  waiting for transfers between devices: 144 us -> 202 us
  Pallas kernels: 192 us -> 166 us
  other arithmetic: 3.42 us -> 23 us
  local copies, waits for them, and re-layouts: 14.7 us -> 21 us
    all_gather x2, waiting for transfers between devices: 72.1 us -> 186 us  [long_attention(): gathered.append(lax.all_gather(kv, 'req', axis=0, tiled=True))]
    all_to_all x0 -> x1, blocking collectives: none -> 71.9 us  [local(): lax.all_to_all(outgoing, 'req', split_axis=1, concat_axis=1, tiled=True)]
    all_to_all x1 -> x0, waiting for transfers between devices: 50.1 us -> none  [local(): lax.all_to_all(outgoing, 'req', split_axis=1, concat_axis=1, tiled=True)]
    pallas_call x2 -> x3, Pallas kernels: 192 us -> 166 us  [long_attention_chunk(): pl.pallas_call(kernel, grid_spec=grid_spec, out_shape=out_shape, input_ou...]
    convert_element_type x0 -> x2, other arithmetic: none -> 14.5 us  [the longest x1 8.78 us: long_attention(): out.transpose(2, 0, 1, 3).reshape(rows, heads_kv * group * HEAD_SIZE)]
    ppermute x0 -> x4, starting transfers between devices: none -> 9.19 us  [the longest x1 5.1 us: long_attention(): lax.ppermute(q_long, 'req', [(s + half, s) for s in range(half)])]
    all_to_all x1 -> x0, starting transfers between devices: 6.65 us -> none  [local(): lax.all_to_all(outgoing, 'req', split_axis=1, concat_axis=1, tiled=True)]
    ppermute x1, waiting for transfers between devices: 6.41 us -> 0.01 us  [short_attention(): v_prev = lax.ppermute(v_short, 'req', perm)]
  transfers between devices with their start and end apart: 6 -> 9, of which waited for: 5 -> 3; matrix products, arithmetic and copies ran while one was open for 5% -> 6% of each run, Pallas kernels for 23% -> 31%
where the time goes in v6:
time: 545 us; the launch traced here: 543 us
  waiting for transfers between devices  202 us (37%)
  Pallas kernels  166 us (30%)
  blocking collectives  71.9 us (13%)
  matrix products  31.4 us (6%)
  other arithmetic  23 us (4%)
  local copies, waits for them, and re-layouts  21 us (4%)
  between operations  14.3 us (3%)
  starting transfers between devices  13.6 us (2%)
    all_gather x2, waiting for transfers between devices, long_attention(): gathered.append(lax.all_gather(kv, 'req', axis=0, tiled=True))  186 us
    pallas_call x3, Pallas kernels, long_attention_chunk(): pl.pallas_call(kernel, grid_spec=grid_spec, out_shape=out_shape, input_ou...  166 us
    all_to_all x1, blocking collectives, local(): lax.all_to_all(outgoing, 'req', split_axis=1, concat_axis=1, tiled=True)  71.9 us
    dot_general x1, matrix products, local(): jnp.dot(attended, out_weight, preferred_element_type=jnp.float32)  28.2 us
    reduce_scatter x1, waiting for transfers between devices, local(): lax.psum_scatter(jnp.dot(attended, out_weight, preferred_element_type=jnp...  15.5 us
  transfers between devices with their start and end apart: 9, of which 3 were waited for; matrix products, arithmetic and copies ran while one was open for 6% of the time, Pallas kernels for 31%

profile of v6, /device:TPU:29, one launch (start us, length us, event | category | flops | bytes accessed | tf_op | source)
XLA Modules:
  0.0 543.0 jit_solution(6311148946665837948)
XLA Ops:
  7.2 1.2 fusion.40
  8.4 1.1 fusion.41
  9.5 0.9 pad_maximum_fusion.1
  10.4 0.9 pad_maximum_fusion
  11.4 0.3 stack.35
  11.7 0.3 stack.36
  12.8 0.6 select_reduce_fusion.2
  13.7 0.2 copy.61
  14.0 0.6 broadcast_compare_fusion
  14.6 0.5 convert_reduce_fusion
  15.1 0.7 fusion.1
  15.8 1.6 copy.41
  17.4 71.9 %all_to_all.5 = bf16[2,16,3,8192]{3,0,2,1:T(2,128)(2,1)} all-to-all(bf16[2,16,3,8192]{3,0,2,1:T(2,128)(2,1)S(1)} %bitcast.66), channel_id=1, replica_groups=mesh['req'=16,'tp'=2] {'req'}, dimensions={1} | all-to-all | bytes 3145728 | tf_op jit(solution)/shard_map/all_to_all | solution.py:283
  89.5 5.1 collective-permute-start
  94.6 0.7 copy.60
  95.3 2.2 collective-permute-start.5
  97.6 2.1 collective-permute-start.4
  99.7 0.6 add_add_fusion.b_ref
  100.2 0.6 fusion.35.b_ref
  100.8 0.7 convert_reduce_fusion.1
  101.6 0.6 multiply_subtract_fusion.1
  102.2 81.7 %all-gather.5.cloned.1.call-done.k_ref.v_ref = bf16[4096,1024]{1,0:T(8,128)(2,1)} async-done(((bf16[256,1024]{1,0:T(8,128)(2,1)}), bf16[4096,1024]{1,0:T(8,128)(2,1)}) %all-gather.5.cloned.1.call-update) | async-done | bytes 8388624 | tf_op jit(solution)/shard_map/all_gather | solution.py:180
  183.9 55.2 %shard_map.86 = (f32[4,4,512,128]{3,2,1,0:T(8,128)}, f32[4,4,512,128]{3,2,1,0:T(8,128)}, f32[4,4,512,128]{3,2,1,0:T(8,128)}) custom-call(s32[3]{0:T(128)} %add_add_fusion.b_ref, bf16[512,2048]{1,0:T(8,128)(2,1)} %copy-done, bf16[4096,1024]{1,0:T(8,128)(2,1)} %all-gather.5.cloned.1.call-done.k_ref.v_ref, ...), custom_call_target="tpu_custom_call" | custom-call | tf_op jit(solution)/shard_map/pallas_call | solution.py:157
  239.1 11.8 %shard_map.87 = (f32[4,4,512,128]{3,2,1,0:T(8,128)}, f32[4,4,512,128]{3,2,1,0:T(8,128)}, f32[4,4,512,128]{3,2,1,0:T(8,128)}) custom-call(s32[3]{0:T(128)} %fusion.35.b_ref, bf16[512,2048]{1,0:T(8,128)(2,1)} %collective-permute-done.q_ref, bf16[4096,1024]{1,0:T(8,128)(2,1)} %all-gather.5.cloned.1.call-done.k_ref.v_ref, ...), custom_call_target="tpu_custom_call" | custom-call | tf_op jit(solution)/shard_map/pallas_call | solution.py:157
  250.9 5.8 %fusion.7 = bf16[4,4,512,128]{3,2,1,0:T(8,128)(2,1)} fusion(f32[4,4,512,128]{3,2,1,0:T(8,128)} %get-tuple-element.32, f32[4,4,512,128]{3,2,1,0:T(8,128)} %get-tuple-element.33), kind=kLoop, calls=%fused_computation.13 | loop fusion | flops 4194304 | bytes 10485760 | tf_op jit(solution)/shard_map/convert_element_type | solution.py:196
  256.7 1.3 collective-permute-start.2
  258.3 0.6 fusion.34.b_ref
  259.1 1.0 pad_maximum_fusion.3
  260.1 2.6 copy.47
  262.7 1.1 slice.46
  263.8 0.5 fusion.42
  264.4 0.3 fusion.12
  264.7 2.8 copy.42
  267.5 1.3 collective-permute-start.1
  268.8 0.5 fusion.20
  269.3 2.8 copy.43
  272.2 1.5 collective-permute-start.3
  273.7 104.4 %all-gather.3.cloned.1.call-done.k_ref.v_ref = bf16[4096,1024]{1,0:T(8,128)(2,1)} async-done(((bf16[256,1024]{1,0:T(8,128)(2,1)}), bf16[4096,1024]{1,0:T(8,128)(2,1)}) %all-gather.3.cloned.1.call-update) | async-done | bytes 8388624 | tf_op jit(solution)/shard_map/all_gather | solution.py:180
  378.1 99.0 %shard_map.88 = (f32[4,4,512,128]{3,2,1,0:T(8,128)}, f32[4,4,512,128]{3,2,1,0:T(8,128)}, f32[4,4,512,128]{3,2,1,0:T(8,128)}) custom-call(s32[3]{0:T(128)} %fusion.34.b_ref, bf16[512,2048]{1,0:T(8,128)(2,1)} %copy-done, bf16[4096,1024]{1,0:T(8,128)(2,1)} %all-gather.3.cloned.1.call-done.k_ref.v_ref, ...), custom_call_target="tpu_custom_call", output_to_operand_aliasing={{0}: (4, {}), {1}: (5, {}), {2}: (6, {})} | custom-call | tf_op jit(solution)/shard_map/pallas_call | solution.py:157
  477.2 8.8 %fusion.11 = bf16[512,4,4,128]{3,0,2,1:T(8,128)(2,1)S(1)} fusion(f32[4,4,512,128]{3,2,1,0:T(8,128)} %get-tuple-element.34, f32[4,4,512]{2,1,0:T(4,128)S(1)} %bitcast.76, f32[4,4,512]{2,1,0:T(4,128)S(1)} %bitcast.75, pred[]{:T(512)S(6)} %ge.11, bf16[4,4,512,128]{3,2,1,0:T(8,128)(2,1)} %collective-permute-done.2, f32[4,4,512,128]{3,2,1,0:T(8,128)} %get-tuple-element.29, ...), kind=kLoop, calls=%fused_computation.20 | loop fusion | flops 13631488 | bytes 16875520 | tf_op jit(solution)/shard_map/convert_element_type | solution.py:210
  486.0 2.3 copy.44
  488.3 28.2 %convolution_convert_fusion = bf16[640,8192]{1,0:T(8,128)(2,1)} fusion(bf16[2048,8192]{1,0:T(8,128)(2,1)} %param.10, bf16[128,2048]{0,1:T(8,128)(2,1)S(1)} %bitcast.79, bf16[512,2048]{0,1:T(8,128)(2,1)} %bitcast.68), kind=kOutput, calls=%fused_computation | convolution fusion | flops 21485322240 | bytes 46661632 | tf_op jit(solution)/shard_map/dot_general | solution.py:312
  516.6 0.6 copy-done.14
  517.2 0.3 convolution_convert_fusion.2
  517.5 0.5 copy-done.3
  517.9 1.3 fusion
  519.2 1.7 copy.62
  520.9 15.5 %reduce-scatter.2.cloned.1.call-done = bf16[320,8192]{1,0:T(8,128)(2,1)} async-done(((bf16[640,8192]{1,0:T(8,128)(2,1)}), bf16[320,8192]{1,0:T(8,128)(2,1)}) %reduce-scatter.2.cloned.1.call-update) | async-done | bytes 5242896 | tf_op jit(solution)/shard_map/reduce_scatter | solution.py:311
  (82 shorter events, 1.9 us)
Async XLA Ops:
  7.2 4.2 copy-start.4
  7.2 4.5 copy-start.5
  7.2 176.7 %all-gather.5.cloned.1.call-start = ((), (), s32[]{:S(2)}) async-start(), calls=%async_computation.3 | async-start | bytes 8912896 | tf_op jit(solution)/shard_map/all_gather | solution.py:180
  9.5 2.6 copy-start.8
  9.5 2.9 copy-start.15
  9.5 3.3 copy-start.18
  10.4 367.7 %all-gather.3.cloned.1.call-start = ((), (), s32[]{:S(2)}) async-start(), calls=%async_computation.2 | async-start | bytes 8912896 | tf_op jit(solution)/shard_map/all_gather | solution.py:180
  11.3 525.1 %reduce-scatter.2.cloned.1.call-start = ((), (), s32[]{:S(2)}) async-start(), calls=%async_computation.4 | async-start | bytes 15728640 | tf_op jit(solution)/shard_map/reduce_scatter | solution.py:311
  12.6 1.3 copy-start.13
  12.8 0.7 copy-start.16
  12.8 0.6 copy-start.9
  12.8 0.6 copy-start.11
  13.4 4.0 copy-start.19
  15.8 73.6 %copy-start.1 = (bf16[640,2048]{1,0:T(8,128)(2,1)S(1)}, bf16[640,2048]{1,0:T(8,128)(2,1)}, u32[]{:S(2)}) copy-start(bf16[640,2048]{1,0:T(8,128)(2,1)} %param.7) | copy-start | bytes 7864324
  17.4 77.2 %slice-start = ((bf16[640,512]{1,0:T(8,128)(2,1)}), bf16[128,512]{1,0:T(8,128)(2,1)S(1)}, s32[]{:S(2)}) async-start(bf16[640,512]{1,0:T(8,128)(2,1)} %param.8), calls=%async_computation.5 | async-start | bytes 262144 | tf_op jit(solution)/shard_map/slice | solution.py:305
  89.5 94.4 %copy-start = (bf16[512,2048]{1,0:T(8,128)(2,1)}, bf16[512,2048]{1,0:T(8,128)(2,1)S(1)}, u32[]{:S(2)}) copy-start(bf16[512,2048]{1,0:T(8,128)(2,1)S(1)} %slice.36.q_ref) | copy-start | bytes 6291460
  89.5 149.6 %collective-permute-start = (bf16[512,2048]{1,0:T(8,128)(2,1)S(1)}, bf16[512,2048]{1,0:T(8,128)(2,1)}, u32[]{:S(2)}, u32[]{:S(2)}) collective-permute-start(bf16[512,2048]{1,0:T(8,128)(2,1)S(1)} %slice.36.q_ref), channel_id=1, source_target_pairs={{16,0},{18,2},{20,4},{22,6},{24,8},{26,10},{28,12},{30,14},{17,1},... | collective-permute-start | bytes 6291464 | tf_op jit(solution)/shard_map/ppermute | solution.py:181
  95.3 163.7 %collective-permute-start.5 = (bf16[128,512]{0,1:T(8,128)(2,1)}, bf16[128,512]{0,1:T(8,128)(2,1)}, u32[]{:S(2)}, u32[]{:S(2)}) collective-permute-start(bf16[128,512]{0,1:T(8,128)(2,1)} %copy.60), channel_id=1, source_target_pairs={{0,2},{2,4},{4,6},{6,8},{8,10},{10,12},{12,14},{14,16},{16,18},{18... | collective-permute-start | bytes 393224 | tf_op jit(solution)/shard_map/ppermute | solution.py:217
  97.5 141.6 %copy-start.6 = (bf16[128,512]{1,0:T(8,128)(2,1)}, bf16[128,512]{1,0:T(8,128)(2,1)S(1)}, u32[]{:S(2)}) copy-start(bf16[128,512]{1,0:T(8,128)(2,1)S(1)} %slice.43) | copy-start | bytes 393220
  97.6 161.3 %collective-permute-start.4 = (bf16[128,512]{1,0:T(8,128)(2,1)S(1)}, bf16[128,512]{1,0:T(8,128)(2,1)S(1)}, u32[]{:S(2)}, u32[]{:S(2)}) collective-permute-start(bf16[128,512]{1,0:T(8,128)(2,1)S(1)} %slice.43), channel_id=1, source_target_pairs={{0,2},{2,4},{4,6},{6,8},{8,10},{10,12},{12,14},{14,16},{16,18},{18... | collective-permute-start | bytes 393224 | tf_op jit(solution)/shard_map/ppermute | solution.py:218
  250.9 7.1 %copy-start.10 = (s32[51]{0:T(128)S(1)}, s32[51]{0:T(128)}, u32[]{:S(2)}) copy-start(s32[51]{0:T(128)} %copy-done.9) | copy-start | bytes 616
  250.9 7.1 %copy-start.12 = (s32[51]{0:T(128)S(1)}, s32[51]{0:T(128)}, u32[]{:S(2)}) copy-start(s32[51]{0:T(128)} %copy-done.11) | copy-start | bytes 616
  250.9 7.2 %copy-start.17 = (s32[128]{0:T(128)S(1)}, s32[128]{0:T(128)}, u32[]{:S(2)}) copy-start(s32[128]{0:T(128)} %copy-done.16) | copy-start | bytes 1540
  250.9 8.0 %copy-start.7 = (bf16[128,512]{1,0:T(8,128)(2,1)S(1)}, bf16[128,512]{1,0:T(8,128)(2,1)}, u32[]{:S(2)}) copy-start(bf16[128,512]{1,0:T(8,128)(2,1)} %copy-done.6) | copy-start | bytes 393220
  250.9 9.2 %copy-start.2 = (bf16[640,2048]{1,0:T(8,128)(2,1)S(1)}, bf16[640,2048]{1,0:T(8,128)(2,1)}, u32[]{:S(2)}) copy-start(bf16[640,2048]{1,0:T(8,128)(2,1)} %param.7) | copy-start | bytes 7864324
  256.7 220.5 %collective-permute-start.2 = (bf16[4,4,512,128]{3,2,1,0:T(8,128)(2,1)}, bf16[4,4,512,128]{3,2,1,0:T(8,128)(2,1)}, u32[]{:S(2)}, u32[]{:S(2)}) collective-permute-start(bf16[4,4,512,128]{3,2,1,0:T(8,128)(2,1)} %fusion.7), channel_id=1, source_target_pairs={{0,16},{2,18},{4,20},{6,22},{8,24},{10,26},{12,28},{14,30},{1,17},... | collective-permute-start | bytes 6291464 | tf_op jit(solution)/shard_map/ppermute | solution.py:198
  264.4 4.5 copy-start.20
  267.5 209.6 %collective-permute-start.1 = (f32[4,4,512,1]{2,1,3,0:T(4,128)S(1)}, f32[4,4,512,1]{2,1,3,0:T(4,128)S(1)}, u32[]{:S(2)}, u32[]{:S(2)}) collective-permute-start(f32[4,4,512,1]{2,1,3,0:T(4,128)S(1)} %copy.42), channel_id=1, source_target_pairs={{0,16},{2,18},{4,20},{6,22},{8,24},{10,26},{12,28},{14,30},{1,17},... | collective-permute-start | bytes 98312 | tf_op jit(solution)/shard_map/ppermute | solution.py:199
  272.2 205.0 %collective-permute-start.3 = (f32[4,4,512,1]{2,1,3,0:T(4,128)S(1)}, f32[4,4,512,1]{2,1,3,0:T(4,128)S(1)}, u32[]{:S(2)}, u32[]{:S(2)}) collective-permute-start(f32[4,4,512,1]{2,1,3,0:T(4,128)S(1)} %copy.43), channel_id=1, source_target_pairs={{0,16},{2,18},{4,20},{6,22},{8,24},{10,26},{12,28},{14,30},{1,17},... | collective-permute-start | bytes 98312 | tf_op jit(solution)/shard_map/ppermute | solution.py:200
  516.5 0.7 copy-start.14
  516.5 1.4 copy-start.3
Sparse Core Ops, SparseCore 0:
  11.4 172.4 all-gather.4
  187.2 190.8 all-gather.2
  516.7 19.7 reduce-scatter.1

commit v7 on v3

--- a/solution.py
+++ b/solution.py
@@ -60,6 +60,7 @@
     def step(masked):
         k = k_ref[...]
         v = v_ref[...]
+        v_ext = jnp.concatenate([v, jnp.ones(v.shape, v.dtype)], axis=1)
         if masked:
             rows = i * tq + lax.broadcasted_iota(jnp.int32, (tq, tk), 0)
             cols = lax.broadcasted_iota(jnp.int32, (tq, tk), 1)
@@ -77,11 +78,12 @@
             m_new = jnp.maximum(m_prev, jnp.max(s, axis=1, keepdims=True))
             p = jnp.exp(s - m_new[:, :1])
             alpha = jnp.exp(m_prev - m_new)
-            l_out[g] = alpha * l_out[g] + jnp.sum(p, axis=1, keepdims=True)
-            acc_out[g] = acc_out[g] * alpha + lax.dot_general(
-                p.astype(jnp.bfloat16), v, (((1,), (0,)), ((), ())),
+            pv = lax.dot_general(
+                p.astype(jnp.bfloat16), v_ext, (((1,), (0,)), ((), ())),
                 preferred_element_type=jnp.float32,
             )
+            l_out[g] = alpha * l_out[g] + pv[:, HEAD_SIZE:]
+            acc_out[g] = acc_out[g] * alpha + pv[:, :HEAD_SIZE]
             m_out[g] = m_new
 
     @pl.when(t * per_tile + per_tile - 1 < b)

time: 414 us -> 398 us (0.961)
  Pallas kernels: 192 us -> 160 us
  waiting for transfers between devices: 144 us -> 159 us
    pallas_call x2, Pallas kernels: 192 us -> 160 us  [long_attention_chunk(): pl.pallas_call(kernel, grid_spec=grid_spec, out_shape=out_shape, input_ou...]
    all_gather x2, waiting for transfers between devices: 72.1 us -> 87.8 us  [long_attention(): kv = lax.all_gather(kv, 'req', axis=0, tiled=True)]
  transfers between devices with their start and end apart: 6 -> 6, of which waited for: 5 -> 5; matrix products, arithmetic and copies ran while one was open for 5% -> 5% of each run, Pallas kernels for 23% -> 20%
where the time goes in v7:
time: 398 us; the launch traced here: 397 us
  Pallas kernels  160 us (40%)
  waiting for transfers between devices  159 us (40%)
  matrix products  32.5 us (8%)
  local copies, waits for them, and re-layouts  14.7 us (4%)
  between operations  14.1 us (4%)
  starting transfers between devices  12 us (3%)
    pallas_call x2, Pallas kernels, long_attention_chunk(): pl.pallas_call(kernel, grid_spec=grid_spec, out_shape=out_shape, input_ou...  160 us
    all_gather x2, waiting for transfers between devices, long_attention(): kv = lax.all_gather(kv, 'req', axis=0, tiled=True)  87.8 us
    all_to_all x1, waiting for transfers between devices, local(): lax.all_to_all(outgoing, 'req', split_axis=1, concat_axis=1, tiled=True)  50.1 us
    dot_general x1, matrix products, local(): jnp.dot(attended, out_weight, preferred_element_type=jnp.float32)  27.9 us
    reduce_scatter x1, waiting for transfers between devices, local(): lax.psum_scatter(jnp.dot(attended, out_weight, preferred_element_type=jnp...  15 us
  transfers between devices with their start and end apart: 6, of which 5 were waited for; matrix products, arithmetic and copies ran while one was open for 5% of the time, Pallas kernels for 20%

profile of v7, /device:TPU:29, one launch (start us, length us, event | category | flops | bytes accessed | tf_op | source)
XLA Modules:
  0.0 396.6 jit_solution(62461042404657061)
XLA Ops:
  7.2 1.1 fusion.31
  8.3 1.1 fusion.32
  9.4 0.9 pad_maximum_fusion.1
  10.3 0.0 all-gather.3.cloned.1.call-start
  10.4 0.9 pad_maximum_fusion
  11.3 0.3 stack.10
  11.6 0.3 stack.9
  12.0 0.1 rem.82
  12.1 0.1 div.59
  12.2 0.1 ne.107
  12.3 0.1 copy.24
  12.4 0.1 reduce-window.8
  12.5 0.1 reduce
  12.6 0.1 convert_reduce_fusion.2
  12.7 0.1 select_reduce_fusion.2
  12.8 0.1 broadcast_in_dim.123
  12.9 0.2 broadcast_in_dim.124
  13.1 0.2 copy.44
  13.3 0.5 convert_reduce_fusion
  13.8 0.7 fusion.1
  14.5 2.8 copy.25
  17.3 6.6 %all-to-all-start = ((bf16[2,16,3,8192]{3,0,2,1:T(2,128)(2,1)}), bf16[2,16,3,8192]{3,0,2,1:T(2,128)(2,1)}, u32[]{:S(2)}, u32[]{:S(2)}) async-start(bf16[2,16,3,8192]{3,0,2,1:T(2,128)(2,1)} %bitcast.52), calls=%async_computation | async-start | bytes 3145728 | tf_op jit(solution)/shard_map/all_to_all | solution.py:244
  24.0 0.1 copy.43
  24.1 3.1 collective-permute-start.1
  27.2 0.9 slice.35
  28.1 2.1 collective-permute-start
  30.3 0.1 convert_reduce_fusion.1
  30.4 0.1 select_reduce_fusion
  30.5 0.2 and_and_fusion
  30.7 6.4 %collective-permute-done = bf16[128,512]{1,0:T(8,128)(2,1)S(1)} collective-permute-done((bf16[128,512]{1,0:T(8,128)(2,1)S(1)}, bf16[128,512]{1,0:T(8,128)(2,1)S(1)}, u32[]{:S(2)}, u32[]{:S(2)}) %collective-permute-start) | collective-permute-done | bytes 131104 | tf_op jit(solution)/shard_map/ppermute | solution.py:179
  37.1 0.1 copy.26
  37.3 50.1 %all-to-all-done = bf16[2,16,3,8192]{3,0,2,1:T(2,128)(2,1)} async-done(((bf16[2,16,3,8192]{3,0,2,1:T(2,128)(2,1)}), bf16[2,16,3,8192]{3,0,2,1:T(2,128)(2,1)}, u32[]{:S(2)}, u32[]{:S(2)}) %all-to-all-start) | async-done | bytes 1572896 | tf_op jit(solution)/shard_map/all_to_all | solution.py:244
  87.4 1.5 slice.30.q_ref
  88.9 2.6 copy.28
  91.5 1.1 slice.38
  92.6 0.5 fusion.33
  93.1 0.3 fusion.5
  93.4 0.5 fusion.13
  93.9 0.2 copy.42
  94.1 54.1 %all-gather.5.cloned.1.call-done.k_ref.v_ref = bf16[4096,1024]{1,0:T(8,128)(2,1)} async-done(((bf16[256,1024]{1,0:T(8,128)(2,1)}), bf16[4096,1024]{1,0:T(8,128)(2,1)}) %all-gather.5.cloned.1.call-update) | async-done | bytes 8388624 | tf_op jit(solution)/shard_map/all_gather | solution.py:167
  148.3 80.1 %shard_map.86 = (f32[4,4,512,128]{3,2,1,0:T(8,128)}, f32[4,4,512,128]{3,2,1,0:T(8,128)}, f32[4,4,512,128]{3,2,1,0:T(8,128)}) custom-call(s32[1]{0:T(128)} %bitcast.b_ref, bf16[512,2048]{1,0:T(8,128)(2,1)} %slice.30.q_ref, bf16[4096,1024]{1,0:T(8,128)(2,1)} %all-gather.5.cloned.1.call-done.k_ref.v_ref, bf16[4096,1024]{1,0:T(8,128)(2,1)} %all-gather.5.cloned.1.call-done.k_ref.v_ref), custom_call_target="tpu_custom_call" | custom-call | tf_op jit(solution)/shard_map/pallas_call | solution.py:147
  228.4 33.7 %all-gather.3.cloned.1.call-done.k_ref.v_ref = bf16[4096,1024]{1,0:T(8,128)(2,1)} async-done(((bf16[256,1024]{1,0:T(8,128)(2,1)}), bf16[4096,1024]{1,0:T(8,128)(2,1)}) %all-gather.3.cloned.1.call-update) | async-done | bytes 8388624 | tf_op jit(solution)/shard_map/all_gather | solution.py:167
  262.1 80.3 %shard_map.87 = bf16[512,2048]{1,0:T(8,128)(2,1)} custom-call(s32[1]{0:T(128)} %bitcast.b_ref, bf16[512,2048]{1,0:T(8,128)(2,1)} %slice.30.q_ref, bf16[4096,1024]{1,0:T(8,128)(2,1)} %all-gather.3.cloned.1.call-done.k_ref.v_ref, bf16[4096,1024]{1,0:T(8,128)(2,1)} %all-gather.3.cloned.1.call-done.k_ref.v_ref, f32[4,4,512,128]{3,2,1,0:T(8,128)} %get-tuple-element.8.refs_0_, ...), custom_call_target="tpu_custom_call" | custom-call | tf_op jit(solution)/shard_map/pallas_call | solution.py:147
  342.4 27.9 %convolution_convert_fusion = bf16[640,8192]{1,0:T(8,128)(2,1)} fusion(bf16[2048,8192]{1,0:T(8,128)(2,1)} %param.10, bf16[128,2048]{1,0:T(8,128)(2,1)S(1)} %copy.42, bf16[512,2048]{1,0:T(8,128)(2,1)} %shard_map.87), kind=kOutput, calls=%fused_computation | convolution fusion | flops 21485322240 | bytes 46661632 | tf_op jit(solution)/shard_map/dot_general | solution.py:273
  370.3 0.3 convolution_convert_fusion.2
  370.6 2.7 fusion
  373.3 1.7 copy.45
  375.0 15.0 %reduce-scatter.2.cloned.1.call-done = bf16[320,8192]{1,0:T(8,128)(2,1)} async-done(((bf16[640,8192]{1,0:T(8,128)(2,1)}), bf16[320,8192]{1,0:T(8,128)(2,1)}) %reduce-scatter.2.cloned.1.call-update) | async-done | bytes 5242896 | tf_op jit(solution)/shard_map/reduce_scatter | solution.py:272
  (36 shorter events, 0.3 us)
Async XLA Ops:
  7.2 141.1 %all-gather.5.cloned.1.call-start = ((), (), s32[]{:S(2)}) async-start(), calls=%async_computation.3 | async-start | bytes 8912896 | tf_op jit(solution)/shard_map/all_gather | solution.py:167
  8.3 3.0 copy-start.2
  9.4 2.2 copy-start.1
  10.3 251.8 %all-gather.3.cloned.1.call-start = ((), (), s32[]{:S(2)}) async-start(), calls=%async_computation.2 | async-start | bytes 8912896 | tf_op jit(solution)/shard_map/all_gather | solution.py:167
  10.4 1.6 copy-start.3
  10.4 1.9 copy-start.4
  10.4 2.3 copy-start.5
  17.3 6.7 %slice-start = ((bf16[640,512]{1,0:T(8,128)(2,1)}), bf16[128,512]{1,0:T(8,128)(2,1)S(1)}, s32[]{:S(2)}) async-start(bf16[640,512]{1,0:T(8,128)(2,1)} %param.8), calls=%async_computation.5 | async-start | bytes 262144 | tf_op jit(solution)/shard_map/slice | solution.py:266
  17.3 70.1 %copy-start = (bf16[640,2048]{1,0:T(8,128)(2,1)S(1)}, bf16[640,2048]{1,0:T(8,128)(2,1)}, u32[]{:S(2)}) copy-start(bf16[640,2048]{1,0:T(8,128)(2,1)} %param.7) | copy-start | bytes 7864324
  17.3 70.1 %all-to-all-start = ((bf16[2,16,3,8192]{3,0,2,1:T(2,128)(2,1)}), bf16[2,16,3,8192]{3,0,2,1:T(2,128)(2,1)}, u32[]{:S(2)}, u32[]{:S(2)}) async-start(bf16[2,16,3,8192]{3,0,2,1:T(2,128)(2,1)} %bitcast.52), calls=%async_computation | async-start | bytes 3145728 | tf_op jit(solution)/shard_map/all_to_all | solution.py:244
  24.0 366.1 %reduce-scatter.2.cloned.1.call-start = ((), (), s32[]{:S(2)}) async-start(), calls=%async_computation.4 | async-start | bytes 15728640 | tf_op jit(solution)/shard_map/reduce_scatter | solution.py:272
  24.1 13.1 %collective-permute-start.1 = (bf16[128,512]{0,1:T(8,128)(2,1)S(1)}, bf16[128,512]{0,1:T(8,128)(2,1)S(1)}, u32[]{:S(2)}, u32[]{:S(2)}) collective-permute-start(bf16[128,512]{0,1:T(8,128)(2,1)S(1)} %copy.43), channel_id=1, source_target_pairs={{0,2},{2,4},{4,6},{6,8},{8,10},{10,12},{12,14},{14,16},{16,18},{18... | collective-permute-start | bytes 393224 | tf_op jit(solution)/shard_map/ppermute | solution.py:178
  28.1 8.9 %collective-permute-start = (bf16[128,512]{1,0:T(8,128)(2,1)S(1)}, bf16[128,512]{1,0:T(8,128)(2,1)S(1)}, u32[]{:S(2)}, u32[]{:S(2)}) collective-permute-start(bf16[128,512]{1,0:T(8,128)(2,1)S(1)} %slice.35), channel_id=1, source_target_pairs={{0,2},{2,4},{4,6},{6,8},{8,10},{10,12},{12,14},{14,16},{16,18},{18... | collective-permute-start | bytes 393224 | tf_op jit(solution)/shard_map/ppermute | solution.py:179
Sparse Core Ops, SparseCore 0:
  10.8 137.4 all-gather.4
  151.1 111.0 all-gather.2
  370.4 19.5 reduce-scatter.1

commit v8 on v7

--- a/solution.py
+++ b/solution.py
@@ -16,6 +16,7 @@
 
 
 NEGATIVE_FILL = -1e30
+LOG2_E = 1.4426950408889634
 
 
 def short_layout(offset, short_pages, short_fill):
@@ -45,6 +46,7 @@
     b = b_ref[0]
     per_tile = tk // chunk_rows
     scale = HEAD_SIZE ** (-0.5)
+    log2_scale = scale * LOG2_E
 
     @pl.when(t == 0)
     def _init():
@@ -71,13 +73,13 @@
             qg = q_ref[:, g * HEAD_SIZE:(g + 1) * HEAD_SIZE]
             s = lax.dot_general(
                 qg, k, (((1,), (1,)), ((), ())), preferred_element_type=jnp.float32
-            ) * scale
+            )
             if masked:
                 s = jnp.where(allowed, s, NEGATIVE_FILL)
             m_prev = m_out[g]
-            m_new = jnp.maximum(m_prev, jnp.max(s, axis=1, keepdims=True))
-            p = jnp.exp(s - m_new[:, :1])
-            alpha = jnp.exp(m_prev - m_new)
+            m_new = jnp.maximum(m_prev, jnp.max(s, axis=1, keepdims=True) * scale)
+            p = jnp.exp2(s * log2_scale - m_new[:, :1] * LOG2_E)
+            alpha = jnp.exp2((m_prev - m_new) * LOG2_E)
             pv = lax.dot_general(
                 p.astype(jnp.bfloat16), v_ext, (((1,), (0,)), ((), ())),
                 preferred_element_type=jnp.float32,
@@ -269,12 +271,25 @@
         short_fill,
     )
     attended = jnp.concatenate([att_long, att_short])
-    mixed_out = lax.psum_scatter(
-        jnp.dot(attended, out_weight, preferred_element_type=jnp.float32).astype(jnp.bfloat16),
-        "tp",
-        scatter_dimension=0,
-        tiled=True,
-    )
+    tp_count = lax.axis_size("tp")
+    if tp_count == 2:
+        tp_index = lax.axis_index("tp")
+        half_rows = tok_rows // 2
+        theirs = lax.dynamic_slice_in_dim(attended, (1 - tp_index) * half_rows, half_rows, 0)
+        sent = jnp.dot(theirs, out_weight, preferred_element_type=jnp.float32).astype(jnp.bfloat16)
+        received = lax.ppermute(sent, "tp", [(0, 1), (1, 0)])
+        mine = lax.dynamic_slice_in_dim(attended, tp_index * half_rows, half_rows, 0)
+        own = jnp.dot(mine, out_weight, preferred_element_type=jnp.float32).astype(jnp.bfloat16)
+        first_group = jnp.where(tp_index == 0, own, received).astype(jnp.float32)
+        second_group = jnp.where(tp_index == 0, received, own).astype(jnp.float32)
+        mixed_out = (first_group + second_group).astype(jnp.bfloat16)
+    else:
+        mixed_out = lax.psum_scatter(
+            jnp.dot(attended, out_weight, preferred_element_type=jnp.float32).astype(jnp.bfloat16),
+            "tp",
+            scatter_dimension=0,
+            tiled=True,
+        )
     written_cache = jnp.einsum(
         "sct,xscr->xtr", routing, incoming, preferred_element_type=jnp.float32
     ).astype(jnp.bfloat16)

time: 398 us -> 395 us (level)
  matrix products: 32.5 us -> 44.5 us
  Pallas kernels: 160 us -> 152 us
  waiting for transfers between devices: 159 us -> 153 us
    reduce_scatter x1 -> x0, waiting for transfers between devices: 15 us -> none  [local(): lax.psum_scatter(jnp.dot(attended, out_weight, preferred_element_type=jnp...]
    dot_general x1 -> x2, matrix products: 27.9 us -> 39.8 us  [the longest x1 20.9 us: local(): jnp.dot(mine, out_weight, preferred_element_type=jnp.float32)]
    pallas_call x2, Pallas kernels: 160 us -> 152 us  [long_attention_chunk(): pl.pallas_call(kernel, grid_spec=grid_spec, out_shape=out_shape, input_ou...]
    all_gather x2, waiting for transfers between devices: 87.8 us -> 92.9 us  [long_attention(): kv = lax.all_gather(kv, 'req', axis=0, tiled=True)]
  transfers between devices with their start and end apart: 6 -> 6, of which waited for: 5 -> 5; matrix products, arithmetic and copies ran while one was open for 5% -> 5% of each run, Pallas kernels for 20% -> 19%
where the time goes in v8:
time: 395 us; the launch traced here: 394 us
  waiting for transfers between devices  153 us (39%)
  Pallas kernels  152 us (38%)
  matrix products  44.5 us (11%)
  between operations  14.4 us (4%)
  local copies, waits for them, and re-layouts  13.7 us (3%)
  starting transfers between devices  12.2 us (3%)
    pallas_call x2, Pallas kernels, long_attention_chunk(): pl.pallas_call(kernel, grid_spec=grid_spec, out_shape=out_shape, input_ou...  152 us
    all_gather x2, waiting for transfers between devices, long_attention(): kv = lax.all_gather(kv, 'req', axis=0, tiled=True)  92.9 us
    all_to_all x1, waiting for transfers between devices, local(): lax.all_to_all(outgoing, 'req', split_axis=1, concat_axis=1, tiled=True)  50 us
    dot_general x1, matrix products, local(): jnp.dot(mine, out_weight, preferred_element_type=jnp.float32)  20.9 us
    dot_general x1, matrix products, local(): jnp.dot(theirs, out_weight, preferred_element_type=jnp.float32)  18.9 us
  transfers between devices with their start and end apart: 6, of which 5 were waited for; matrix products, arithmetic and copies ran while one was open for 5% of the time, Pallas kernels for 19%

profile of v8, /device:TPU:29, one launch (start us, length us, event | category | flops | bytes accessed | tf_op | source)
XLA Modules:
  0.0 394.0 jit_solution(16124979783536866209)
XLA Ops:
  7.2 1.1 fusion.38
  8.3 1.1 fusion.39
  9.4 0.9 pad_maximum_fusion.1
  10.4 0.9 pad_maximum_fusion
  11.3 0.3 stack.10
  11.6 0.3 stack.9
  12.0 0.1 copy.24
  12.1 0.1 reduce-window.8
  12.2 0.1 reduce
  12.3 0.1 rem.82
  12.4 0.1 div.59
  12.5 0.1 ne.107
  12.6 0.1 convert_reduce_fusion.2
  12.7 0.1 select_reduce_fusion.2
  12.8 0.1 broadcast_in_dim.123
  12.9 0.2 broadcast_in_dim.124
  13.1 0.2 copy.44
  13.3 0.5 convert_reduce_fusion
  13.8 0.7 fusion.1
  14.5 2.8 copy.25
  17.3 6.6 %all-to-all-start = ((bf16[2,16,3,8192]{3,0,2,1:T(2,128)(2,1)}), bf16[2,16,3,8192]{3,0,2,1:T(2,128)(2,1)}, u32[]{:S(2)}, u32[]{:S(2)}) async-start(bf16[2,16,3,8192]{3,0,2,1:T(2,128)(2,1)} %bitcast.53), calls=%async_computation | async-start | bytes 3145728 | tf_op jit(solution)/shard_map/all_to_all | solution.py:246
  24.0 0.1 copy.43
  24.1 3.1 collective-permute-start.1
  27.2 0.9 slice.35
  28.1 2.1 collective-permute-start
  30.2 0.1 convert_reduce_fusion.1
  30.3 0.1 select_reduce_fusion
  30.5 0.2 and_and_fusion
  30.6 6.5 %collective-permute-done = bf16[128,512]{1,0:T(8,128)(2,1)S(1)} collective-permute-done((bf16[128,512]{1,0:T(8,128)(2,1)S(1)}, bf16[128,512]{1,0:T(8,128)(2,1)S(1)}, u32[]{:S(2)}, u32[]{:S(2)}) %collective-permute-start) | collective-permute-done | bytes 131104 | tf_op jit(solution)/shard_map/ppermute | solution.py:181
  37.2 0.1 copy.26
  37.4 50.0 %all-to-all-done = bf16[2,16,3,8192]{3,0,2,1:T(2,128)(2,1)} async-done(((bf16[2,16,3,8192]{3,0,2,1:T(2,128)(2,1)}), bf16[2,16,3,8192]{3,0,2,1:T(2,128)(2,1)}, u32[]{:S(2)}, u32[]{:S(2)}) %all-to-all-start) | async-done | bytes 1572896 | tf_op jit(solution)/shard_map/all_to_all | solution.py:246
  87.4 2.6 copy.28
  90.0 1.5 slice.30.q_ref
  91.5 0.5 fusion.40
  92.0 0.3 fusion.2
  92.3 0.5 fusion.14
  92.9 0.2 copy.42
  93.1 55.2 %all-gather.5.cloned.1.call-done.k_ref.v_ref = bf16[4096,1024]{1,0:T(8,128)(2,1)} async-done(((bf16[256,1024]{1,0:T(8,128)(2,1)}), bf16[4096,1024]{1,0:T(8,128)(2,1)}) %all-gather.5.cloned.1.call-update) | async-done | bytes 8388624 | tf_op jit(solution)/shard_map/all_gather | solution.py:169
  148.3 76.1 %shard_map.86 = (f32[4,4,512,128]{3,2,1,0:T(8,128)}, f32[4,4,512,128]{3,2,1,0:T(8,128)}, f32[4,4,512,128]{3,2,1,0:T(8,128)}) custom-call(s32[1]{0:T(128)} %bitcast.b_ref, bf16[512,2048]{1,0:T(8,128)(2,1)} %slice.30.q_ref, bf16[4096,1024]{1,0:T(8,128)(2,1)} %all-gather.5.cloned.1.call-done.k_ref.v_ref, bf16[4096,1024]{1,0:T(8,128)(2,1)} %all-gather.5.cloned.1.call-done.k_ref.v_ref), custom_call_target="tpu_custom_call" | custom-call | tf_op jit(solution)/shard_map/pallas_call | solution.py:149
  224.4 37.7 %all-gather.3.cloned.1.call-done.k_ref.v_ref = bf16[4096,1024]{1,0:T(8,128)(2,1)} async-done(((bf16[256,1024]{1,0:T(8,128)(2,1)}), bf16[4096,1024]{1,0:T(8,128)(2,1)}) %all-gather.3.cloned.1.call-update) | async-done | bytes 8388624 | tf_op jit(solution)/shard_map/all_gather | solution.py:169
  262.1 76.3 %shard_map.87 = bf16[512,2048]{1,0:T(8,128)(2,1)} custom-call(s32[1]{0:T(128)} %bitcast.b_ref, bf16[512,2048]{1,0:T(8,128)(2,1)} %slice.30.q_ref, bf16[4096,1024]{1,0:T(8,128)(2,1)} %all-gather.3.cloned.1.call-done.k_ref.v_ref, bf16[4096,1024]{1,0:T(8,128)(2,1)} %all-gather.3.cloned.1.call-done.k_ref.v_ref, f32[4,4,512,128]{3,2,1,0:T(8,128)} %get-tuple-element.8.refs_0_, ...), custom_call_target="tpu_custom_call" | custom-call | tf_op jit(solution)/shard_map/pallas_call | solution.py:149
  338.4 18.9 %convolution_convert_fusion = bf16[320,8192]{1,0:T(8,128)(2,1)} fusion(bf16[2048,8192]{1,0:T(8,128)(2,1)} %param.10, s32[]{:T(128)S(6)} %select_n.109, bf16[512,2048]{1,0:T(8,128)(2,1)} %shard_map.87, bf16[128,2048]{1,0:T(8,128)(2,1)S(1)} %copy.42), kind=kOutput, calls=%fused_computation | convolution fusion | flops 10742661120 | bytes 41418756 | tf_op jit(solution)/shard_map/dot_general | solution.py:279
  357.3 0.3 collective-permute-start.2
  357.6 0.3 convolution_convert_fusion.3
  357.9 2.7 fusion
  360.6 1.7 copy.45
  362.3 4.0 %collective-permute-done.2 = bf16[320,8192]{1,0:T(8,128)(2,1)} collective-permute-done((bf16[320,8192]{1,0:T(8,128)(2,1)}, bf16[320,8192]{1,0:T(8,128)(2,1)}, u32[]{:S(2)}, u32[]{:S(2)}) %collective-permute-start.2) | collective-permute-done | bytes 5242912 | tf_op jit(solution)/shard_map/ppermute | solution.py:280
  366.3 20.9 %add_convert_fusion = bf16[320,8192]{1,0:T(8,128)(2,1)} fusion(bf16[320,8192]{1,0:T(8,128)(2,1)} %collective-permute-done.2, bf16[2048,8192]{1,0:T(8,128)(2,1)} %param.10, pred[]{:T(512)S(6)} %eq.58, s32[]{:T(128)S(6)} %select_n.108, bf16[512,2048]{1,0:T(8,128)(2,1)S(1)} %copy-done.3, bf16[128,2048]{1,0:T(8,128)(2,1)S(1)} %copy.42), kind=kOutput, calls=%fused_computation.2 | convolution fusion | flops 10758389760 | bytes 46661636 | tf_op jit(solution)/shard_map/dot_general | solution.py:282
  (39 shorter events, 0.3 us)
Async XLA Ops:
  7.2 141.1 %all-gather.5.cloned.1.call-start = ((), (), s32[]{:S(2)}) async-start(), calls=%async_computation.2 | async-start | bytes 8912896 | tf_op jit(solution)/shard_map/all_gather | solution.py:169
  8.3 3.0 copy-start.2
  9.4 2.2 copy-start.1
  10.3 251.8 %all-gather.3.cloned.1.call-start = ((), (), s32[]{:S(2)}) async-start(), calls=%async_computation.1 | async-start | bytes 8912896 | tf_op jit(solution)/shard_map/all_gather | solution.py:169
  10.4 1.6 copy-start.5
  10.4 1.9 copy-start.4
  10.4 2.3 copy-start.6
  17.3 6.7 %slice-start.1 = ((bf16[640,512]{1,0:T(8,128)(2,1)}), bf16[128,512]{1,0:T(8,128)(2,1)S(1)}, s32[]{:S(2)}) async-start(bf16[640,512]{1,0:T(8,128)(2,1)} %param.8), calls=%async_computation.4 | async-start | bytes 262144 | tf_op jit(solution)/shard_map/slice | solution.py:268
  17.3 70.1 %copy-start = (bf16[640,2048]{1,0:T(8,128)(2,1)S(1)}, bf16[640,2048]{1,0:T(8,128)(2,1)}, u32[]{:S(2)}) copy-start(bf16[640,2048]{1,0:T(8,128)(2,1)} %param.7) | copy-start | bytes 7864324
  17.3 70.1 %all-to-all-start = ((bf16[2,16,3,8192]{3,0,2,1:T(2,128)(2,1)}), bf16[2,16,3,8192]{3,0,2,1:T(2,128)(2,1)}, u32[]{:S(2)}, u32[]{:S(2)}) async-start(bf16[2,16,3,8192]{3,0,2,1:T(2,128)(2,1)} %bitcast.53), calls=%async_computation | async-start | bytes 3145728 | tf_op jit(solution)/shard_map/all_to_all | solution.py:246
  24.1 13.3 %collective-permute-start.1 = (bf16[128,512]{0,1:T(8,128)(2,1)S(1)}, bf16[128,512]{0,1:T(8,128)(2,1)S(1)}, u32[]{:S(2)}, u32[]{:S(2)}) collective-permute-start(bf16[128,512]{0,1:T(8,128)(2,1)S(1)} %copy.43), channel_id=1, source_target_pairs={{0,2},{2,4},{4,6},{6,8},{8,10},{10,12},{12,14},{14,16},{16,18},{18... | collective-permute-start | bytes 393224 | tf_op jit(solution)/shard_map/ppermute | solution.py:180
  28.1 9.1 %collective-permute-start = (bf16[128,512]{1,0:T(8,128)(2,1)S(1)}, bf16[128,512]{1,0:T(8,128)(2,1)S(1)}, u32[]{:S(2)}, u32[]{:S(2)}) collective-permute-start(bf16[128,512]{1,0:T(8,128)(2,1)S(1)} %slice.35), channel_id=1, source_target_pairs={{0,2},{2,4},{4,6},{6,8},{8,10},{10,12},{12,14},{14,16},{16,18},{18... | collective-permute-start | bytes 393224 | tf_op jit(solution)/shard_map/ppermute | solution.py:181
  90.0 1.5 slice-start
  357.3 9.0 %collective-permute-start.2 = (bf16[320,8192]{1,0:T(8,128)(2,1)}, bf16[320,8192]{1,0:T(8,128)(2,1)}, u32[]{:S(2)}, u32[]{:S(2)}) collective-permute-start(bf16[320,8192]{1,0:T(8,128)(2,1)} %convolution_convert_fusion), channel_id=1, source_target_pairs={{0,1},{1,0},{2,3},{3,2},{4,5},{5,4},{6,7},{7,6},{8,9},{9,8},{10,11... | collective-permute-start | bytes 15728648 | tf_op jit(solution)/shard_map/ppermute | solution.py:280
  360.6 5.7 %copy-start.3 = (bf16[512,2048]{1,0:T(8,128)(2,1)S(1)}, bf16[512,2048]{1,0:T(8,128)(2,1)}, u32[]{:S(2)}) copy-start(bf16[512,2048]{1,0:T(8,128)(2,1)} %shard_map.87) | copy-start | bytes 6291460
Sparse Core Ops, SparseCore 0:
  10.8 137.4 all-gather.4
  151.1 111.0 all-gather.2

commit v9 on v8

--- a/solution.py
+++ b/solution.py
@@ -12,7 +12,7 @@
 SHORT_DEV = 128
 PAGE_ROWS = 16
 BLOCK_TOKENS = 640
-LONG_CHUNKS = 2
+LONG_CHUNK_ROWS = (320, 192)
 
 
 NEGATIVE_FILL = -1e30
@@ -32,7 +32,7 @@
     return (prompt, offset - begin_at, offset < limit_at)
 
 
-def flash_kernel(b_ref, q_ref, k_ref, v_ref, *refs, group, tq, tk, chunk_rows, chunk, first, last):
+def flash_kernel(b_ref, q_ref, k_ref, v_ref, *refs, group, tq, tk, chunk_rows, chunk_start, first, last):
     if first:
         m_out, l_out, acc_out = refs[-3:]
         m_in, l_in, acc_in = m_out, l_out, acc_out
@@ -67,7 +67,7 @@
             rows = i * tq + lax.broadcasted_iota(jnp.int32, (tq, tk), 0)
             cols = lax.broadcasted_iota(jnp.int32, (tq, tk), 1)
             src = t * per_tile + cols // chunk_rows
-            key_pos = chunk * chunk_rows + cols % chunk_rows
+            key_pos = chunk_start + cols % chunk_rows
             allowed = (src < b) | ((src == b) & (key_pos <= rows))
         for g in range(group):
             qg = q_ref[:, g * HEAD_SIZE:(g + 1) * HEAD_SIZE]
@@ -105,18 +105,17 @@
                 ).astype(o_ref.dtype)
 
 
-def long_attention_chunk(b_arr, q_long, kv_chunk, state, chunk, first, last):
+def long_attention_chunk(b_arr, q_long, kv_chunk, state, chunk_rows, chunk_start, first, last):
     rows, q_cols = q_long.shape
     kv_cols = kv_chunk.shape[1] // 2
     heads_kv = kv_cols // HEAD_SIZE
     group = q_cols // kv_cols
-    chunk_rows = LONG_DEV // LONG_CHUNKS
     total = kv_chunk.shape[0]
-    tk = min(512, total)
+    tk = chunk_rows * max(1, LONG_DEV // chunk_rows)
     per_tile = tk // chunk_rows
     tq = LONG_DEV
     kernel = functools.partial(
-        flash_kernel, group=group, tq=tq, tk=tk, chunk_rows=chunk_rows, chunk=chunk,
+        flash_kernel, group=group, tq=tq, tk=tk, chunk_rows=chunk_rows, chunk_start=chunk_start,
         first=first, last=last,
     )
     state_shape = jax.ShapeDtypeStruct((heads_kv, group, rows, HEAD_SIZE), jnp.float32)
@@ -159,17 +158,17 @@
 
 def long_attention(my_index, q_long, k_long, v_long):
     b_arr = jnp.reshape(my_index, (1,)).astype(jnp.int32)
-    chunk_rows = LONG_DEV // LONG_CHUNKS
     state = None
-    for c in range(LONG_CHUNKS):
+    start = 0
+    for c, rows in enumerate(LONG_CHUNK_ROWS):
         kv = jnp.concatenate(
-            [k_long[c * chunk_rows:(c + 1) * chunk_rows], v_long[c * chunk_rows:(c + 1) * chunk_rows]],
-            axis=1,
+            [k_long[start:start + rows], v_long[start:start + rows]], axis=1
         )
         kv = lax.all_gather(kv, "req", axis=0, tiled=True)
         state = long_attention_chunk(
-            b_arr, q_long, kv, state, c, c == 0, c == LONG_CHUNKS - 1
+            b_arr, q_long, kv, state, rows, start, c == 0, c == len(LONG_CHUNK_ROWS) - 1
         )
+        start += rows
     return state
 
 

time: 395 us -> 449 us (1.14)
  Pallas kernels: 152 us -> 216 us
  waiting for transfers between devices: 153 us -> 140 us
    pallas_call x2, Pallas kernels: 152 us -> 216 us  [long_attention_chunk(): pl.pallas_call(kernel, grid_spec=grid_spec, out_shape=out_shape, input_ou...]
    all_gather x2, waiting for transfers between devices: 92.9 us -> 80.1 us  [long_attention(): kv = lax.all_gather(kv, 'req', axis=0, tiled=True)]
  transfers between devices with their start and end apart: 6 -> 6, of which waited for: 5 -> 4; matrix products, arithmetic and copies ran while one was open for 5% -> 4% of each run, Pallas kernels for 19% -> 34%
where the time goes in v9:
time: 449 us; the launch traced here: 444 us
  Pallas kernels  216 us (48%)
  waiting for transfers between devices  140 us (31%)
  matrix products  44.5 us (10%)
  between operations  14.4 us (3%)
  local copies, waits for them, and re-layouts  13.6 us (3%)
  starting transfers between devices  12.2 us (3%)
    pallas_call x2, Pallas kernels, long_attention_chunk(): pl.pallas_call(kernel, grid_spec=grid_spec, out_shape=out_shape, input_ou...  216 us
    all_gather x2, waiting for transfers between devices, long_attention(): kv = lax.all_gather(kv, 'req', axis=0, tiled=True)  80.1 us
    all_to_all x1, waiting for transfers between devices, local(): lax.all_to_all(outgoing, 'req', split_axis=1, concat_axis=1, tiled=True)  47.2 us
    dot_general x1, matrix products, local(): jnp.dot(mine, out_weight, preferred_element_type=jnp.float32)  20.9 us
    dot_general x1, matrix products, local(): jnp.dot(theirs, out_weight, preferred_element_type=jnp.float32)  18.9 us
  transfers between devices with their start and end apart: 6, of which 4 were waited for; matrix products, arithmetic and copies ran while one was open for 4% of the time, Pallas kernels for 34%

profile of v9, /device:TPU:29, one launch (start us, length us, event | category | flops | bytes accessed | tf_op | source)
XLA Modules:
  0.0 444.5 jit_solution(7590739550418811626)
XLA Ops:
  7.2 1.1 slice.33
  8.3 1.0 slice.34
  9.3 1.0 pad_maximum_fusion
  10.3 0.0 all-gather.3.cloned.1.call-start
  10.4 0.8 pad_maximum_fusion.1
  11.3 0.3 stack.10
  11.6 0.3 stack.9
  11.9 0.1 copy.24
  12.0 0.1 reduce-window.8
  12.1 0.1 reduce
  12.2 0.1 rem.82
  12.3 0.1 div.59
  12.4 0.1 ne.107
  12.5 0.1 convert_reduce_fusion.2
  12.6 0.1 select_reduce_fusion.2
  12.8 0.1 broadcast_in_dim.123
  12.9 0.2 broadcast_in_dim.124
  13.0 0.2 copy.44
  13.3 0.5 convert_reduce_fusion
  13.8 0.7 fusion.1
  14.5 2.8 copy.25
  17.2 6.6 %all-to-all-start = ((bf16[2,16,3,8192]{3,0,2,1:T(2,128)(2,1)}), bf16[2,16,3,8192]{3,0,2,1:T(2,128)(2,1)}, u32[]{:S(2)}, u32[]{:S(2)}) async-start(bf16[2,16,3,8192]{3,0,2,1:T(2,128)(2,1)} %bitcast.53), calls=%async_computation | async-start | bytes 3145728 | tf_op jit(solution)/shard_map/all_to_all | solution.py:245
  23.9 0.1 copy.43
  24.0 3.1 collective-permute-start.1
  27.1 0.9 slice.35
  28.0 2.1 collective-permute-start
  30.2 0.1 convert_reduce_fusion.1
  30.3 0.1 select_reduce_fusion
  30.4 0.2 and_and_fusion
  30.6 8.7 %collective-permute-done = bf16[128,512]{1,0:T(8,128)(2,1)S(1)} collective-permute-done((bf16[128,512]{1,0:T(8,128)(2,1)S(1)}, bf16[128,512]{1,0:T(8,128)(2,1)S(1)}, u32[]{:S(2)}, u32[]{:S(2)}) %collective-permute-start) | collective-permute-done | bytes 131104 | tf_op jit(solution)/shard_map/ppermute | solution.py:180
  39.3 0.1 copy.26
  39.5 47.2 %all-to-all-done = bf16[2,16,3,8192]{3,0,2,1:T(2,128)(2,1)} async-done(((bf16[2,16,3,8192]{3,0,2,1:T(2,128)(2,1)}), bf16[2,16,3,8192]{3,0,2,1:T(2,128)(2,1)}, u32[]{:S(2)}, u32[]{:S(2)}) %all-to-all-start) | async-done | bytes 1572896 | tf_op jit(solution)/shard_map/all_to_all | solution.py:245
  86.7 2.6 copy.28
  89.3 1.5 slice.30.q_ref
  90.8 0.5 fusion.38
  91.3 0.3 fusion.2
  91.6 0.5 fusion.14
  92.2 0.2 copy.42
  92.4 80.1 %all-gather.5.cloned.1.call-done.k_ref.v_ref = bf16[5120,1024]{1,0:T(8,128)(2,1)} async-done(((bf16[320,1024]{1,0:T(8,128)(2,1)}), bf16[5120,1024]{1,0:T(8,128)(2,1)}) %all-gather.5.cloned.1.call-update) | async-done | bytes 10485776 | tf_op jit(solution)/shard_map/all_gather | solution.py:167
  172.5 150.6 %shard_map.86 = (f32[4,4,512,128]{3,2,1,0:T(8,128)}, f32[4,4,512,128]{3,2,1,0:T(8,128)}, f32[4,4,512,128]{3,2,1,0:T(8,128)}) custom-call(s32[1]{0:T(128)} %bitcast.b_ref, bf16[512,2048]{1,0:T(8,128)(2,1)} %slice.30.q_ref, bf16[5120,1024]{1,0:T(8,128)(2,1)} %all-gather.5.cloned.1.call-done.k_ref.v_ref, bf16[5120,1024]{1,0:T(8,128)(2,1)} %all-gather.5.cloned.1.call-done.k_ref.v_ref), custom_call_target="tpu_custom_call" | custom-call | tf_op jit(solution)/shard_map/pallas_call | solution.py:148
  323.1 65.8 %shard_map.87 = bf16[512,2048]{1,0:T(8,128)(2,1)} custom-call(s32[1]{0:T(128)} %bitcast.b_ref, bf16[512,2048]{1,0:T(8,128)(2,1)} %slice.30.q_ref, bf16[3072,1024]{1,0:T(8,128)(2,1)} %all-gather.3.cloned.1.call-done.k_ref.v_ref, bf16[3072,1024]{1,0:T(8,128)(2,1)} %all-gather.3.cloned.1.call-done.k_ref.v_ref, f32[4,4,512,128]{3,2,1,0:T(8,128)} %get-tuple-element.8.refs_0_, ...), custom_call_target="tpu_custom_call" | custom-call | tf_op jit(solution)/shard_map/pallas_call | solution.py:148
  388.9 18.9 %convolution_convert_fusion = bf16[320,8192]{1,0:T(8,128)(2,1)} fusion(bf16[2048,8192]{1,0:T(8,128)(2,1)} %param.10, s32[]{:T(128)S(6)} %select_n.109, bf16[512,2048]{1,0:T(8,128)(2,1)} %shard_map.87, bf16[128,2048]{1,0:T(8,128)(2,1)S(1)} %copy.42), kind=kOutput, calls=%fused_computation | convolution fusion | flops 10742661120 | bytes 41418756 | tf_op jit(solution)/shard_map/dot_general | solution.py:278
  407.8 0.3 collective-permute-start.2
  408.1 0.3 convolution_convert_fusion.3
  408.3 2.7 fusion
  411.0 1.7 copy.45
  412.8 4.0 collective-permute-done.2
  416.8 20.9 %add_convert_fusion = bf16[320,8192]{1,0:T(8,128)(2,1)} fusion(bf16[320,8192]{1,0:T(8,128)(2,1)} %collective-permute-done.2, bf16[2048,8192]{1,0:T(8,128)(2,1)} %param.10, pred[]{:T(512)S(6)} %eq.58, s32[]{:T(128)S(6)} %select_n.108, bf16[512,2048]{1,0:T(8,128)(2,1)S(1)} %copy-done.3, bf16[128,2048]{1,0:T(8,128)(2,1)S(1)} %copy.42), kind=kOutput, calls=%fused_computation.2 | convolution fusion | flops 10758389760 | bytes 46661636 | tf_op jit(solution)/shard_map/dot_general | solution.py:281
  (43 shorter events, 0.3 us)
Async XLA Ops:
  7.2 3.2 slice-start.1
  7.2 3.2 slice-start.3
  7.2 165.3 %all-gather.5.cloned.1.call-start = ((), (), s32[]{:S(2)}) async-start(), calls=%async_computation.2 | async-start | bytes 11141120 | tf_op jit(solution)/shard_map/all_gather | solution.py:167
  9.3 1.9 copy-start.2
  10.3 1.3 copy-start.1
  10.3 312.8 %all-gather.3.cloned.1.call-start = ((), (), s32[]{:S(2)}) async-start(), calls=%async_computation.1 | async-start | bytes 6684672 | tf_op jit(solution)/shard_map/all_gather | solution.py:167
  10.4 1.5 copy-start.5
  10.4 1.8 copy-start.4
  10.4 2.2 copy-start.6
  17.2 6.7 %slice-start.2 = ((bf16[640,512]{1,0:T(8,128)(2,1)}), bf16[128,512]{1,0:T(8,128)(2,1)S(1)}, s32[]{:S(2)}) async-start(bf16[640,512]{1,0:T(8,128)(2,1)} %param.8), calls=%async_computation.5 | async-start | bytes 262144 | tf_op jit(solution)/shard_map/slice | solution.py:267
  17.2 69.5 %copy-start = (bf16[640,2048]{1,0:T(8,128)(2,1)S(1)}, bf16[640,2048]{1,0:T(8,128)(2,1)}, u32[]{:S(2)}) copy-start(bf16[640,2048]{1,0:T(8,128)(2,1)} %param.7) | copy-start | bytes 7864324
  17.2 69.5 %all-to-all-start = ((bf16[2,16,3,8192]{3,0,2,1:T(2,128)(2,1)}), bf16[2,16,3,8192]{3,0,2,1:T(2,128)(2,1)}, u32[]{:S(2)}, u32[]{:S(2)}) async-start(bf16[2,16,3,8192]{3,0,2,1:T(2,128)(2,1)} %bitcast.53), calls=%async_computation | async-start | bytes 3145728 | tf_op jit(solution)/shard_map/all_to_all | solution.py:245
  24.0 15.5 %collective-permute-start.1 = (bf16[128,512]{0,1:T(8,128)(2,1)S(1)}, bf16[128,512]{0,1:T(8,128)(2,1)S(1)}, u32[]{:S(2)}, u32[]{:S(2)}) collective-permute-start(bf16[128,512]{0,1:T(8,128)(2,1)S(1)} %copy.43), channel_id=1, source_target_pairs={{0,2},{2,4},{4,6},{6,8},{8,10},{10,12},{12,14},{14,16},{16,18},{18... | collective-permute-start | bytes 393224 | tf_op jit(solution)/shard_map/ppermute | solution.py:179
  28.0 11.3 %collective-permute-start = (bf16[128,512]{1,0:T(8,128)(2,1)S(1)}, bf16[128,512]{1,0:T(8,128)(2,1)S(1)}, u32[]{:S(2)}, u32[]{:S(2)}) collective-permute-start(bf16[128,512]{1,0:T(8,128)(2,1)S(1)} %slice.35), channel_id=1, source_target_pairs={{0,2},{2,4},{4,6},{6,8},{8,10},{10,12},{12,14},{14,16},{16,18},{18... | collective-permute-start | bytes 393224 | tf_op jit(solution)/shard_map/ppermute | solution.py:180
  89.3 1.5 slice-start
  407.8 9.0 %collective-permute-start.2 = (bf16[320,8192]{1,0:T(8,128)(2,1)}, bf16[320,8192]{1,0:T(8,128)(2,1)}, u32[]{:S(2)}, u32[]{:S(2)}) collective-permute-start(bf16[320,8192]{1,0:T(8,128)(2,1)} %convolution_convert_fusion), channel_id=1, source_target_pairs={{0,1},{1,0},{2,3},{3,2},{4,5},{5,4},{6,7},{7,6},{8,9},{9,8},{10,11... | collective-permute-start | bytes 15728648 | tf_op jit(solution)/shard_map/ppermute | solution.py:279
  411.0 5.8 %copy-start.3 = (bf16[512,2048]{1,0:T(8,128)(2,1)S(1)}, bf16[512,2048]{1,0:T(8,128)(2,1)}, u32[]{:S(2)}) copy-start(bf16[512,2048]{1,0:T(8,128)(2,1)} %shard_map.87) | copy-start | bytes 6291460
Sparse Core Ops, SparseCore 0:
  10.7 161.7 all-gather.4
  175.2 92.7 all-gather.2

commit v10 on v8

--- a/solution.py
+++ b/solution.py
@@ -157,7 +157,7 @@
     )(*operands)
 
 
-def long_attention(my_index, q_long, k_long, v_long):
+def long_attention(my_index, q_long, k_long, v_long, outgoing):
     b_arr = jnp.reshape(my_index, (1,)).astype(jnp.int32)
     chunk_rows = LONG_DEV // LONG_CHUNKS
     state = None
@@ -167,10 +167,13 @@
             axis=1,
         )
         kv = lax.all_gather(kv, "req", axis=0, tiled=True)
+        if c == LONG_CHUNKS - 1:
+            outgoing, kv, state = lax.optimization_barrier((outgoing, kv, state))
+            incoming = lax.all_to_all(outgoing, "req", split_axis=1, concat_axis=1, tiled=True)
         state = long_attention_chunk(
             b_arr, q_long, kv, state, c, c == 0, c == LONG_CHUNKS - 1
         )
-    return state
+    return state, incoming
 
 
 def short_attention(my_index, req_count, q_short, k_short, v_short, short_pages, short_fill):
@@ -243,7 +246,6 @@
         "ks,xkr->xsr", send_map, kv_pages, preferred_element_type=jnp.float32
     ).astype(jnp.bfloat16)
     outgoing = outgoing.reshape(2, req_count, capacity, PAGE_ROWS * width)
-    incoming = lax.all_to_all(outgoing, "req", split_axis=1, concat_axis=1, tiled=True)
     mine_mask = owners == my_index
     placing = mine_mask[:, :, None] & (
         order_in[:, :, None] == jnp.arange(capacity, dtype=jnp.int32)[None, None, :]
@@ -257,9 +259,9 @@
         target.astype(jnp.bfloat16),
         preferred_element_type=jnp.float32,
     ).astype(jnp.bfloat16)
-    incoming, queries = lax.optimization_barrier((incoming, queries))
-    att_long = long_attention(
-        my_index, queries[:LONG_DEV], rotated_key_rows[:LONG_DEV], stream_value_rows[:LONG_DEV]
+    att_long, incoming = long_attention(
+        my_index, queries[:LONG_DEV], rotated_key_rows[:LONG_DEV], stream_value_rows[:LONG_DEV],
+        outgoing,
     )
     att_short = short_attention(
         my_index,

time: 395 us -> 407 us (1.030)
  waiting for transfers between devices: 153 us -> 161 us
    all_gather x2, waiting for transfers between devices: 92.9 us -> 126 us  [long_attention(): kv = lax.all_gather(kv, 'req', axis=0, tiled=True)]
    all_to_all x1, waiting for transfers between devices: 50 us -> 35.6 us  [long_attention(): lax.all_to_all(outgoing, 'req', split_axis=1, concat_axis=1, tiled=True)]
    ppermute x1, waiting for transfers between devices: 6.54 us -> 0.01 us  [short_attention(): v_prev = lax.ppermute(v_short, 'req', perm)]
  transfers between devices with their start and end apart: 6 -> 6, of which waited for: 5 -> 3; matrix products, arithmetic and copies ran while one was open for 5% -> 5% of each run, Pallas kernels for 19% -> 19%
where the time goes in v10:
time: 407 us; the launch traced here: 404 us
  waiting for transfers between devices  161 us (40%)
  Pallas kernels  152 us (37%)
  matrix products  45.6 us (11%)
  between operations  14.4 us (4%)
  local copies, waits for them, and re-layouts  13.9 us (3%)
  starting transfers between devices  10.9 us (3%)
  other arithmetic  5.74 us (1%)
    pallas_call x2, Pallas kernels, long_attention_chunk(): pl.pallas_call(kernel, grid_spec=grid_spec, out_shape=out_shape, input_ou...  152 us
    all_gather x2, waiting for transfers between devices, long_attention(): kv = lax.all_gather(kv, 'req', axis=0, tiled=True)  126 us
    all_to_all x1, waiting for transfers between devices, long_attention(): lax.all_to_all(outgoing, 'req', split_axis=1, concat_axis=1, tiled=True)  35.6 us
    dot_general x1, matrix products, local(): jnp.dot(mine, out_weight, preferred_element_type=jnp.float32)  20.9 us
    dot_general x1, matrix products, local(): jnp.dot(theirs, out_weight, preferred_element_type=jnp.float32)  18.9 us
  transfers between devices with their start and end apart: 6, of which 3 were waited for; matrix products, arithmetic and copies ran while one was open for 5% of the time, Pallas kernels for 19%

profile of v10, /device:TPU:29, one launch (start us, length us, event | category | flops | bytes accessed | tf_op | source)
XLA Modules:
  0.0 404.3 jit_solution(4186844091202598255)
XLA Ops:
  7.2 1.1 fusion.38
  8.3 1.1 fusion.39
  9.4 0.9 pad_maximum_fusion.1
  10.3 0.9 pad_maximum_fusion
  11.2 0.1 copy.66
  11.4 3.1 collective-permute-start.1
  14.5 1.9 collective-permute-start
  16.5 0.3 stack.10
  16.8 1.1 stack.9
  17.9 0.1 rem.82
  18.0 0.1 div.59
  18.1 0.1 ne.107
  18.2 0.1 copy.47
  18.4 0.1 reduce
  18.5 0.1 convert_reduce_fusion.2
  18.7 0.1 select_reduce_fusion.2
  18.8 0.4 copy-done.7
  19.2 0.1 broadcast_in_dim.123
  19.3 0.2 broadcast_in_dim.124
  19.5 0.9 copy.68
  20.4 0.5 broadcast_compare_fusion
  21.0 0.5 convert_reduce_fusion
  21.5 0.1 convert_reduce_fusion.1
  21.6 0.1 select_reduce_fusion
  21.8 3.2 fusion.1
  24.9 0.2 and_and_fusion
  25.1 1.5 slice.30.q_ref
  26.6 4.2 %copy.48 = bf16[2,48,8192]{2,0,1:T(2,128)(2,1)} copy(bf16[2,48,8192]{2,1,0:T(8,128)(2,1)} %fusion.1) | data formatting | bytes 3145728 | tf_op jit(solution)/shard_map/convert_element_type | solution.py:247
  30.9 0.3 copy.67
  31.1 0.9 pad_maximum_fusion.2
  32.1 0.1 copy.49
  32.2 0.9 pad_maximum_fusion.3
  33.2 0.5 fusion.40
  33.7 0.3 fusion.2
  34.0 0.5 fusion.14
  34.5 0.2 copy.65
  34.7 88.1 %all-gather.5.cloned.1.call-done.k_ref.v_ref = bf16[4096,1024]{1,0:T(8,128)(2,1)} async-done(((bf16[256,1024]{1,0:T(8,128)(2,1)}), bf16[4096,1024]{1,0:T(8,128)(2,1)}) %all-gather.5.cloned.1.call-update) | async-done | bytes 8388624 | tf_op jit(solution)/shard_map/all_gather | solution.py:169
  122.9 76.1 %shard_map.86 = (f32[4,4,512,128]{3,2,1,0:T(8,128)}, f32[4,4,512,128]{3,2,1,0:T(8,128)}, f32[4,4,512,128]{3,2,1,0:T(8,128)}) custom-call(s32[1]{0:T(128)} %bitcast.b_ref, bf16[512,2048]{1,0:T(8,128)(2,1)} %slice.30.q_ref, bf16[4096,1024]{1,0:T(8,128)(2,1)} %all-gather.5.cloned.1.call-done.k_ref.v_ref, bf16[4096,1024]{1,0:T(8,128)(2,1)} %all-gather.5.cloned.1.call-done.k_ref.v_ref), custom_call_target="tpu_custom_call" | custom-call | tf_op jit(solution)/shard_map/pallas_call | solution.py:149
  199.0 37.7 %all-gather.3.cloned.1.call-done.k_ref.v_ref = bf16[4096,1024]{1,0:T(8,128)(2,1)} async-done(((bf16[256,1024]{1,0:T(8,128)(2,1)}), bf16[4096,1024]{1,0:T(8,128)(2,1)}) %all-gather.3.cloned.1.call-update) | async-done | bytes 8388624 | tf_op jit(solution)/shard_map/all_gather | solution.py:169
  236.7 76.3 %shard_map.87 = bf16[512,2048]{1,0:T(8,128)(2,1)} custom-call(s32[1]{0:T(128)} %bitcast.b_ref, bf16[512,2048]{1,0:T(8,128)(2,1)} %slice.30.q_ref, bf16[4096,1024]{1,0:T(8,128)(2,1)} %all-gather.3.cloned.1.call-done.k_ref.v_ref, bf16[4096,1024]{1,0:T(8,128)(2,1)} %all-gather.3.cloned.1.call-done.k_ref.v_ref, f32[4,4,512,128]{3,2,1,0:T(8,128)} %get-tuple-element.14.refs_0_, ...), custom_call_target="tpu_custom_call" | custom-call | tf_op jit(solution)/shard_map/pallas_call | solution.py:149
  313.0 18.9 %convolution_convert_fusion = bf16[320,8192]{1,0:T(8,128)(2,1)} fusion(bf16[2048,8192]{1,0:T(8,128)(2,1)} %param.10, s32[]{:T(128)S(6)} %select_n.109, bf16[512,2048]{1,0:T(8,128)(2,1)} %shard_map.87, bf16[128,2048]{1,0:T(8,128)(2,1)S(1)} %copy.65), kind=kOutput, calls=%fused_computation | convolution fusion | flops 10742661120 | bytes 41418756 | tf_op jit(solution)/shard_map/dot_general | solution.py:281
  331.9 0.3 collective-permute-start.2
  332.2 5.5 %all-to-all-start = ((bf16[2,16,3,8192]{3,0,2,1:T(2,128)(2,1)}), bf16[2,16,3,8192]{3,0,2,1:T(2,128)(2,1)S(1)}, u32[]{:S(2)}, u32[]{:S(2)}) async-start(bf16[2,16,3,8192]{3,0,2,1:T(2,128)(2,1)} %bitcast.5), calls=%async_computation | async-start | bytes 3145728 | tf_op jit(solution)/shard_map/all_to_all | solution.py:172
  337.7 0.3 convolution_convert_fusion.3
  338.0 35.6 %all-to-all-done = bf16[2,16,3,8192]{3,0,2,1:T(2,128)(2,1)S(1)} async-done(((bf16[2,16,3,8192]{3,0,2,1:T(2,128)(2,1)}), bf16[2,16,3,8192]{3,0,2,1:T(2,128)(2,1)S(1)}, u32[]{:S(2)}, u32[]{:S(2)}) %all-to-all-start) | async-done | bytes 1572896 | tf_op jit(solution)/shard_map/all_to_all | solution.py:172
  373.5 1.3 fusion
  374.8 1.7 copy.69
  376.6 20.9 %add_convert_fusion = bf16[320,8192]{1,0:T(8,128)(2,1)} fusion(bf16[320,8192]{1,0:T(8,128)(2,1)} %collective-permute-done.2, bf16[2048,8192]{1,0:T(8,128)(2,1)} %param.10, pred[]{:T(512)S(6)} %eq.58, s32[]{:T(128)S(6)} %select_n.108, bf16[512,2048]{1,0:T(8,128)(2,1)S(1)} %copy-done.3, bf16[128,2048]{1,0:T(8,128)(2,1)S(1)} %copy.65), kind=kOutput, calls=%fused_computation.2 | convolution fusion | flops 10758389760 | bytes 46661636 | tf_op jit(solution)/shard_map/dot_general | solution.py:284
  (49 shorter events, 0.4 us)
Async XLA Ops:
  7.2 115.7 %all-gather.5.cloned.1.call-start = ((), (), s32[]{:S(2)}) async-start(), calls=%async_computation.2 | async-start | bytes 8912896 | tf_op jit(solution)/shard_map/all_gather | solution.py:169
  8.3 3.0 slice-start.1
  9.4 5.1 %copy-start.1 = (bf16[640,512]{1,0:T(8,128)(2,1)S(1)}, bf16[640,512]{1,0:T(8,128)(2,1)}, u32[]{:S(2)}) copy-start(bf16[640,512]{1,0:T(8,128)(2,1)} %param.9) | copy-start | bytes 1966084
  10.3 6.5 %copy-start.2 = (bf16[640,512]{1,0:T(8,128)(2,1)S(1)}, bf16[640,512]{1,0:T(8,128)(2,1)}, u32[]{:S(2)}) copy-start(bf16[640,512]{1,0:T(8,128)(2,1)} %param.8) | copy-start | bytes 1966084
  10.3 226.4 %all-gather.3.cloned.1.call-start = ((), (), s32[]{:S(2)}) async-start(), calls=%async_computation.1 | async-start | bytes 8912896 | tf_op jit(solution)/shard_map/all_gather | solution.py:169
  11.2 6.7 %copy-start.4 = (s32[640]{0:T(1024)S(1)}, s32[640]{0:T(1024)}, u32[]{:S(2)}) copy-start(s32[640]{0:T(1024)} %param.13) | copy-start | bytes 7684
  11.2 7.0 %copy-start.6 = (s32[51]{0:T(128)S(1)}, s32[51]{0:T(128)}, u32[]{:S(2)}) copy-start(s32[51]{0:T(128)} %param.11) | copy-start | bytes 616
  11.2 7.4 %copy-start.9 = (s32[51]{0:T(128)S(1)}, s32[51]{0:T(128)}, u32[]{:S(2)}) copy-start(s32[51]{0:T(128)} %param.12) | copy-start | bytes 616
  11.4 20.8 %collective-permute-start.1 = (bf16[128,512]{0,1:T(8,128)(2,1)S(1)}, bf16[128,512]{0,1:T(8,128)(2,1)}, u32[]{:S(2)}, u32[]{:S(2)}) collective-permute-start(bf16[128,512]{0,1:T(8,128)(2,1)S(1)} %copy.66), channel_id=1, source_target_pairs={{0,2},{2,4},{4,6},{6,8},{8,10},{10,12},{12,14},{14,16},{16,18},{18... | collective-permute-start | bytes 393224 | tf_op jit(solution)/shard_map/ppermute | solution.py:183
  14.5 16.6 %collective-permute-start = (bf16[128,512]{1,0:T(8,128)(2,1)S(1)}, bf16[128,512]{1,0:T(8,128)(2,1)}, u32[]{:S(2)}, u32[]{:S(2)}) collective-permute-start(bf16[128,512]{1,0:T(8,128)(2,1)S(1)} %slice.35), channel_id=1, source_target_pairs={{0,2},{2,4},{4,6},{6,8},{8,10},{10,12},{12,14},{14,16},{16,18},{18... | collective-permute-start | bytes 393224 | tf_op jit(solution)/shard_map/ppermute | solution.py:184
  18.6 0.6 copy-start.7
  19.2 1.2 copy-start.10
  21.7 3.2 copy-start.8
  21.7 3.4 copy-start
  26.6 4.2 %slice-start = ((bf16[640,2048]{1,0:T(8,128)(2,1)}), bf16[128,2048]{1,0:T(8,128)(2,1)S(1)}, s32[]{:S(2)}) async-start(bf16[640,2048]{1,0:T(8,128)(2,1)} %param.7), calls=%async_computation.3 | async-start | bytes 1048576 | tf_op jit(solution)/shard_map/slice | solution.py:269
  33.2 0.8 copy-start.11
  331.9 5.8 %copy-start.5 = (pred[16,40]{1,0:T(8,128)(4,1)S(1)}, pred[16,40]{1,0:T(8,128)(4,1)}, u32[]{:S(2)}) copy-start(pred[16,40]{1,0:T(8,128)(4,1)} %get-tuple-element.22) | copy-start | bytes 1924
  331.9 44.7 %collective-permute-start.2 = (bf16[320,8192]{1,0:T(8,128)(2,1)}, bf16[320,8192]{1,0:T(8,128)(2,1)}, u32[]{:S(2)}, u32[]{:S(2)}) collective-permute-start(bf16[320,8192]{1,0:T(8,128)(2,1)} %convolution_convert_fusion), channel_id=1, source_target_pairs={{0,1},{1,0},{2,3},{3,2},{4,5},{5,4},{6,7},{7,6},{8,9},{9,8},{10,11... | collective-permute-start | bytes 15728648 | tf_op jit(solution)/shard_map/ppermute | solution.py:282
  332.2 41.3 %all-to-all-start = ((bf16[2,16,3,8192]{3,0,2,1:T(2,128)(2,1)}), bf16[2,16,3,8192]{3,0,2,1:T(2,128)(2,1)S(1)}, u32[]{:S(2)}, u32[]{:S(2)}) async-start(bf16[2,16,3,8192]{3,0,2,1:T(2,128)(2,1)} %bitcast.5), calls=%async_computation | async-start | bytes 3145728 | tf_op jit(solution)/shard_map/all_to_all | solution.py:172
  374.8 1.8 copy-start.3
Sparse Core Ops, SparseCore 0:
  10.8 112.0 all-gather.4
  125.6 111.0 all-gather.2

commit v11 on v8

--- a/solution.py
+++ b/solution.py
@@ -63,30 +63,30 @@
         k = k_ref[...]
         v = v_ref[...]
         v_ext = jnp.concatenate([v, jnp.ones(v.shape, v.dtype)], axis=1)
+        s = lax.dot_general(
+            q_ref[...], k, (((1,), (1,)), ((), ())), preferred_element_type=jnp.float32
+        )
         if masked:
-            rows = i * tq + lax.broadcasted_iota(jnp.int32, (tq, tk), 0)
-            cols = lax.broadcasted_iota(jnp.int32, (tq, tk), 1)
+            shape = (group * tq, k.shape[0])
+            rows = i * tq + lax.broadcasted_iota(jnp.int32, shape, 0) % tq
+            cols = lax.broadcasted_iota(jnp.int32, shape, 1)
             src = t * per_tile + cols // chunk_rows
             key_pos = chunk * chunk_rows + cols % chunk_rows
             allowed = (src < b) | ((src == b) & (key_pos <= rows))
-        for g in range(group):
-            qg = q_ref[:, g * HEAD_SIZE:(g + 1) * HEAD_SIZE]
-            s = lax.dot_general(
-                qg, k, (((1,), (1,)), ((), ())), preferred_element_type=jnp.float32
-            )
-            if masked:
-                s = jnp.where(allowed, s, NEGATIVE_FILL)
-            m_prev = m_out[g]
-            m_new = jnp.maximum(m_prev, jnp.max(s, axis=1, keepdims=True) * scale)
-            p = jnp.exp2(s * log2_scale - m_new[:, :1] * LOG2_E)
-            alpha = jnp.exp2((m_prev - m_new) * LOG2_E)
-            pv = lax.dot_general(
-                p.astype(jnp.bfloat16), v_ext, (((1,), (0,)), ((), ())),
-                preferred_element_type=jnp.float32,
-            )
-            l_out[g] = alpha * l_out[g] + pv[:, HEAD_SIZE:]
-            acc_out[g] = acc_out[g] * alpha + pv[:, :HEAD_SIZE]
-            m_out[g] = m_new
+            s = jnp.where(allowed, s, NEGATIVE_FILL)
+        m_prev = m_out[...].reshape(group * tq, HEAD_SIZE)
+        m_new = jnp.maximum(m_prev, jnp.max(s, axis=1, keepdims=True) * scale)
+        p = jnp.exp2(s * log2_scale - m_new[:, :1] * LOG2_E)
+        alpha = jnp.exp2((m_prev - m_new) * LOG2_E)
+        pv = lax.dot_general(
+            p.astype(jnp.bfloat16), v_ext, (((1,), (0,)), ((), ())),
+            preferred_element_type=jnp.float32,
+        )
+        l_new = alpha * l_out[...].reshape(group * tq, HEAD_SIZE) + pv[:, HEAD_SIZE:]
+        acc_new = acc_out[...].reshape(group * tq, HEAD_SIZE) * alpha + pv[:, :HEAD_SIZE]
+        l_out[...] = l_new.reshape(group, tq, HEAD_SIZE)
+        acc_out[...] = acc_new.reshape(group, tq, HEAD_SIZE)
+        m_out[...] = m_new.reshape(group, tq, HEAD_SIZE)
 
     @pl.when(t * per_tile + per_tile - 1 < b)
     def _full():
@@ -126,8 +126,12 @@
         (tk, HEAD_SIZE), lambda h, i, t, b: (jnp.minimum(t, b[0] // per_tile), heads_kv + h)
     )
     q_spec = pl.BlockSpec((tq, group * HEAD_SIZE), lambda h, i, t, b: (i, h))
-    in_specs = [q_spec, kv_spec_k, kv_spec_v]
-    operands = [b_arr, q_long, kv_chunk, kv_chunk]
+    stacked_spec = pl.BlockSpec((None, group * tq, HEAD_SIZE), lambda h, i, t, b: (h, i, 0))
+    q_stacked = q_long.reshape(rows, heads_kv, group, HEAD_SIZE).transpose(1, 2, 0, 3).reshape(
+        heads_kv, group * rows, HEAD_SIZE
+    )
+    in_specs = [stacked_spec, kv_spec_k, kv_spec_v]
+    operands = [b_arr, q_stacked, kv_chunk, kv_chunk]
     aliases = {}
     if not first:
         in_specs += [state_spec] * 3

time: 395 us -> 418 us (1.058)
  Pallas kernels: 152 us -> 198 us
  waiting for transfers between devices: 153 us -> 123 us
  local copies, waits for them, and re-layouts: 13.7 us -> 20.2 us
    pallas_call x2, Pallas kernels: 152 us -> 198 us  [long_attention_chunk(): pl.pallas_call(kernel, grid_spec=grid_spec, out_shape=out_shape, input_ou...]
    all_gather x2, waiting for transfers between devices: 92.9 us -> 63.3 us  [long_attention(): kv = lax.all_gather(kv, 'req', axis=0, tiled=True)]
    reshape x0 -> x2, local copies, waits for them, and re-layouts: none -> 6.21 us  [long_attention_chunk(): q_long.reshape(rows, heads_kv, group, HEAD_SIZE).transpose(1, 2, 0, 3)]
  transfers between devices with their start and end apart: 6 -> 6, of which waited for: 5 -> 5; matrix products, arithmetic and copies ran while one was open for 5% -> 6% of each run, Pallas kernels for 19% -> 24%
where the time goes in v11:
time: 418 us; the launch traced here: 417 us
  Pallas kernels  198 us (47%)
  waiting for transfers between devices  123 us (29%)
  matrix products  44.7 us (11%)
  local copies, waits for them, and re-layouts  20.2 us (5%)
  between operations  14.4 us (3%)
  starting transfers between devices  12.2 us (3%)
  other arithmetic  4.32 us (1%)
    pallas_call x2, Pallas kernels, long_attention_chunk(): pl.pallas_call(kernel, grid_spec=grid_spec, out_shape=out_shape, input_ou...  198 us
    all_gather x2, waiting for transfers between devices, long_attention(): kv = lax.all_gather(kv, 'req', axis=0, tiled=True)  63.3 us
    all_to_all x1, waiting for transfers between devices, local(): lax.all_to_all(outgoing, 'req', split_axis=1, concat_axis=1, tiled=True)  49.1 us
    dot_general x1, matrix products, local(): jnp.dot(mine, out_weight, preferred_element_type=jnp.float32)  21.2 us
    dot_general x1, matrix products, local(): jnp.dot(theirs, out_weight, preferred_element_type=jnp.float32)  18.9 us
  transfers between devices with their start and end apart: 6, of which 5 were waited for; matrix products, arithmetic and copies ran while one was open for 6% of the time, Pallas kernels for 24%

profile of v11, /device:TPU:29, one launch (start us, length us, event | category | flops | bytes accessed | tf_op | source)
XLA Modules:
  0.0 417.4 jit_solution(2015620534572283160)
XLA Ops:
  7.2 1.1 fusion.38
  8.3 1.1 fusion.39
  9.4 0.9 pad_maximum_fusion.1
  10.4 0.9 pad_maximum_fusion
  11.3 0.3 stack.10
  11.6 0.3 stack.9
  12.0 0.1 copy.26
  12.2 0.1 reduce
  12.5 0.1 ne.107
  12.6 0.1 convert_reduce_fusion.2
  12.7 0.1 select_reduce_fusion.2
  12.9 0.2 broadcast_in_dim.124
  13.1 0.2 copy.47
  13.3 0.5 convert_reduce_fusion
  13.8 0.7 fusion.1
  14.5 2.8 copy.27
  17.3 6.6 %all-to-all-start = ((bf16[2,16,3,8192]{3,0,2,1:T(2,128)(2,1)}), bf16[2,16,3,8192]{3,0,2,1:T(2,128)(2,1)}, u32[]{:S(2)}, u32[]{:S(2)}) async-start(bf16[2,16,3,8192]{3,0,2,1:T(2,128)(2,1)} %bitcast.58), calls=%async_computation | async-start | bytes 3145728 | tf_op jit(solution)/shard_map/all_to_all | solution.py:250
  24.0 0.1 copy.46
  24.1 3.1 collective-permute-start.1
  27.2 0.9 slice.35
  28.1 2.1 collective-permute-start
  30.2 0.1 convert_reduce_fusion.1
  30.3 0.1 select_reduce_fusion
  30.5 0.2 and_and_fusion
  30.6 6.5 %collective-permute-done = bf16[128,512]{1,0:T(8,128)(2,1)S(1)} collective-permute-done((bf16[128,512]{1,0:T(8,128)(2,1)S(1)}, bf16[128,512]{1,0:T(8,128)(2,1)S(1)}, u32[]{:S(2)}, u32[]{:S(2)}) %collective-permute-start) | collective-permute-done | bytes 131104 | tf_op jit(solution)/shard_map/ppermute | solution.py:185
  37.2 0.1 copy.29
  37.3 0.9 pad_maximum_fusion.3
  38.3 49.1 %all-to-all-done = bf16[2,16,3,8192]{3,0,2,1:T(2,128)(2,1)} async-done(((bf16[2,16,3,8192]{3,0,2,1:T(2,128)(2,1)}), bf16[2,16,3,8192]{3,0,2,1:T(2,128)(2,1)}, u32[]{:S(2)}, u32[]{:S(2)}) %all-to-all-start) | async-done | bytes 1572896 | tf_op jit(solution)/shard_map/all_to_all | solution.py:250
  87.4 2.6 copy.31
  90.0 1.0 slice-done.1
  91.0 0.5 fusion.40
  91.5 0.3 fusion.2
  91.9 0.5 fusion.14
  92.4 0.2 copy.45
  92.6 0.8 slice-done
  93.4 2.7 reshape.294
  96.1 3.5 copy.28
  99.7 48.6 %all-gather.5.cloned.1.call-done.k_ref.v_ref = bf16[4096,1024]{1,0:T(8,128)(2,1)} async-done(((bf16[256,1024]{1,0:T(8,128)(2,1)}), bf16[4096,1024]{1,0:T(8,128)(2,1)}) %all-gather.5.cloned.1.call-update) | async-done | bytes 8388624 | tf_op jit(solution)/shard_map/all_gather | solution.py:173
  148.3 99.1 %shard_map.86 = (f32[4,4,512,128]{3,2,1,0:T(8,128)}, f32[4,4,512,128]{3,2,1,0:T(8,128)}, f32[4,4,512,128]{3,2,1,0:T(8,128)}) custom-call(s32[1]{0:T(128)} %bitcast.b_ref, bf16[4,2048,128]{2,1,0:T(8,128)(2,1)} %bitcast.56, bf16[4096,1024]{1,0:T(8,128)(2,1)} %all-gather.5.cloned.1.call-done.k_ref.v_ref, bf16[4096,1024]{1,0:T(8,128)(2,1)} %all-gather.5.cloned.1.call-done.k_ref.v_ref), custom_call_target="tpu_custom_call" | custom-call | tf_op jit(solution)/shard_map/pallas_call | solution.py:153
  247.4 14.7 %all-gather.3.cloned.1.call-done.k_ref.v_ref = bf16[4096,1024]{1,0:T(8,128)(2,1)} async-done(((bf16[256,1024]{1,0:T(8,128)(2,1)}), bf16[4096,1024]{1,0:T(8,128)(2,1)}) %all-gather.3.cloned.1.call-update) | async-done | bytes 8388624 | tf_op jit(solution)/shard_map/all_gather | solution.py:173
  262.1 99.4 %shard_map.87 = bf16[512,2048]{1,0:T(8,128)(2,1)} custom-call(s32[1]{0:T(128)} %bitcast.b_ref, bf16[4,2048,128]{2,1,0:T(8,128)(2,1)} %bitcast.57, bf16[4096,1024]{1,0:T(8,128)(2,1)} %all-gather.3.cloned.1.call-done.k_ref.v_ref, bf16[4096,1024]{1,0:T(8,128)(2,1)} %all-gather.3.cloned.1.call-done.k_ref.v_ref, f32[4,4,512,128]{3,2,1,0:T(8,128)} %get-tuple-element.8.refs_0_, ...), custom_call_target="tpu_custom_call" | custom-call | tf_op jit(solution)/shard_map/pallas_call | solution.py:153
  361.5 18.9 %convolution_convert_fusion = bf16[320,8192]{1,0:T(8,128)(2,1)} fusion(bf16[2048,8192]{1,0:T(8,128)(2,1)} %param.10, s32[]{:T(128)S(6)} %select_n.109, bf16[512,2048]{1,0:T(8,128)(2,1)} %shard_map.87, bf16[128,2048]{1,0:T(8,128)(2,1)S(1)} %copy.45), kind=kOutput, calls=%fused_computation | convolution fusion | flops 10742661120 | bytes 41418756 | tf_op jit(solution)/shard_map/dot_general | solution.py:283
  380.4 0.3 collective-permute-start.2
  380.7 0.3 convolution_convert_fusion.3
  381.0 2.7 fusion
  383.7 1.7 copy.48
  385.4 4.0 collective-permute-done.2
  389.4 21.2 %add_convert_fusion = bf16[320,8192]{1,0:T(8,128)(2,1)} fusion(bf16[320,8192]{1,0:T(8,128)(2,1)} %collective-permute-done.2, bf16[2048,8192]{1,0:T(8,128)(2,1)} %param.10, pred[]{:T(512)S(6)} %eq.58, s32[]{:T(128)S(6)} %select_n.108, bf16[512,2048]{1,0:T(8,128)(2,1)S(1)} %copy-done.3, bf16[128,2048]{1,0:T(8,128)(2,1)S(1)} %copy.45), kind=kOutput, calls=%fused_computation.2 | convolution fusion | flops 10758389760 | bytes 46661636 | tf_op jit(solution)/shard_map/dot_general | solution.py:286
  (42 shorter events, 0.6 us)
Async XLA Ops:
  7.2 141.1 %all-gather.5.cloned.1.call-start = ((), (), s32[]{:S(2)}) async-start(), calls=%async_computation.2 | async-start | bytes 8912896 | tf_op jit(solution)/shard_map/all_gather | solution.py:173
  8.3 3.0 copy-start.2
  9.4 2.2 copy-start.1
  10.3 251.8 %all-gather.3.cloned.1.call-start = ((), (), s32[]{:S(2)}) async-start(), calls=%async_computation.1 | async-start | bytes 8912896 | tf_op jit(solution)/shard_map/all_gather | solution.py:173
  10.4 1.6 copy-start.5
  10.4 1.9 copy-start.4
  10.4 2.3 copy-start.6
  17.3 6.7 %slice-start.2 = ((bf16[640,512]{1,0:T(8,128)(2,1)}), bf16[128,512]{1,0:T(8,128)(2,1)S(1)}, s32[]{:S(2)}) async-start(bf16[640,512]{1,0:T(8,128)(2,1)} %param.8), calls=%async_computation.5 | async-start | bytes 262144 | tf_op jit(solution)/shard_map/slice | solution.py:272
  17.3 70.1 %copy-start = (bf16[640,2048]{1,0:T(8,128)(2,1)S(1)}, bf16[640,2048]{1,0:T(8,128)(2,1)}, u32[]{:S(2)}) copy-start(bf16[640,2048]{1,0:T(8,128)(2,1)} %param.7) | copy-start | bytes 7864324
  17.3 70.1 %all-to-all-start = ((bf16[2,16,3,8192]{3,0,2,1:T(2,128)(2,1)}), bf16[2,16,3,8192]{3,0,2,1:T(2,128)(2,1)}, u32[]{:S(2)}, u32[]{:S(2)}) async-start(bf16[2,16,3,8192]{3,0,2,1:T(2,128)(2,1)} %bitcast.58), calls=%async_computation | async-start | bytes 3145728 | tf_op jit(solution)/shard_map/all_to_all | solution.py:250
  24.1 13.3 %collective-permute-start.1 = (bf16[128,512]{0,1:T(8,128)(2,1)S(1)}, bf16[128,512]{0,1:T(8,128)(2,1)}, u32[]{:S(2)}, u32[]{:S(2)}) collective-permute-start(bf16[128,512]{0,1:T(8,128)(2,1)S(1)} %copy.46), channel_id=1, source_target_pairs={{0,2},{2,4},{4,6},{6,8},{8,10},{10,12},{12,14},{14,16},{16,18},{18... | collective-permute-start | bytes 393224 | tf_op jit(solution)/shard_map/ppermute | solution.py:184
  28.1 9.1 %collective-permute-start = (bf16[128,512]{1,0:T(8,128)(2,1)S(1)}, bf16[128,512]{1,0:T(8,128)(2,1)S(1)}, u32[]{:S(2)}, u32[]{:S(2)}) collective-permute-start(bf16[128,512]{1,0:T(8,128)(2,1)S(1)} %slice.35), channel_id=1, source_target_pairs={{0,2},{2,4},{4,6},{6,8},{8,10},{10,12},{12,14},{14,16},{16,18},{18... | collective-permute-start | bytes 393224 | tf_op jit(solution)/shard_map/ppermute | solution.py:185
  90.0 1.0 slice-start.1
  91.9 1.6 slice-start
  380.4 9.0 %collective-permute-start.2 = (bf16[320,8192]{1,0:T(8,128)(2,1)}, bf16[320,8192]{1,0:T(8,128)(2,1)}, u32[]{:S(2)}, u32[]{:S(2)}) collective-permute-start(bf16[320,8192]{1,0:T(8,128)(2,1)} %convolution_convert_fusion), channel_id=1, source_target_pairs={{0,1},{1,0},{2,3},{3,2},{4,5},{5,4},{6,7},{7,6},{8,9},{9,8},{10,11... | collective-permute-start | bytes 15728648 | tf_op jit(solution)/shard_map/ppermute | solution.py:284
  383.7 5.7 %copy-start.3 = (bf16[512,2048]{1,0:T(8,128)(2,1)S(1)}, bf16[512,2048]{1,0:T(8,128)(2,1)}, u32[]{:S(2)}) copy-start(bf16[512,2048]{1,0:T(8,128)(2,1)} %shard_map.87) | copy-start | bytes 6291460
Sparse Core Ops, SparseCore 0:
  10.8 137.4 all-gather.4
  151.1 111.0 all-gather.2

commit v12 on v8

--- a/solution.py
+++ b/solution.py
@@ -114,7 +114,7 @@
     total = kv_chunk.shape[0]
     tk = min(512, total)
     per_tile = tk // chunk_rows
-    tq = LONG_DEV
+    tq = LONG_DEV // 2
     kernel = functools.partial(
         flash_kernel, group=group, tq=tq, tk=tk, chunk_rows=chunk_rows, chunk=chunk,
         first=first, last=last,

time: 395 us -> 417 us (1.056)
  Pallas kernels: 152 us -> 195 us
  waiting for transfers between devices: 153 us -> 133 us
    pallas_call x2, Pallas kernels: 152 us -> 195 us  [long_attention_chunk(): pl.pallas_call(kernel, grid_spec=grid_spec, out_shape=out_shape, input_ou...]
    all_gather x2, waiting for transfers between devices: 92.9 us -> 72.3 us  [long_attention(): kv = lax.all_gather(kv, 'req', axis=0, tiled=True)]
  transfers between devices with their start and end apart: 6 -> 6, of which waited for: 5 -> 5; matrix products, arithmetic and copies ran while one was open for 5% -> 4% of each run, Pallas kernels for 19% -> 23%
where the time goes in v12:
time: 417 us; the launch traced here: 416 us
  Pallas kernels  195 us (47%)
  waiting for transfers between devices  133 us (32%)
  matrix products  44.5 us (11%)
  between operations  14.4 us (3%)
  local copies, waits for them, and re-layouts  13.7 us (3%)
  starting transfers between devices  12.2 us (3%)
    pallas_call x2, Pallas kernels, long_attention_chunk(): pl.pallas_call(kernel, grid_spec=grid_spec, out_shape=out_shape, input_ou...  195 us
    all_gather x2, waiting for transfers between devices, long_attention(): kv = lax.all_gather(kv, 'req', axis=0, tiled=True)  72.3 us
    all_to_all x1, waiting for transfers between devices, local(): lax.all_to_all(outgoing, 'req', split_axis=1, concat_axis=1, tiled=True)  50 us
    dot_general x1, matrix products, local(): jnp.dot(mine, out_weight, preferred_element_type=jnp.float32)  20.9 us
    dot_general x1, matrix products, local(): jnp.dot(theirs, out_weight, preferred_element_type=jnp.float32)  18.9 us
  transfers between devices with their start and end apart: 6, of which 5 were waited for; matrix products, arithmetic and copies ran while one was open for 4% of the time, Pallas kernels for 23%

profile of v12, /device:TPU:29, one launch (start us, length us, event | category | flops | bytes accessed | tf_op | source)
XLA Modules:
  0.0 416.1 jit_solution(10352417831193108296)
XLA Ops:
  7.2 1.1 fusion.38
  8.3 1.1 fusion.39
  9.4 0.9 pad_maximum_fusion.1
  10.4 0.9 pad_maximum_fusion
  11.3 0.3 stack.10
  11.6 0.3 stack.9
  12.0 0.1 copy.24
  12.1 0.1 reduce-window.8
  12.2 0.1 reduce
  12.3 0.1 rem.82
  12.4 0.1 div.59
  12.5 0.1 ne.107
  12.6 0.1 convert_reduce_fusion.2
  12.7 0.1 select_reduce_fusion.2
  12.8 0.1 broadcast_in_dim.123
  12.9 0.2 broadcast_in_dim.124
  13.1 0.2 copy.44
  13.3 0.5 convert_reduce_fusion
  13.8 0.7 fusion.1
  14.5 2.8 copy.25
  17.3 6.6 %all-to-all-start = ((bf16[2,16,3,8192]{3,0,2,1:T(2,128)(2,1)}), bf16[2,16,3,8192]{3,0,2,1:T(2,128)(2,1)}, u32[]{:S(2)}, u32[]{:S(2)}) async-start(bf16[2,16,3,8192]{3,0,2,1:T(2,128)(2,1)} %bitcast.53), calls=%async_computation | async-start | bytes 3145728 | tf_op jit(solution)/shard_map/all_to_all | solution.py:246
  24.0 0.1 copy.43
  24.1 3.1 collective-permute-start.1
  27.2 0.9 slice.35
  28.1 2.1 collective-permute-start
  30.2 0.1 convert_reduce_fusion.1
  30.3 0.1 select_reduce_fusion
  30.5 0.2 and_and_fusion
  30.6 6.5 %collective-permute-done = bf16[128,512]{1,0:T(8,128)(2,1)S(1)} collective-permute-done((bf16[128,512]{1,0:T(8,128)(2,1)S(1)}, bf16[128,512]{1,0:T(8,128)(2,1)S(1)}, u32[]{:S(2)}, u32[]{:S(2)}) %collective-permute-start) | collective-permute-done | bytes 131104 | tf_op jit(solution)/shard_map/ppermute | solution.py:181
  37.2 0.1 copy.26
  37.4 50.0 %all-to-all-done = bf16[2,16,3,8192]{3,0,2,1:T(2,128)(2,1)} async-done(((bf16[2,16,3,8192]{3,0,2,1:T(2,128)(2,1)}), bf16[2,16,3,8192]{3,0,2,1:T(2,128)(2,1)}, u32[]{:S(2)}, u32[]{:S(2)}) %all-to-all-start) | async-done | bytes 1572896 | tf_op jit(solution)/shard_map/all_to_all | solution.py:246
  87.4 2.6 copy.28
  90.0 1.5 slice.30.q_ref
  91.5 0.5 fusion.40
  92.0 0.3 fusion.2
  92.3 0.5 fusion.14
  92.9 0.2 copy.42
  93.1 55.2 %all-gather.5.cloned.1.call-done.k_ref.v_ref = bf16[4096,1024]{1,0:T(8,128)(2,1)} async-done(((bf16[256,1024]{1,0:T(8,128)(2,1)}), bf16[4096,1024]{1,0:T(8,128)(2,1)}) %all-gather.5.cloned.1.call-update) | async-done | bytes 8388624 | tf_op jit(solution)/shard_map/all_gather | solution.py:169
  148.3 96.8 %shard_map.86 = (f32[4,4,512,128]{3,2,1,0:T(8,128)}, f32[4,4,512,128]{3,2,1,0:T(8,128)}, f32[4,4,512,128]{3,2,1,0:T(8,128)}) custom-call(s32[1]{0:T(128)} %bitcast.b_ref, bf16[512,2048]{1,0:T(8,128)(2,1)} %slice.30.q_ref, bf16[4096,1024]{1,0:T(8,128)(2,1)} %all-gather.5.cloned.1.call-done.k_ref.v_ref, bf16[4096,1024]{1,0:T(8,128)(2,1)} %all-gather.5.cloned.1.call-done.k_ref.v_ref), custom_call_target="tpu_custom_call" | custom-call | tf_op jit(solution)/shard_map/pallas_call | solution.py:149
  245.1 17.0 %all-gather.3.cloned.1.call-done.k_ref.v_ref = bf16[4096,1024]{1,0:T(8,128)(2,1)} async-done(((bf16[256,1024]{1,0:T(8,128)(2,1)}), bf16[4096,1024]{1,0:T(8,128)(2,1)}) %all-gather.3.cloned.1.call-update) | async-done | bytes 8388624 | tf_op jit(solution)/shard_map/all_gather | solution.py:169
  262.1 98.4 %shard_map.87 = bf16[512,2048]{1,0:T(8,128)(2,1)} custom-call(s32[1]{0:T(128)} %bitcast.b_ref, bf16[512,2048]{1,0:T(8,128)(2,1)} %slice.30.q_ref, bf16[4096,1024]{1,0:T(8,128)(2,1)} %all-gather.3.cloned.1.call-done.k_ref.v_ref, bf16[4096,1024]{1,0:T(8,128)(2,1)} %all-gather.3.cloned.1.call-done.k_ref.v_ref, f32[4,4,512,128]{3,2,1,0:T(8,128)} %get-tuple-element.8.refs_0_, ...), custom_call_target="tpu_custom_call" | custom-call | tf_op jit(solution)/shard_map/pallas_call | solution.py:149
  360.5 18.9 %convolution_convert_fusion = bf16[320,8192]{1,0:T(8,128)(2,1)} fusion(bf16[2048,8192]{1,0:T(8,128)(2,1)} %param.10, s32[]{:T(128)S(6)} %select_n.109, bf16[512,2048]{1,0:T(8,128)(2,1)} %shard_map.87, bf16[128,2048]{1,0:T(8,128)(2,1)S(1)} %copy.42), kind=kOutput, calls=%fused_computation | convolution fusion | flops 10742661120 | bytes 41418756 | tf_op jit(solution)/shard_map/dot_general | solution.py:279
  379.4 0.3 collective-permute-start.2
  379.7 0.3 convolution_convert_fusion.3
  379.9 2.7 fusion
  382.6 1.7 copy.45
  384.4 4.0 collective-permute-done.2
  388.4 20.9 %add_convert_fusion = bf16[320,8192]{1,0:T(8,128)(2,1)} fusion(bf16[320,8192]{1,0:T(8,128)(2,1)} %collective-permute-done.2, bf16[2048,8192]{1,0:T(8,128)(2,1)} %param.10, pred[]{:T(512)S(6)} %eq.58, s32[]{:T(128)S(6)} %select_n.108, bf16[512,2048]{1,0:T(8,128)(2,1)S(1)} %copy-done.3, bf16[128,2048]{1,0:T(8,128)(2,1)S(1)} %copy.42), kind=kOutput, calls=%fused_computation.2 | convolution fusion | flops 10758389760 | bytes 46661636 | tf_op jit(solution)/shard_map/dot_general | solution.py:282
  (39 shorter events, 0.3 us)
Async XLA Ops:
  7.2 141.1 %all-gather.5.cloned.1.call-start = ((), (), s32[]{:S(2)}) async-start(), calls=%async_computation.2 | async-start | bytes 8912896 | tf_op jit(solution)/shard_map/all_gather | solution.py:169
  8.3 3.0 copy-start.2
  9.4 2.2 copy-start.1
  10.3 251.8 %all-gather.3.cloned.1.call-start = ((), (), s32[]{:S(2)}) async-start(), calls=%async_computation.1 | async-start | bytes 8912896 | tf_op jit(solution)/shard_map/all_gather | solution.py:169
  10.4 1.6 copy-start.5
  10.4 1.9 copy-start.4
  10.4 2.3 copy-start.6
  17.3 6.7 %slice-start.1 = ((bf16[640,512]{1,0:T(8,128)(2,1)}), bf16[128,512]{1,0:T(8,128)(2,1)S(1)}, s32[]{:S(2)}) async-start(bf16[640,512]{1,0:T(8,128)(2,1)} %param.8), calls=%async_computation.4 | async-start | bytes 262144 | tf_op jit(solution)/shard_map/slice | solution.py:268
  17.3 70.1 %copy-start = (bf16[640,2048]{1,0:T(8,128)(2,1)S(1)}, bf16[640,2048]{1,0:T(8,128)(2,1)}, u32[]{:S(2)}) copy-start(bf16[640,2048]{1,0:T(8,128)(2,1)} %param.7) | copy-start | bytes 7864324
  17.3 70.1 %all-to-all-start = ((bf16[2,16,3,8192]{3,0,2,1:T(2,128)(2,1)}), bf16[2,16,3,8192]{3,0,2,1:T(2,128)(2,1)}, u32[]{:S(2)}, u32[]{:S(2)}) async-start(bf16[2,16,3,8192]{3,0,2,1:T(2,128)(2,1)} %bitcast.53), calls=%async_computation | async-start | bytes 3145728 | tf_op jit(solution)/shard_map/all_to_all | solution.py:246
  24.1 13.3 %collective-permute-start.1 = (bf16[128,512]{0,1:T(8,128)(2,1)S(1)}, bf16[128,512]{0,1:T(8,128)(2,1)S(1)}, u32[]{:S(2)}, u32[]{:S(2)}) collective-permute-start(bf16[128,512]{0,1:T(8,128)(2,1)S(1)} %copy.43), channel_id=1, source_target_pairs={{0,2},{2,4},{4,6},{6,8},{8,10},{10,12},{12,14},{14,16},{16,18},{18... | collective-permute-start | bytes 393224 | tf_op jit(solution)/shard_map/ppermute | solution.py:180
  28.1 9.1 %collective-permute-start = (bf16[128,512]{1,0:T(8,128)(2,1)S(1)}, bf16[128,512]{1,0:T(8,128)(2,1)S(1)}, u32[]{:S(2)}, u32[]{:S(2)}) collective-permute-start(bf16[128,512]{1,0:T(8,128)(2,1)S(1)} %slice.35), channel_id=1, source_target_pairs={{0,2},{2,4},{4,6},{6,8},{8,10},{10,12},{12,14},{14,16},{16,18},{18... | collective-permute-start | bytes 393224 | tf_op jit(solution)/shard_map/ppermute | solution.py:181
  90.0 1.5 slice-start
  379.4 9.0 %collective-permute-start.2 = (bf16[320,8192]{1,0:T(8,128)(2,1)}, bf16[320,8192]{1,0:T(8,128)(2,1)}, u32[]{:S(2)}, u32[]{:S(2)}) collective-permute-start(bf16[320,8192]{1,0:T(8,128)(2,1)} %convolution_convert_fusion), channel_id=1, source_target_pairs={{0,1},{1,0},{2,3},{3,2},{4,5},{5,4},{6,7},{7,6},{8,9},{9,8},{10,11... | collective-permute-start | bytes 15728648 | tf_op jit(solution)/shard_map/ppermute | solution.py:280
  382.6 5.7 %copy-start.3 = (bf16[512,2048]{1,0:T(8,128)(2,1)S(1)}, bf16[512,2048]{1,0:T(8,128)(2,1)}, u32[]{:S(2)}) copy-start(bf16[512,2048]{1,0:T(8,128)(2,1)} %shard_map.87) | copy-start | bytes 6291460
Sparse Core Ops, SparseCore 0:
  10.8 137.4 all-gather.4
  151.1 111.0 all-gather.2

commit v13 on v8

--- a/solution.py
+++ b/solution.py
@@ -112,7 +112,7 @@
     group = q_cols // kv_cols
     chunk_rows = LONG_DEV // LONG_CHUNKS
     total = kv_chunk.shape[0]
-    tk = min(512, total)
+    tk = min(1024, total)
     per_tile = tk // chunk_rows
     tq = LONG_DEV
     kernel = functools.partial(

time: 395 us -> 381 us (0.965)
  Pallas kernels: 152 us -> 125 us
  waiting for transfers between devices: 153 us -> 167 us
    pallas_call x2, Pallas kernels: 152 us -> 125 us  [long_attention_chunk(): pl.pallas_call(kernel, grid_spec=grid_spec, out_shape=out_shape, input_ou...]
    all_gather x2, waiting for transfers between devices: 92.9 us -> 107 us  [long_attention(): kv = lax.all_gather(kv, 'req', axis=0, tiled=True)]
  transfers between devices with their start and end apart: 6 -> 6, of which waited for: 5 -> 5; matrix products, arithmetic and copies ran while one was open for 5% -> 5% of each run, Pallas kernels for 19% -> 16%
where the time goes in v13:
time: 381 us; the launch traced here: 380 us
  waiting for transfers between devices  167 us (44%)
  Pallas kernels  125 us (33%)
  matrix products  44.5 us (12%)
  between operations  14.4 us (4%)
  local copies, waits for them, and re-layouts  13.7 us (4%)
  starting transfers between devices  12.2 us (3%)
    pallas_call x2, Pallas kernels, long_attention_chunk(): pl.pallas_call(kernel, grid_spec=grid_spec, out_shape=out_shape, input_ou...  125 us
    all_gather x2, waiting for transfers between devices, long_attention(): kv = lax.all_gather(kv, 'req', axis=0, tiled=True)  107 us
    all_to_all x1, waiting for transfers between devices, local(): lax.all_to_all(outgoing, 'req', split_axis=1, concat_axis=1, tiled=True)  50 us
    dot_general x1, matrix products, local(): jnp.dot(mine, out_weight, preferred_element_type=jnp.float32)  20.9 us
    dot_general x1, matrix products, local(): jnp.dot(theirs, out_weight, preferred_element_type=jnp.float32)  18.9 us
  transfers between devices with their start and end apart: 6, of which 5 were waited for; matrix products, arithmetic and copies ran while one was open for 5% of the time, Pallas kernels for 16%

profile of v13, /device:TPU:29, one launch (start us, length us, event | category | flops | bytes accessed | tf_op | source)
XLA Modules:
  0.0 380.4 jit_solution(3419102217984250643)
XLA Ops:
  7.2 1.1 fusion.38
  8.3 1.1 fusion.39
  9.4 0.9 pad_maximum_fusion.1
  10.4 0.9 pad_maximum_fusion
  11.3 0.3 stack.10
  11.6 0.3 stack.9
  12.0 0.1 copy.24
  12.1 0.1 reduce-window.8
  12.2 0.1 reduce
  12.3 0.1 rem.82
  12.4 0.1 div.59
  12.5 0.1 ne.107
  12.6 0.1 convert_reduce_fusion.2
  12.7 0.1 select_reduce_fusion.2
  12.8 0.1 broadcast_in_dim.123
  12.9 0.2 broadcast_in_dim.124
  13.1 0.2 copy.44
  13.3 0.5 convert_reduce_fusion
  13.8 0.7 fusion.1
  14.5 2.8 copy.25
  17.3 6.6 %all-to-all-start = ((bf16[2,16,3,8192]{3,0,2,1:T(2,128)(2,1)}), bf16[2,16,3,8192]{3,0,2,1:T(2,128)(2,1)}, u32[]{:S(2)}, u32[]{:S(2)}) async-start(bf16[2,16,3,8192]{3,0,2,1:T(2,128)(2,1)} %bitcast.53), calls=%async_computation | async-start | bytes 3145728 | tf_op jit(solution)/shard_map/all_to_all | solution.py:246
  24.0 0.1 copy.43
  24.1 3.1 collective-permute-start.1
  27.2 0.9 slice.35
  28.1 2.1 collective-permute-start
  30.2 0.1 convert_reduce_fusion.1
  30.3 0.1 select_reduce_fusion
  30.5 0.2 and_and_fusion
  30.6 6.5 %collective-permute-done = bf16[128,512]{1,0:T(8,128)(2,1)S(1)} collective-permute-done((bf16[128,512]{1,0:T(8,128)(2,1)S(1)}, bf16[128,512]{1,0:T(8,128)(2,1)S(1)}, u32[]{:S(2)}, u32[]{:S(2)}) %collective-permute-start) | collective-permute-done | bytes 131104 | tf_op jit(solution)/shard_map/ppermute | solution.py:181
  37.2 0.1 copy.26
  37.4 50.0 %all-to-all-done = bf16[2,16,3,8192]{3,0,2,1:T(2,128)(2,1)} async-done(((bf16[2,16,3,8192]{3,0,2,1:T(2,128)(2,1)}), bf16[2,16,3,8192]{3,0,2,1:T(2,128)(2,1)}, u32[]{:S(2)}, u32[]{:S(2)}) %all-to-all-start) | async-done | bytes 1572896 | tf_op jit(solution)/shard_map/all_to_all | solution.py:246
  87.4 2.6 copy.28
  90.0 1.5 slice.30.q_ref
  91.5 0.5 fusion.40
  92.0 0.3 fusion.2
  92.3 0.5 fusion.14
  92.9 0.2 copy.42
  93.1 55.2 %all-gather.5.cloned.1.call-done.k_ref.v_ref = bf16[4096,1024]{1,0:T(8,128)(2,1)} async-done(((bf16[256,1024]{1,0:T(8,128)(2,1)}), bf16[4096,1024]{1,0:T(8,128)(2,1)}) %all-gather.5.cloned.1.call-update) | async-done | bytes 8388624 | tf_op jit(solution)/shard_map/all_gather | solution.py:169
  148.3 62.4 %shard_map.86 = (f32[4,4,512,128]{3,2,1,0:T(8,128)}, f32[4,4,512,128]{3,2,1,0:T(8,128)}, f32[4,4,512,128]{3,2,1,0:T(8,128)}) custom-call(s32[1]{0:T(128)} %bitcast.b_ref, bf16[512,2048]{1,0:T(8,128)(2,1)} %slice.30.q_ref, bf16[4096,1024]{1,0:T(8,128)(2,1)} %all-gather.5.cloned.1.call-done.k_ref.v_ref, bf16[4096,1024]{1,0:T(8,128)(2,1)} %all-gather.5.cloned.1.call-done.k_ref.v_ref), custom_call_target="tpu_custom_call" | custom-call | tf_op jit(solution)/shard_map/pallas_call | solution.py:149
  210.7 51.4 %all-gather.3.cloned.1.call-done.k_ref.v_ref = bf16[4096,1024]{1,0:T(8,128)(2,1)} async-done(((bf16[256,1024]{1,0:T(8,128)(2,1)}), bf16[4096,1024]{1,0:T(8,128)(2,1)}) %all-gather.3.cloned.1.call-update) | async-done | bytes 8388624 | tf_op jit(solution)/shard_map/all_gather | solution.py:169
  262.1 62.6 %shard_map.87 = bf16[512,2048]{1,0:T(8,128)(2,1)} custom-call(s32[1]{0:T(128)} %bitcast.b_ref, bf16[512,2048]{1,0:T(8,128)(2,1)} %slice.30.q_ref, bf16[4096,1024]{1,0:T(8,128)(2,1)} %all-gather.3.cloned.1.call-done.k_ref.v_ref, bf16[4096,1024]{1,0:T(8,128)(2,1)} %all-gather.3.cloned.1.call-done.k_ref.v_ref, f32[4,4,512,128]{3,2,1,0:T(8,128)} %get-tuple-element.8.refs_0_, ...), custom_call_target="tpu_custom_call" | custom-call | tf_op jit(solution)/shard_map/pallas_call | solution.py:149
  324.7 18.9 %convolution_convert_fusion = bf16[320,8192]{1,0:T(8,128)(2,1)} fusion(bf16[2048,8192]{1,0:T(8,128)(2,1)} %param.10, s32[]{:T(128)S(6)} %select_n.109, bf16[512,2048]{1,0:T(8,128)(2,1)} %shard_map.87, bf16[128,2048]{1,0:T(8,128)(2,1)S(1)} %copy.42), kind=kOutput, calls=%fused_computation | convolution fusion | flops 10742661120 | bytes 41418756 | tf_op jit(solution)/shard_map/dot_general | solution.py:279
  343.6 0.3 collective-permute-start.2
  344.0 0.3 convolution_convert_fusion.3
  344.2 2.7 fusion
  346.9 1.7 copy.45
  348.7 4.0 %collective-permute-done.2 = bf16[320,8192]{1,0:T(8,128)(2,1)} collective-permute-done((bf16[320,8192]{1,0:T(8,128)(2,1)}, bf16[320,8192]{1,0:T(8,128)(2,1)}, u32[]{:S(2)}, u32[]{:S(2)}) %collective-permute-start.2) | collective-permute-done | bytes 5242912 | tf_op jit(solution)/shard_map/ppermute | solution.py:280
  352.6 20.9 %add_convert_fusion = bf16[320,8192]{1,0:T(8,128)(2,1)} fusion(bf16[320,8192]{1,0:T(8,128)(2,1)} %collective-permute-done.2, bf16[2048,8192]{1,0:T(8,128)(2,1)} %param.10, pred[]{:T(512)S(6)} %eq.58, s32[]{:T(128)S(6)} %select_n.108, bf16[512,2048]{1,0:T(8,128)(2,1)S(1)} %copy-done.3, bf16[128,2048]{1,0:T(8,128)(2,1)S(1)} %copy.42), kind=kOutput, calls=%fused_computation.2 | convolution fusion | flops 10758389760 | bytes 46661636 | tf_op jit(solution)/shard_map/dot_general | solution.py:282
  (39 shorter events, 0.3 us)
Async XLA Ops:
  7.2 141.1 %all-gather.5.cloned.1.call-start = ((), (), s32[]{:S(2)}) async-start(), calls=%async_computation.2 | async-start | bytes 8912896 | tf_op jit(solution)/shard_map/all_gather | solution.py:169
  8.3 3.0 copy-start.2
  9.4 2.2 copy-start.1
  10.3 251.8 %all-gather.3.cloned.1.call-start = ((), (), s32[]{:S(2)}) async-start(), calls=%async_computation.1 | async-start | bytes 8912896 | tf_op jit(solution)/shard_map/all_gather | solution.py:169
  10.4 1.6 copy-start.5
  10.4 1.9 copy-start.4
  10.4 2.3 copy-start.6
  17.3 6.7 %slice-start.1 = ((bf16[640,512]{1,0:T(8,128)(2,1)}), bf16[128,512]{1,0:T(8,128)(2,1)S(1)}, s32[]{:S(2)}) async-start(bf16[640,512]{1,0:T(8,128)(2,1)} %param.8), calls=%async_computation.4 | async-start | bytes 262144 | tf_op jit(solution)/shard_map/slice | solution.py:268
  17.3 70.1 %copy-start = (bf16[640,2048]{1,0:T(8,128)(2,1)S(1)}, bf16[640,2048]{1,0:T(8,128)(2,1)}, u32[]{:S(2)}) copy-start(bf16[640,2048]{1,0:T(8,128)(2,1)} %param.7) | copy-start | bytes 7864324
  17.3 70.1 %all-to-all-start = ((bf16[2,16,3,8192]{3,0,2,1:T(2,128)(2,1)}), bf16[2,16,3,8192]{3,0,2,1:T(2,128)(2,1)}, u32[]{:S(2)}, u32[]{:S(2)}) async-start(bf16[2,16,3,8192]{3,0,2,1:T(2,128)(2,1)} %bitcast.53), calls=%async_computation | async-start | bytes 3145728 | tf_op jit(solution)/shard_map/all_to_all | solution.py:246
  24.1 13.3 %collective-permute-start.1 = (bf16[128,512]{0,1:T(8,128)(2,1)S(1)}, bf16[128,512]{0,1:T(8,128)(2,1)S(1)}, u32[]{:S(2)}, u32[]{:S(2)}) collective-permute-start(bf16[128,512]{0,1:T(8,128)(2,1)S(1)} %copy.43), channel_id=1, source_target_pairs={{0,2},{2,4},{4,6},{6,8},{8,10},{10,12},{12,14},{14,16},{16,18},{18... | collective-permute-start | bytes 393224 | tf_op jit(solution)/shard_map/ppermute | solution.py:180
  28.1 9.1 %collective-permute-start = (bf16[128,512]{1,0:T(8,128)(2,1)S(1)}, bf16[128,512]{1,0:T(8,128)(2,1)S(1)}, u32[]{:S(2)}, u32[]{:S(2)}) collective-permute-start(bf16[128,512]{1,0:T(8,128)(2,1)S(1)} %slice.35), channel_id=1, source_target_pairs={{0,2},{2,4},{4,6},{6,8},{8,10},{10,12},{12,14},{14,16},{16,18},{18... | collective-permute-start | bytes 393224 | tf_op jit(solution)/shard_map/ppermute | solution.py:181
  90.0 1.5 slice-start
  343.6 9.0 %collective-permute-start.2 = (bf16[320,8192]{1,0:T(8,128)(2,1)}, bf16[320,8192]{1,0:T(8,128)(2,1)}, u32[]{:S(2)}, u32[]{:S(2)}) collective-permute-start(bf16[320,8192]{1,0:T(8,128)(2,1)} %convolution_convert_fusion), channel_id=1, source_target_pairs={{0,1},{1,0},{2,3},{3,2},{4,5},{5,4},{6,7},{7,6},{8,9},{9,8},{10,11... | collective-permute-start | bytes 15728648 | tf_op jit(solution)/shard_map/ppermute | solution.py:280
  346.9 5.7 %copy-start.3 = (bf16[512,2048]{1,0:T(8,128)(2,1)S(1)}, bf16[512,2048]{1,0:T(8,128)(2,1)}, u32[]{:S(2)}) copy-start(bf16[512,2048]{1,0:T(8,128)(2,1)} %shard_map.87) | copy-start | bytes 6291460
Sparse Core Ops, SparseCore 0:
  10.8 137.4 all-gather.4
  151.1 111.0 all-gather.2

commit v14 on v13

--- a/solution.py
+++ b/solution.py
@@ -112,7 +112,7 @@
     group = q_cols // kv_cols
     chunk_rows = LONG_DEV // LONG_CHUNKS
     total = kv_chunk.shape[0]
-    tk = min(1024, total)
+    tk = min(2048, total)
     per_tile = tk // chunk_rows
     tq = LONG_DEV
     kernel = functools.partial(

time: 381 us -> 380 us (level); the launches traced: 380 us -> 373 us
  Pallas kernels: 125 us -> 111 us
  waiting for transfers between devices: 167 us -> 174 us
    pallas_call x2, Pallas kernels: 125 us -> 111 us  [long_attention_chunk(): pl.pallas_call(kernel, grid_spec=grid_spec, out_shape=out_shape, input_ou...]
    all_gather x2, waiting for transfers between devices: 107 us -> 113 us  [long_attention(): kv = lax.all_gather(kv, 'req', axis=0, tiled=True)]
  transfers between devices with their start and end apart: 6 -> 6, of which waited for: 5 -> 5; matrix products, arithmetic and copies ran while one was open for 5% -> 5% of each run, Pallas kernels for 16% -> 15%
where the time goes in v14:
time: 380 us; the launch traced here: 373 us
  waiting for transfers between devices  174 us (46%)
  Pallas kernels  111 us (29%)
  matrix products  44.5 us (12%)
  between operations  14.6 us (4%)
  local copies, waits for them, and re-layouts  13.7 us (4%)
  starting transfers between devices  12.1 us (3%)
    all_gather x2, waiting for transfers between devices, long_attention(): kv = lax.all_gather(kv, 'req', axis=0, tiled=True)  113 us
    pallas_call x2, Pallas kernels, long_attention_chunk(): pl.pallas_call(kernel, grid_spec=grid_spec, out_shape=out_shape, input_ou...  111 us
    all_to_all x1, waiting for transfers between devices, local(): lax.all_to_all(outgoing, 'req', split_axis=1, concat_axis=1, tiled=True)  50 us
    dot_general x1, matrix products, local(): jnp.dot(mine, out_weight, preferred_element_type=jnp.float32)  20.9 us
    dot_general x1, matrix products, local(): jnp.dot(theirs, out_weight, preferred_element_type=jnp.float32)  18.9 us
  transfers between devices with their start and end apart: 6, of which 5 were waited for; matrix products, arithmetic and copies ran while one was open for 5% of the time, Pallas kernels for 15%

profile of v14, /device:TPU:29, one launch (start us, length us, event | category | flops | bytes accessed | tf_op | source)
XLA Modules:
  0.0 373.4 jit_solution(8122801422807915663)
XLA Ops:
  7.2 1.1 fusion.38
  8.3 1.1 fusion.39
  9.4 0.9 pad_maximum_fusion.1
  10.4 0.9 pad_maximum_fusion
  11.3 0.3 stack.10
  11.6 0.3 stack.9
  12.0 0.1 copy.24
  12.1 0.1 reduce-window.8
  12.2 0.1 reduce
  12.3 0.1 rem.82
  12.4 0.1 div.59
  12.5 0.1 ne.107
  12.6 0.1 convert_reduce_fusion.2
  12.7 0.1 select_reduce_fusion.2
  12.8 0.1 broadcast_in_dim.123
  12.9 0.2 broadcast_in_dim.124
  13.1 0.2 copy.44
  13.3 0.5 convert_reduce_fusion
  13.8 0.7 fusion.1
  14.5 2.8 copy.25
  17.3 6.6 %all-to-all-start = ((bf16[2,16,3,8192]{3,0,2,1:T(2,128)(2,1)}), bf16[2,16,3,8192]{3,0,2,1:T(2,128)(2,1)}, u32[]{:S(2)}, u32[]{:S(2)}) async-start(bf16[2,16,3,8192]{3,0,2,1:T(2,128)(2,1)} %bitcast.53), calls=%async_computation | async-start | bytes 3145728 | tf_op jit(solution)/shard_map/all_to_all | solution.py:246
  24.0 0.1 copy.43
  24.1 3.1 collective-permute-start.1
  27.2 0.9 slice.35
  28.1 1.9 collective-permute-start
  30.0 0.1 convert_reduce_fusion.1
  30.1 0.1 select_reduce_fusion
  30.3 0.2 and_and_fusion
  30.5 6.7 %collective-permute-done = bf16[128,512]{1,0:T(8,128)(2,1)S(1)} collective-permute-done((bf16[128,512]{1,0:T(8,128)(2,1)S(1)}, bf16[128,512]{1,0:T(8,128)(2,1)S(1)}, u32[]{:S(2)}, u32[]{:S(2)}) %collective-permute-start) | collective-permute-done | bytes 131104 | tf_op jit(solution)/shard_map/ppermute | solution.py:181
  37.2 0.1 copy.26
  37.4 50.0 %all-to-all-done = bf16[2,16,3,8192]{3,0,2,1:T(2,128)(2,1)} async-done(((bf16[2,16,3,8192]{3,0,2,1:T(2,128)(2,1)}), bf16[2,16,3,8192]{3,0,2,1:T(2,128)(2,1)}, u32[]{:S(2)}, u32[]{:S(2)}) %all-to-all-start) | async-done | bytes 1572896 | tf_op jit(solution)/shard_map/all_to_all | solution.py:246
  87.4 2.6 copy.28
  90.0 1.5 slice.30.q_ref
  91.5 0.5 fusion.40
  92.0 0.3 fusion.2
  92.3 0.5 fusion.14
  92.9 0.2 copy.42
  93.1 55.2 %all-gather.5.cloned.1.call-done.k_ref.v_ref = bf16[4096,1024]{1,0:T(8,128)(2,1)} async-done(((bf16[256,1024]{1,0:T(8,128)(2,1)}), bf16[4096,1024]{1,0:T(8,128)(2,1)}) %all-gather.5.cloned.1.call-update) | async-done | bytes 8388624 | tf_op jit(solution)/shard_map/all_gather | solution.py:169
  148.3 55.9 %shard_map.86 = (f32[4,4,512,128]{3,2,1,0:T(8,128)}, f32[4,4,512,128]{3,2,1,0:T(8,128)}, f32[4,4,512,128]{3,2,1,0:T(8,128)}) custom-call(s32[1]{0:T(128)} %bitcast.b_ref, bf16[512,2048]{1,0:T(8,128)(2,1)} %slice.30.q_ref, bf16[4096,1024]{1,0:T(8,128)(2,1)} %all-gather.5.cloned.1.call-done.k_ref.v_ref, bf16[4096,1024]{1,0:T(8,128)(2,1)} %all-gather.5.cloned.1.call-done.k_ref.v_ref), custom_call_target="tpu_custom_call" | custom-call | tf_op jit(solution)/shard_map/pallas_call | solution.py:149
  204.1 58.0 %all-gather.3.cloned.1.call-done.k_ref.v_ref = bf16[4096,1024]{1,0:T(8,128)(2,1)} async-done(((bf16[256,1024]{1,0:T(8,128)(2,1)}), bf16[4096,1024]{1,0:T(8,128)(2,1)}) %all-gather.3.cloned.1.call-update) | async-done | bytes 8388624 | tf_op jit(solution)/shard_map/all_gather | solution.py:169
  262.1 55.5 %shard_map.87 = bf16[512,2048]{1,0:T(8,128)(2,1)} custom-call(s32[1]{0:T(128)} %bitcast.b_ref, bf16[512,2048]{1,0:T(8,128)(2,1)} %slice.30.q_ref, bf16[4096,1024]{1,0:T(8,128)(2,1)} %all-gather.3.cloned.1.call-done.k_ref.v_ref, bf16[4096,1024]{1,0:T(8,128)(2,1)} %all-gather.3.cloned.1.call-done.k_ref.v_ref, f32[4,4,512,128]{3,2,1,0:T(8,128)} %get-tuple-element.8.refs_0_, ...), custom_call_target="tpu_custom_call" | custom-call | tf_op jit(solution)/shard_map/pallas_call | solution.py:149
  317.6 18.9 %convolution_convert_fusion = bf16[320,8192]{1,0:T(8,128)(2,1)} fusion(bf16[2048,8192]{1,0:T(8,128)(2,1)} %param.10, s32[]{:T(128)S(6)} %select_n.109, bf16[512,2048]{1,0:T(8,128)(2,1)} %shard_map.87, bf16[128,2048]{1,0:T(8,128)(2,1)S(1)} %copy.42), kind=kOutput, calls=%fused_computation | convolution fusion | flops 10742661120 | bytes 41418756 | tf_op jit(solution)/shard_map/dot_general | solution.py:279
  336.5 0.3 collective-permute-start.2
  336.8 0.3 convolution_convert_fusion.3
  337.1 2.7 fusion
  339.8 1.7 copy.45
  341.5 4.0 %collective-permute-done.2 = bf16[320,8192]{1,0:T(8,128)(2,1)} collective-permute-done((bf16[320,8192]{1,0:T(8,128)(2,1)}, bf16[320,8192]{1,0:T(8,128)(2,1)}, u32[]{:S(2)}, u32[]{:S(2)}) %collective-permute-start.2) | collective-permute-done | bytes 5242912 | tf_op jit(solution)/shard_map/ppermute | solution.py:280
  345.5 20.9 %add_convert_fusion = bf16[320,8192]{1,0:T(8,128)(2,1)} fusion(bf16[320,8192]{1,0:T(8,128)(2,1)} %collective-permute-done.2, bf16[2048,8192]{1,0:T(8,128)(2,1)} %param.10, pred[]{:T(512)S(6)} %eq.58, s32[]{:T(128)S(6)} %select_n.108, bf16[512,2048]{1,0:T(8,128)(2,1)S(1)} %copy-done.3, bf16[128,2048]{1,0:T(8,128)(2,1)S(1)} %copy.42), kind=kOutput, calls=%fused_computation.2 | convolution fusion | flops 10758389760 | bytes 46661636 | tf_op jit(solution)/shard_map/dot_general | solution.py:282
  (39 shorter events, 0.3 us)
Async XLA Ops:
  7.2 141.1 %all-gather.5.cloned.1.call-start = ((), (), s32[]{:S(2)}) async-start(), calls=%async_computation.2 | async-start | bytes 8912896 | tf_op jit(solution)/shard_map/all_gather | solution.py:169
  8.3 3.0 copy-start.2
  9.4 2.2 copy-start.1
  10.3 251.8 %all-gather.3.cloned.1.call-start = ((), (), s32[]{:S(2)}) async-start(), calls=%async_computation.1 | async-start | bytes 8912896 | tf_op jit(solution)/shard_map/all_gather | solution.py:169
  10.4 1.6 copy-start.5
  10.4 1.9 copy-start.4
  10.4 2.3 copy-start.6
  17.3 6.7 %slice-start.1 = ((bf16[640,512]{1,0:T(8,128)(2,1)}), bf16[128,512]{1,0:T(8,128)(2,1)S(1)}, s32[]{:S(2)}) async-start(bf16[640,512]{1,0:T(8,128)(2,1)} %param.8), calls=%async_computation.4 | async-start | bytes 262144 | tf_op jit(solution)/shard_map/slice | solution.py:268
  17.3 70.1 %copy-start = (bf16[640,2048]{1,0:T(8,128)(2,1)S(1)}, bf16[640,2048]{1,0:T(8,128)(2,1)}, u32[]{:S(2)}) copy-start(bf16[640,2048]{1,0:T(8,128)(2,1)} %param.7) | copy-start | bytes 7864324
  17.3 70.1 %all-to-all-start = ((bf16[2,16,3,8192]{3,0,2,1:T(2,128)(2,1)}), bf16[2,16,3,8192]{3,0,2,1:T(2,128)(2,1)}, u32[]{:S(2)}, u32[]{:S(2)}) async-start(bf16[2,16,3,8192]{3,0,2,1:T(2,128)(2,1)} %bitcast.53), calls=%async_computation | async-start | bytes 3145728 | tf_op jit(solution)/shard_map/all_to_all | solution.py:246
  24.1 13.3 %collective-permute-start.1 = (bf16[128,512]{0,1:T(8,128)(2,1)S(1)}, bf16[128,512]{0,1:T(8,128)(2,1)S(1)}, u32[]{:S(2)}, u32[]{:S(2)}) collective-permute-start(bf16[128,512]{0,1:T(8,128)(2,1)S(1)} %copy.43), channel_id=1, source_target_pairs={{0,2},{2,4},{4,6},{6,8},{8,10},{10,12},{12,14},{14,16},{16,18},{18... | collective-permute-start | bytes 393224 | tf_op jit(solution)/shard_map/ppermute | solution.py:180
  28.1 9.1 %collective-permute-start = (bf16[128,512]{1,0:T(8,128)(2,1)S(1)}, bf16[128,512]{1,0:T(8,128)(2,1)S(1)}, u32[]{:S(2)}, u32[]{:S(2)}) collective-permute-start(bf16[128,512]{1,0:T(8,128)(2,1)S(1)} %slice.35), channel_id=1, source_target_pairs={{0,2},{2,4},{4,6},{6,8},{8,10},{10,12},{12,14},{14,16},{16,18},{18... | collective-permute-start | bytes 393224 | tf_op jit(solution)/shard_map/ppermute | solution.py:181
  90.0 1.5 slice-start
  336.5 9.0 %collective-permute-start.2 = (bf16[320,8192]{1,0:T(8,128)(2,1)}, bf16[320,8192]{1,0:T(8,128)(2,1)}, u32[]{:S(2)}, u32[]{:S(2)}) collective-permute-start(bf16[320,8192]{1,0:T(8,128)(2,1)} %convolution_convert_fusion), channel_id=1, source_target_pairs={{0,1},{1,0},{2,3},{3,2},{4,5},{5,4},{6,7},{7,6},{8,9},{9,8},{10,11... | collective-permute-start | bytes 15728648 | tf_op jit(solution)/shard_map/ppermute | solution.py:280
  339.8 5.7 %copy-start.3 = (bf16[512,2048]{1,0:T(8,128)(2,1)S(1)}, bf16[512,2048]{1,0:T(8,128)(2,1)}, u32[]{:S(2)}) copy-start(bf16[512,2048]{1,0:T(8,128)(2,1)} %shard_map.87) | copy-start | bytes 6291460
Sparse Core Ops, SparseCore 0:
  10.8 137.4 all-gather.4
  151.1 111.0 all-gather.2
